TPU v7x, 256 devices: a whole 4x4x8 slice. The times are simulated.
256 devices in a mesh: sa: 8 (over z), sb: 4 (over y_lo, core), sl: 8 (over x, y_hi).
Axes of the slice: x: 4, y: 4 (y_hi: 2, y_lo: 2; y = y_hi * 2 + y_lo), z: 8, core: 2. Of those that a mesh axis runs over, the one named last changes fastest.
Arguments:
- stem_cache: bfloat16 [256, 2, 128, 4096], P(('sa', 'sb', 'sl')), may hold values from -6 to 6
- subtree_cache: bfloat16 [256, 2, 4096, 512], P(('sa', 'sb', 'sl')), may hold values from -0.0625 to 0.0625
- final_gates: bfloat16 [2, 512, 512], replicated, may hold values from -0.01171875 to 0.01171875
- group_rows: int32 [32], replicated, may hold values from 0 to 7
Outputs:
- amplitudes: float32 [512, 1024], P(('sa', 'sb', 'sl'))
All inputs are finite; a program needn't handle non-finite values.
Results may differ from a plain program's by a relative error of at most 0.0029.
Values may be sent and summed in bfloat16 or wider, within the bound.
No kernel may reach another device: no remote copies, remote signals or barrier semaphores. Data moves between devices by JAX's collectives and lax.ppermute only.
A program may use at most 64 MiB of HBM per device.

v0:
```python
import jax
import jax.numpy as jnp
from jax import lax
from jax.sharding import PartitionSpec as P

RB = 16


def swapped(shard, axis, apart):
    return lax.ppermute(shard, axis, [(i, i ^ 1 << apart) for i in range(lax.axis_size(axis))])


def complex_dot(left_real, left_imag, right):
    real = jnp.dot(left_real, right[0], preferred_element_type=jnp.float32) - jnp.dot(
        left_imag, right[1], preferred_element_type=jnp.float32
    )
    imag = jnp.dot(left_real, right[1], preferred_element_type=jnp.float32) + jnp.dot(
        left_imag, right[0], preferred_element_type=jnp.float32
    )
    return (real, imag)


def local(stem_cache, subtree_cache, final_gates, group_rows):
    stem = stem_cache[0]
    half = stem.shape[1] // 2
    upper = swapped(stem[:, half:], "sb", 0)
    whole = jnp.concatenate([stem[:, :half], upper], axis=1)
    top_bit = lax.axis_size("sa").bit_length() - 2
    subtree = subtree_cache[0]
    left = swapped(whole, "sa", top_bit)
    real, imag = complex_dot(left[0], left[1], subtree)
    partial_s = jnp.stack([real, imag]).astype(jnp.bfloat16)
    total_rows = group_rows.shape[0] * RB
    own_count = total_rows // lax.axis_size(("sa", "sb", "sl"))
    rows = jnp.arange(own_count * lax.axis_size(("sa", "sb", "sl")), dtype=jnp.int32)
    chosen = jnp.take(partial_s, jnp.take(group_rows, rows // RB) * RB + rows % RB, axis=1)
    out_real, out_imag = complex_dot(chosen[0], chosen[1], final_gates)
    return lax.psum_scatter(
        jnp.concatenate([out_real, out_imag], axis=1),
        ("sa", "sb", "sl"),
        scatter_dimension=0,
        tiled=True,
    )


def solution(mesh):
    return jax.shard_map(
        local,
        mesh=mesh,
        in_specs=(
            P(("sa", "sb", "sl"), None, None, None),
            P(("sa", "sb", "sl"), None, None, None),
            P(),
            P(),
        ),
        out_specs=P(("sa", "sb", "sl"), None),
        check_vma=False,
    )
```

profile of v0, /device:TPU:2, one launch (start us, length us, event | category | flops | bytes accessed | tf_op | source)
XLA Modules:
  0.0 397.0 jit_solution(11102751117178020497)
XLA Ops:
  6.5 1.8 fusion.58
  8.5 2.6 collective-permute-done
  11.3 7.3 %collective-permute-start.1 = (bf16[2,128,4096]{2,1,0:T(8,128)(2,1)S(1)}, bf16[2,128,4096]{2,1,0:T(8,128)(2,1)S(1)}, u32[]{:S(2)}, u32[]{:S(2)}) collective-permute-start(bf16[2,128,4096]{2,1,0:T(8,128)(2,1)S(1)} %pad_maximum_fusion), channel_id=1, source_target_pairs={{0,128},{32,160},{64,192},{96,224},{128,0},{160,32},{192,64},{224,... | collective-permute-start | bytes 6291464 | tf_op jit(solution)/shard_map/ppermute | solution.py:10
  19.5 0.7 fusion.61
  20.2 4.4 %compare_select_fusion.2 = s32[512,1]{0,1:T(1,128)S(1)} fusion(s32[]{:T(128)} %bitcast.25, s32[]{:T(128)} %bitcast.26, s32[]{:T(128)} %bitcast.27, s32[]{:T(128)} %bitcast.28, s32[]{:T(128)} %bitcast.29, s32[]{:T(128)} %bitcast.31, s32[]{:T(128)} %bitcast.30), kind=kLoop, calls=%fused_computation.73 | loop fusion | flops 11776 | bytes 2076 | tf_op jit(solution)/shard_map/jit(_take)/gather | solution.py:36
  24.6 0.7 fusion.60
  25.3 15.6 %compare_and_fusion = (pred[512]{0:T(512)(128)(4,1)S(1)}, s32[512]{0:T(512)S(1)}) fusion(pred[512]{0:T(512)(128)(4,1)S(1)} %compare_reduce_fusion, pred[512]{0:T(512)(128)(4,1)S(1)} %compare_reduce_fusion.1, pred[512]{0:T(512)(128)(4,1)S(1)} %compare_reduce_fusion.2, pred[512]{0:T(512)(128)(4,1)S(1)} %compare_reduce_fusion.3, ...), kind=kLoop, calls=%fused_computation.102 | loop fusion | flops 26624 | bytes 17508 | tf_op jit(solution)/shard_map/jit(_take)/and | solution.py:36
  40.9 67.6 %collective-permute-done.1 = bf16[2,128,4096]{2,1,0:T(8,128)(2,1)S(1)} collective-permute-done((bf16[2,128,4096]{2,1,0:T(8,128)(2,1)S(1)}, bf16[2,128,4096]{2,1,0:T(8,128)(2,1)S(1)}, u32[]{:S(2)}, u32[]{:S(2)}) %collective-permute-start.1) | collective-permute-done | bytes 2097184 | tf_op jit(solution)/shard_map/ppermute | solution.py:10
  108.5 0.7 fusion.4
  109.2 0.7 fusion.2
  110.0 0.7 fusion.27
  110.7 0.7 fusion.24
  111.5 0.3 copy.10
  111.7 3.6 gather_fusion
  115.3 2.0 fusion.30
  117.3 1.5 fusion.59
  118.8 0.5 fusion.33
  119.3 0.5 fusion.35
  119.8 0.5 convolution_add_fusion
  120.3 0.5 convolution_subtract_fusion
  120.8 1.5 pad_maximum_fusion.1
  122.3 265.8 %all-reduce.3.cloned.1.call-done = f32[512,1024]{0,1:T(8,128)} async-done(((f32[512,1024]{0,1:T(8,128)}), f32[512,1024]{0,1:T(8,128)}) %all-reduce.3.cloned.1.call-update) | async-done | bytes 2097168
  388.1 1.2 constant_dynamic-slice_fusion
  389.3 0.8 copy.11
  (38 shorter events, 1.2 us)
Async XLA Ops:
  6.5 381.6 %all-reduce.3.cloned.1.call-start = ((), (), s32[]{:S(2)}) async-start(), calls=%async_computation | async-start | bytes 4194304
  6.5 102.0 %copy-start.2 = (bf16[1,2,4096,512]{3,2,1,0:T(8,128)(2,1)S(1)}, bf16[1,2,4096,512]{3,2,1,0:T(8,128)(2,1)}, u32[]{:S(2)}) copy-start(bf16[1,2,4096,512]{3,2,1,0:T(8,128)(2,1)} %param.5) | copy-start | bytes 25165828
  8.4 2.7 collective-permute-start
  11.1 8.4 %copy-start.1 = (s32[32]{0:T(128)S(1)}, s32[32]{0:T(128)}, u32[]{:S(2)}) copy-start(s32[32]{0:T(128)} %param.7) | copy-start | bytes 388
  11.3 97.2 %collective-permute-start.1 = (bf16[2,128,4096]{2,1,0:T(8,128)(2,1)S(1)}, bf16[2,128,4096]{2,1,0:T(8,128)(2,1)S(1)}, u32[]{:S(2)}, u32[]{:S(2)}) collective-permute-start(bf16[2,128,4096]{2,1,0:T(8,128)(2,1)S(1)} %pad_maximum_fusion), channel_id=1, source_target_pairs={{0,128},{32,160},{64,192},{96,224},{128,0},{160,32},{192,64},{224,... | collective-permute-start | bytes 6291464 | tf_op jit(solution)/shard_map/ppermute | solution.py:10
  117.3 1.5 copy-start
Sparse Core Ops, SparseCore 0:
  122.4 265.6 all-reduce.2
where the time goes:
time: 397 us
  waiting for transfers between devices  336 us (85%)
  other arithmetic  24.5 us (6%)
  between operations  13.6 us (3%)
  local copies, waits for them, and re-layouts  10.6 us (3%)
  starting transfers between devices  7.37 us (2%)
  matrix products  4.82 us (1%)
    unnamed x2, waiting for transfers between devices  266 us
    ppermute x2, waiting for transfers between devices, swapped(): lax.ppermute(shard, axis, [(i, i ^ 1 << apart) for i in range(lax.axis_si...  70.2 us
    and x1, other arithmetic, local(): jnp.take(partial_s, jnp.take(group_rows, rows // RB) * RB + rows % RB, ax...  15.6 us
  transfers between devices with their start and end apart: 3, of which 3 were waited for; matrix products, arithmetic and copies ran while one was open for 6% of the time, Pallas kernels for 0%

commit v1 on v0

v1 whole, which is shorter than its diff:
```python
import jax
import jax.numpy as jnp
from jax import lax
from jax.sharding import PartitionSpec as P

RB = 16
ALL = ("sa", "sb", "sl")


def swapped(shard, axis, apart):
    return lax.ppermute(shard, axis, [(i, i ^ 1 << apart) for i in range(lax.axis_size(axis))])


def complex_dot(left_real, left_imag, right, precision=None):
    dot = lambda a, b: jnp.dot(a, b, preferred_element_type=jnp.float32, precision=precision)
    real = dot(left_real, right[0]) - dot(left_imag, right[1])
    imag = dot(left_real, right[1]) + dot(left_imag, right[0])
    return (real, imag)


def local(stem_cache, subtree_cache, final_gates, group_rows):
    stem = stem_cache[0]
    half = stem.shape[1] // 2
    upper = swapped(stem[:, half:], "sb", 0)
    whole = jnp.concatenate([stem[:, :half], upper], axis=1)
    top_bit = lax.axis_size("sa").bit_length() - 2
    subtree = subtree_cache[0]
    left = swapped(whole, "sa", top_bit)
    real, imag = complex_dot(left[0], left[1], subtree)
    partial_s = jnp.stack([real, imag]).astype(jnp.bfloat16).astype(jnp.float32)
    summed = lax.psum(partial_s, ALL)
    total_rows = group_rows.shape[0] * RB
    own_count = total_rows // lax.axis_size(ALL)
    rows = lax.axis_index(ALL) * own_count + jnp.arange(own_count, dtype=jnp.int32)
    chosen = jnp.take(summed, jnp.take(group_rows, rows // RB) * RB + rows % RB, axis=1)
    gates = final_gates.astype(jnp.float32)
    out_real, out_imag = complex_dot(chosen[0], chosen[1], gates, precision=lax.Precision.HIGHEST)
    return jnp.concatenate([out_real, out_imag], axis=1)


def solution(mesh):
    return jax.shard_map(
        local,
        mesh=mesh,
        in_specs=(
            P(ALL, None, None, None),
            P(ALL, None, None, None),
            P(),
            P(),
        ),
        out_specs=P(ALL, None),
        check_vma=False,
    )
```

time: 397 us -> 390 us (0.982)
  other arithmetic: 24.5 us -> 1.72 us
  waiting for transfers between devices: 336 us -> 350 us
  matrix products: 4.82 us -> 13.3 us
  local copies, waits for them, and re-layouts: 10.6 us -> 4.4 us
    unnamed x2 -> x1, waiting for transfers between devices: 266 us -> 0.02 us
    psum x0 -> x1, waiting for transfers between devices: none -> 258 us  [local(): summed = lax.psum(partial_s, ALL)]
    ppermute x2, waiting for transfers between devices: 70.2 us -> 91.9 us  [swapped(): lax.ppermute(shard, axis, [(i, i ^ 1 << apart) for i in range(lax.axis_si...]
    and x1, other arithmetic: 15.6 us -> 0.02 us  [local(): jnp.take(summed, jnp.take(group_rows, rows // RB) * RB + rows % RB, axis=1)]
    dot_general x8, matrix products: 4.82 us -> 13.3 us  [complex_dot(): jnp.dot(a, b, preferred_element_type=jnp.float32, precision=precision)]
    gather x26 -> x1, other arithmetic: 5.23 us -> 0.01 us  [local(): jnp.take(group_rows, rows // RB) * RB + rows % RB]
  transfers between devices with their start and end apart: 3 -> 3, of which waited for: 3 -> 3; matrix products, arithmetic and copies ran while one was open for 6% -> 0% of each run, Pallas kernels for 0% -> 0%
where the time goes in v1:
time: 390 us
  waiting for transfers between devices  350 us (90%)
  between operations  13.5 us (3%)
  matrix products  13.3 us (3%)
  starting transfers between devices  7.37 us (2%)
  local copies, waits for them, and re-layouts  4.4 us (1%)
    psum x1, waiting for transfers between devices, local(): summed = lax.psum(partial_s, ALL)  258 us
    ppermute x2, waiting for transfers between devices, swapped(): lax.ppermute(shard, axis, [(i, i ^ 1 << apart) for i in range(lax.axis_si...  91.9 us
    dot_general x8, matrix products, complex_dot(): jnp.dot(a, b, preferred_element_type=jnp.float32, precision=precision)  13.3 us
  transfers between devices with their start and end apart: 3, of which 3 were waited for; matrix products, arithmetic and copies ran while one was open for 0% of the time, Pallas kernels for 0%

profile of v1, /device:TPU:2, one launch (start us, length us, event | category | flops | bytes accessed | tf_op | source)
XLA Modules:
  0.0 390.1 jit_solution(4582372322530239566)
XLA Ops:
  6.5 1.7 fusion.52
  8.3 0.1 collective-permute-start
  8.4 2.6 collective-permute-done
  11.0 0.1 pad_maximum_fusion
  11.1 7.3 %collective-permute-start.1 = (bf16[2,128,4096]{2,1,0:T(8,128)(2,1)S(1)}, bf16[2,128,4096]{2,1,0:T(8,128)(2,1)}, u32[]{:S(2)}, u32[]{:S(2)}) collective-permute-start(bf16[2,128,4096]{2,1,0:T(8,128)(2,1)S(1)} %pad_maximum_fusion), channel_id=1, source_target_pairs={{0,128},{32,160},{64,192},{96,224},{128,0},{160,32},{192,64},{224,... | collective-permute-start | bytes 6291464 | tf_op jit(solution)/shard_map/ppermute | solution.py:11
  18.5 0.6 gather_fusion
  19.1 89.2 %collective-permute-done.1 = bf16[2,128,4096]{2,1,0:T(8,128)(2,1)} collective-permute-done((bf16[2,128,4096]{2,1,0:T(8,128)(2,1)S(1)}, bf16[2,128,4096]{2,1,0:T(8,128)(2,1)}, u32[]{:S(2)}, u32[]{:S(2)}) %collective-permute-start.1) | collective-permute-done | bytes 2097184 | tf_op jit(solution)/shard_map/ppermute | solution.py:11
  108.3 3.4 fusion.2
  111.7 0.0 slice-start.1
  111.7 3.4 fusion.4
  115.1 3.2 fusion.24
  118.4 0.0 copy-start.1
  118.4 2.1 fusion.27
  120.5 0.8 maximum_convert_fusion
  121.3 0.0 all-reduce.2.cloned.1.call-update
  121.4 257.9 %all-reduce.2.cloned.1.call-done = f32[2,128,512]{2,1,0:T(8,128)} async-done(((f32[2,128,512]{2,1,0:T(8,128)}), f32[2,128,512]{2,1,0:T(8,128)}) %all-reduce.2.cloned.1.call-update) | async-done | bytes 524304 | tf_op jit(solution)/shard_map/psum | solution.py:31
  379.2 1.4 copy.5
  380.7 0.6 gather_fusion.1
  381.3 0.1 select_bitcast_fusion
  381.4 0.3 fusion.34
  381.7 0.3 fusion.30
  382.0 0.3 convolution_subtract_fusion
  382.3 0.3 convolution_add_fusion
  382.6 0.6 pad_maximum_fusion.1
  (14 shorter events, 0.1 us)
Async XLA Ops:
  6.5 11.9 %copy-start = (s32[32]{0:T(128)S(1)}, s32[32]{0:T(128)}, u32[]{:S(2)}) copy-start(s32[32]{0:T(128)} %param.7) | copy-start | bytes 388
  6.5 372.7 %all-reduce.2.cloned.1.call-start = ((), (), s32[]{:S(2)}) async-start(), calls=%async_computation | async-start | bytes 1048576 | tf_op jit(solution)/shard_map/psum | solution.py:31
  8.3 2.7 collective-permute-start
  11.1 97.2 %collective-permute-start.1 = (bf16[2,128,4096]{2,1,0:T(8,128)(2,1)S(1)}, bf16[2,128,4096]{2,1,0:T(8,128)(2,1)}, u32[]{:S(2)}, u32[]{:S(2)}) collective-permute-start(bf16[2,128,4096]{2,1,0:T(8,128)(2,1)S(1)} %pad_maximum_fusion), channel_id=1, source_target_pairs={{0,128},{32,160},{64,192},{96,224},{128,0},{160,32},{192,64},{224,... | collective-permute-start | bytes 6291464 | tf_op jit(solution)/shard_map/ppermute | solution.py:11
  108.3 10.0 %slice-start = ((s8[8388608]{0:T(1024)(128)(4,1)}), s8[4194304]{0:T(1024)(128)(4,1)S(1)}, s32[]{:S(2)}) async-start(s8[8388608]{0:T(1024)(128)(4,1)} %bitcast.66), calls=%async_computation.1 | async-start | bytes 8388608
  111.7 6.6 %slice-start.1 = ((s8[8388608]{0:T(1024)(128)(4,1)}), s8[4194304]{0:T(1024)(128)(4,1)S(1)}, s32[]{:S(2)}) async-start(s8[8388608]{0:T(1024)(128)(4,1)} %bitcast.66), calls=%async_computation.2 | async-start | bytes 8388608
  118.4 263.0 %copy-start.1 = (bf16[2,512,512]{2,1,0:T(8,128)(2,1)S(1)}, bf16[2,512,512]{2,1,0:T(8,128)(2,1)}, u32[]{:S(2)}) copy-start(bf16[2,512,512]{2,1,0:T(8,128)(2,1)} %param.6) | copy-start | bytes 3145732
Sparse Core Ops, SparseCore 0:
  121.4 257.7 all-reduce.1

commit v2 on v1

--- a/solution.py
+++ b/solution.py
@@ -18,6 +18,25 @@
     return (real, imag)
 
 
+def halving(x, axis, dim):
+    me = lax.axis_index(axis)
+    for bit in reversed(range(lax.axis_size(axis).bit_length() - 1)):
+        half = x.shape[dim] // 2
+        lo = lax.slice_in_dim(x, 0, half, axis=dim)
+        hi = lax.slice_in_dim(x, half, 2 * half, axis=dim)
+        mine = (me >> bit) & 1
+        keep = jnp.where(mine == 1, hi, lo)
+        send = jnp.where(mine == 1, lo, hi)
+        x = keep + swapped(send, axis, bit)
+    return x
+
+
+def doubling(x, axis):
+    for bit in range(lax.axis_size(axis).bit_length() - 1):
+        x = x + swapped(x, axis, bit)
+    return x
+
+
 def local(stem_cache, subtree_cache, final_gates, group_rows):
     stem = stem_cache[0]
     half = stem.shape[1] // 2
@@ -28,11 +47,15 @@
     left = swapped(whole, "sa", top_bit)
     real, imag = complex_dot(left[0], left[1], subtree)
     partial_s = jnp.stack([real, imag]).astype(jnp.bfloat16).astype(jnp.float32)
-    summed = lax.psum(partial_s, ALL)
-    total_rows = group_rows.shape[0] * RB
-    own_count = total_rows // lax.axis_size(ALL)
-    rows = lax.axis_index(ALL) * own_count + jnp.arange(own_count, dtype=jnp.int32)
-    chosen = jnp.take(summed, jnp.take(group_rows, rows // RB) * RB + rows % RB, axis=1)
+    n_sl = lax.axis_size("sl")
+    blocks = partial_s.shape[1] // RB
+    own_count = RB // n_sl
+    q = partial_s.reshape(2, blocks, n_sl, own_count, partial_s.shape[2])
+    q = halving(q, "sl", 2)
+    q = doubling(q, "sb")
+    q = doubling(q, "sa")
+    group = lax.axis_index("sa") * lax.axis_size("sb") + lax.axis_index("sb")
+    chosen = jnp.take(q[:, :, 0], group_rows[group], axis=1)
     gates = final_gates.astype(jnp.float32)
     out_real, out_imag = complex_dot(chosen[0], chosen[1], gates, precision=lax.Precision.HIGHEST)
     return jnp.concatenate([out_real, out_imag], axis=1)

time: 390 us -> 163 us (0.42)
  waiting for transfers between devices: 350 us -> 116 us
  starting transfers between devices: 7.37 us -> 26.6 us
  between operations: 13.5 us -> 2.11 us
    psum x1 -> x0, waiting for transfers between devices: 258 us -> none  [local(): summed = lax.psum(partial_s, ALL)]
    ppermute x2 -> x10, waiting for transfers between devices: 91.9 us -> 116 us  [swapped(): lax.ppermute(shard, axis, [(i, i ^ 1 << apart) for i in range(lax.axis_si...]
    ppermute x2 -> x10, starting transfers between devices: 7.37 us -> 26.6 us  [swapped(): lax.ppermute(shard, axis, [(i, i ^ 1 << apart) for i in range(lax.axis_si...]
  transfers between devices with their start and end apart: 3 -> 10, of which waited for: 3 -> 10; matrix products, arithmetic and copies ran while one was open for 0% -> 0% of each run, Pallas kernels for 0% -> 0%
where the time goes in v2:
time: 163 us
  waiting for transfers between devices  116 us (71%)
  starting transfers between devices  26.6 us (16%)
  matrix products  14.2 us (9%)
  local copies, waits for them, and re-layouts  2.41 us (1%)
  between operations  2.11 us (1%)
  other arithmetic  1.84 us (1%)
    ppermute x10, waiting for transfers between devices, swapped(): lax.ppermute(shard, axis, [(i, i ^ 1 << apart) for i in range(lax.axis_si...  116 us
    ppermute x10, starting transfers between devices, swapped(): lax.ppermute(shard, axis, [(i, i ^ 1 << apart) for i in range(lax.axis_si...  26.6 us
    dot_general x8, matrix products, complex_dot(): jnp.dot(a, b, preferred_element_type=jnp.float32, precision=precision)  14.2 us
  transfers between devices with their start and end apart: 10, of which 10 were waited for; matrix products, arithmetic and copies ran while one was open for 0% of the time, Pallas kernels for 0%

profile of v2, /device:TPU:2, one launch (start us, length us, event | category | flops | bytes accessed | tf_op | source)
XLA Modules:
  0.0 162.7 jit_solution(14462670210363513014)
XLA Ops:
  0.0 1.7 %fusion.36 = (bf16[2,64,4096]{2,1,0:T(8,128)(2,1)S(1)}, bf16[2,64,4096]{2,1,0:T(8,128)(2,1)S(1)}) fusion(bf16[2,128,4096]{2,1,0:T(8,128)(2,1)} %bitcast.48), kind=kLoop, calls=%fused_computation.44 | loop fusion | bytes 4194304 | tf_op jit(solution)/shard_map/slice | solution.py:44
  1.8 2.6 %collective-permute-done = bf16[2,64,4096]{2,1,0:T(8,128)(2,1)S(1)} collective-permute-done((bf16[2,64,4096]{2,1,0:T(8,128)(2,1)S(1)}, bf16[2,64,4096]{2,1,0:T(8,128)(2,1)S(1)}, u32[]{:S(2)}, u32[]{:S(2)}) %collective-permute-start) | collective-permute-done | bytes 1048608 | tf_op jit(solution)/shard_map/ppermute | solution.py:11
  4.6 7.3 %collective-permute-start.1 = (bf16[2,128,4096]{2,1,0:T(8,128)(2,1)S(1)}, bf16[2,128,4096]{2,1,0:T(8,128)(2,1)}, u32[]{:S(2)}, u32[]{:S(2)}) collective-permute-start(bf16[2,128,4096]{2,1,0:T(8,128)(2,1)S(1)} %pad_maximum_fusion), channel_id=1, source_target_pairs={{0,128},{32,160},{64,192},{96,224},{128,0},{160,32},{192,64},{224,... | collective-permute-start | bytes 6291464 | tf_op jit(solution)/shard_map/ppermute | solution.py:11
  11.9 89.9 %collective-permute-done.1 = bf16[2,128,4096]{2,1,0:T(8,128)(2,1)} collective-permute-done((bf16[2,128,4096]{2,1,0:T(8,128)(2,1)S(1)}, bf16[2,128,4096]{2,1,0:T(8,128)(2,1)}, u32[]{:S(2)}, u32[]{:S(2)}) %collective-permute-start.1) | collective-permute-done | bytes 2097184 | tf_op jit(solution)/shard_map/ppermute | solution.py:11
  101.8 3.2 %fusion.2 = f32[128,512]{1,0:T(8,128)S(1)} fusion(bf16[1,2,4096,512]{3,2,1,0:T(8,128)(2,1)} %param.5, bf16[2,128,4096]{2,1,0:T(8,128)(2,1)} %collective-permute-done.1), kind=kOutput, calls=%fused_computation.2 | convolution fusion | flops 536870912 | bytes 5505024 | tf_op jit(solution)/shard_map/dot_general | solution.py:15
  105.0 3.2 %fusion.21 = bf16[128,512]{1,0:T(8,128)(2,1)S(1)} fusion(f32[128,512]{1,0:T(8,128)S(1)} %fusion.2, bf16[1,2,4096,512]{3,2,1,0:T(8,128)(2,1)} %param.5, bf16[2,128,4096]{2,1,0:T(8,128)(2,1)} %collective-permute-done.1), kind=kOutput, calls=%fused_computation.16 | convolution fusion | flops 537001984 | bytes 5636096 | tf_op jit(solution)/shard_map/dot_general | solution.py:15
  108.3 3.2 %fusion.4 = f32[128,512]{1,0:T(8,128)S(1)} fusion(bf16[1,2,4096,512]{3,2,1,0:T(8,128)(2,1)} %param.5, bf16[2,128,4096]{2,1,0:T(8,128)(2,1)} %collective-permute-done.1), kind=kOutput, calls=%fused_computation.4 | convolution fusion | flops 536870912 | bytes 5505024 | tf_op jit(solution)/shard_map/dot_general | solution.py:15
  111.5 3.2 %fusion.18 = bf16[128,512]{1,0:T(8,128)(2,1)S(1)} fusion(f32[128,512]{1,0:T(8,128)S(1)} %fusion.4, bf16[1,2,4096,512]{3,2,1,0:T(8,128)(2,1)} %param.5, bf16[2,128,4096]{2,1,0:T(8,128)(2,1)} %collective-permute-done.1), kind=kOutput, calls=%fused_computation.15 | convolution fusion | flops 537001984 | bytes 5636096 | tf_op jit(solution)/shard_map/dot_general | solution.py:15
  115.4 2.2 %collective-permute-start.2 = (f32[2,8,4,2,512]{4,3,2,1,0:T(2,128)S(1)}, f32[2,8,4,2,512]{4,3,2,1,0:T(2,128)S(1)}, u32[]{:S(2)}, u32[]{:S(2)}) collective-permute-start(f32[2,8,4,2,512]{4,3,2,1,0:T(2,128)S(1)} %broadcast_select_fusion), channel_id=1, source_target_pairs={{0,4},{1,5},{2,6},{3,7},{4,0},{5,1},{6,2},{7,3},{8,12},{9,13},{10,... | collective-permute-start | bytes 786440 | tf_op jit(solution)/shard_map/ppermute | solution.py:11
  117.6 5.7 %collective-permute-done.2 = f32[2,8,4,2,512]{4,3,2,1,0:T(2,128)S(1)} collective-permute-done((f32[2,8,4,2,512]{4,3,2,1,0:T(2,128)S(1)}, f32[2,8,4,2,512]{4,3,2,1,0:T(2,128)S(1)}, u32[]{:S(2)}, u32[]{:S(2)}) %collective-permute-start.2) | collective-permute-done | bytes 262176 | tf_op jit(solution)/shard_map/ppermute | solution.py:11
  124.1 4.6 %collective-permute-done.3 = f32[2,8,2,2,512]{4,3,2,1,0:T(2,128)S(1)} collective-permute-done((f32[2,8,2,2,512]{4,3,2,1,0:T(2,128)S(1)}, f32[2,8,2,2,512]{4,3,2,1,0:T(2,128)S(1)}, u32[]{:S(2)}, u32[]{:S(2)}) %collective-permute-start.3) | collective-permute-done | bytes 131104 | tf_op jit(solution)/shard_map/ppermute | solution.py:11
  128.8 3.3 %collective-permute-start.4 = (f32[2,8,1,2,512]{4,3,2,1,0:T(2,128)S(1)}, f32[2,8,1,2,512]{4,3,2,1,0:T(2,128)S(1)}, u32[]{:S(2)}, u32[]{:S(2)}) collective-permute-start(f32[2,8,1,2,512]{4,3,2,1,0:T(2,128)S(1)} %broadcast_select_fusion.2), channel_id=1, source_target_pairs={{0,1},{1,0},{2,3},{3,2},{4,5},{5,4},{6,7},{7,6},{8,9},{9,8},{10,11... | collective-permute-start | bytes 196616 | tf_op jit(solution)/shard_map/ppermute | solution.py:11
  132.1 2.6 %collective-permute-done.4 = f32[2,8,1,2,512]{4,3,2,1,0:T(2,128)S(1)} collective-permute-done((f32[2,8,1,2,512]{4,3,2,1,0:T(2,128)S(1)}, f32[2,8,1,2,512]{4,3,2,1,0:T(2,128)S(1)}, u32[]{:S(2)}, u32[]{:S(2)}) %collective-permute-start.4) | collective-permute-done | bytes 65568 | tf_op jit(solution)/shard_map/ppermute | solution.py:11
  134.8 1.2 collective-permute-done.5
  136.1 1.7 %collective-permute-start.6 = (f32[2,8,1,2,512]{4,3,2,1,0:T(2,128)S(1)}, f32[2,8,1,2,512]{4,3,2,1,0:T(2,128)S(1)}, u32[]{:S(2)}, u32[]{:S(2)}) collective-permute-start(f32[2,8,1,2,512]{4,3,2,1,0:T(2,128)S(1)} %add.47), channel_id=1, source_target_pairs={{0,16},{8,24},{16,0},{24,8},{1,17},{9,25},{17,1},{25,9},{2,18},{10... | collective-permute-start | bytes 196616 | tf_op jit(solution)/shard_map/ppermute | solution.py:11
  137.8 2.7 %collective-permute-done.6 = f32[2,8,1,2,512]{4,3,2,1,0:T(2,128)S(1)} collective-permute-done((f32[2,8,1,2,512]{4,3,2,1,0:T(2,128)S(1)}, f32[2,8,1,2,512]{4,3,2,1,0:T(2,128)S(1)}, u32[]{:S(2)}, u32[]{:S(2)}) %collective-permute-start.6) | collective-permute-done | bytes 65568 | tf_op jit(solution)/shard_map/ppermute | solution.py:11
  140.5 3.9 %collective-permute-start.7 = (f32[2,8,1,2,512]{4,3,2,1,0:T(2,128)S(1)}, f32[2,8,1,2,512]{4,3,2,1,0:T(2,128)S(1)}, u32[]{:S(2)}, u32[]{:S(2)}) collective-permute-start(f32[2,8,1,2,512]{4,3,2,1,0:T(2,128)S(1)} %add.48), channel_id=1, source_target_pairs={{0,32},{32,0},{64,96},{96,64},{128,160},{160,128},{192,224},{224,1... | collective-permute-start | bytes 196616 | tf_op jit(solution)/shard_map/ppermute | solution.py:11
  144.4 2.2 %collective-permute-done.7 = f32[2,8,1,2,512]{4,3,2,1,0:T(2,128)S(1)} collective-permute-done((f32[2,8,1,2,512]{4,3,2,1,0:T(2,128)S(1)}, f32[2,8,1,2,512]{4,3,2,1,0:T(2,128)S(1)}, u32[]{:S(2)}, u32[]{:S(2)}) %collective-permute-start.7) | collective-permute-done | bytes 65568 | tf_op jit(solution)/shard_map/ppermute | solution.py:11
  146.7 2.3 %collective-permute-start.8 = (f32[2,8,1,2,512]{4,3,2,1,0:T(2,128)S(1)}, f32[2,8,1,2,512]{4,3,2,1,0:T(2,128)S(1)}, u32[]{:S(2)}, u32[]{:S(2)}) collective-permute-start(f32[2,8,1,2,512]{4,3,2,1,0:T(2,128)S(1)} %add.49), channel_id=1, source_target_pairs={{0,64},{32,96},{64,0},{96,32},{128,192},{160,224},{192,128},{224,1... | collective-permute-start | bytes 196616 | tf_op jit(solution)/shard_map/ppermute | solution.py:11
  149.0 3.0 %collective-permute-done.8 = f32[2,8,1,2,512]{4,3,2,1,0:T(2,128)S(1)} collective-permute-done((f32[2,8,1,2,512]{4,3,2,1,0:T(2,128)S(1)}, f32[2,8,1,2,512]{4,3,2,1,0:T(2,128)S(1)}, u32[]{:S(2)}, u32[]{:S(2)}) %collective-permute-start.8) | collective-permute-done | bytes 65568 | tf_op jit(solution)/shard_map/ppermute | solution.py:11
  152.0 5.3 %collective-permute-start.9 = (f32[2,8,1,2,512]{4,3,2,1,0:T(2,128)S(1)}, f32[2,8,1,2,512]{4,3,2,1,0:T(2,128)S(1)}, u32[]{:S(2)}, u32[]{:S(2)}) collective-permute-start(f32[2,8,1,2,512]{4,3,2,1,0:T(2,128)S(1)} %add.50), channel_id=1, source_target_pairs={{0,128},{32,160},{64,192},{96,224},{128,0},{160,32},{192,64},{224,... | collective-permute-start | bytes 196616 | tf_op jit(solution)/shard_map/ppermute | solution.py:11
  157.3 0.6 dynamic_slice.3
  159.8 1.0 collective-permute-done.9
  162.1 0.6 pad_maximum_fusion.1
  (26 shorter events, 3.3 us)
Async XLA Ops:
  1.7 2.7 %collective-permute-start = (bf16[2,64,4096]{2,1,0:T(8,128)(2,1)S(1)}, bf16[2,64,4096]{2,1,0:T(8,128)(2,1)S(1)}, u32[]{:S(2)}, u32[]{:S(2)}) collective-permute-start(bf16[2,64,4096]{2,1,0:T(8,128)(2,1)S(1)} %get-tuple-element.17), channel_id=1, source_target_pairs={{0,8},{8,0},{16,24},{24,16},{1,9},{9,1},{17,25},{25,17},{2,10},{10... | collective-permute-start | bytes 3145736 | tf_op jit(solution)/shard_map/ppermute | solution.py:11
  4.6 97.2 %collective-permute-start.1 = (bf16[2,128,4096]{2,1,0:T(8,128)(2,1)S(1)}, bf16[2,128,4096]{2,1,0:T(8,128)(2,1)}, u32[]{:S(2)}, u32[]{:S(2)}) collective-permute-start(bf16[2,128,4096]{2,1,0:T(8,128)(2,1)S(1)} %pad_maximum_fusion), channel_id=1, source_target_pairs={{0,128},{32,160},{64,192},{96,224},{128,0},{160,32},{192,64},{224,... | collective-permute-start | bytes 6291464 | tf_op jit(solution)/shard_map/ppermute | solution.py:11
  114.8 42.5 %copy-start.1 = (s32[32]{0:T(128)S(1)}, s32[32]{0:T(128)}, u32[]{:S(2)}) copy-start(s32[32]{0:T(128)} %param.7) | copy-start | bytes 388
  114.8 46.0 %copy-start = (bf16[2,512,512]{2,1,0:T(8,128)(2,1)S(1)}, bf16[2,512,512]{2,1,0:T(8,128)(2,1)}, u32[]{:S(2)}) copy-start(bf16[2,512,512]{2,1,0:T(8,128)(2,1)} %param.6) | copy-start | bytes 3145732
  115.4 8.0 %collective-permute-start.2 = (f32[2,8,4,2,512]{4,3,2,1,0:T(2,128)S(1)}, f32[2,8,4,2,512]{4,3,2,1,0:T(2,128)S(1)}, u32[]{:S(2)}, u32[]{:S(2)}) collective-permute-start(f32[2,8,4,2,512]{4,3,2,1,0:T(2,128)S(1)} %broadcast_select_fusion), channel_id=1, source_target_pairs={{0,4},{1,5},{2,6},{3,7},{4,0},{5,1},{6,2},{7,3},{8,12},{9,13},{10,... | collective-permute-start | bytes 786440 | tf_op jit(solution)/shard_map/ppermute | solution.py:11
  123.6 5.1 %collective-permute-start.3 = (f32[2,8,2,2,512]{4,3,2,1,0:T(2,128)S(1)}, f32[2,8,2,2,512]{4,3,2,1,0:T(2,128)S(1)}, u32[]{:S(2)}, u32[]{:S(2)}) collective-permute-start(f32[2,8,2,2,512]{4,3,2,1,0:T(2,128)S(1)} %broadcast_select_fusion.1), channel_id=1, source_target_pairs={{0,2},{1,3},{2,0},{3,1},{4,6},{5,7},{6,4},{7,5},{8,10},{9,11},{10,... | collective-permute-start | bytes 393224 | tf_op jit(solution)/shard_map/ppermute | solution.py:11
  128.8 5.9 %collective-permute-start.4 = (f32[2,8,1,2,512]{4,3,2,1,0:T(2,128)S(1)}, f32[2,8,1,2,512]{4,3,2,1,0:T(2,128)S(1)}, u32[]{:S(2)}, u32[]{:S(2)}) collective-permute-start(f32[2,8,1,2,512]{4,3,2,1,0:T(2,128)S(1)} %broadcast_select_fusion.2), channel_id=1, source_target_pairs={{0,1},{1,0},{2,3},{3,2},{4,5},{5,4},{6,7},{7,6},{8,9},{9,8},{10,11... | collective-permute-start | bytes 196616 | tf_op jit(solution)/shard_map/ppermute | solution.py:11
  134.7 1.3 collective-permute-start.5
  136.1 4.4 %collective-permute-start.6 = (f32[2,8,1,2,512]{4,3,2,1,0:T(2,128)S(1)}, f32[2,8,1,2,512]{4,3,2,1,0:T(2,128)S(1)}, u32[]{:S(2)}, u32[]{:S(2)}) collective-permute-start(f32[2,8,1,2,512]{4,3,2,1,0:T(2,128)S(1)} %add.47), channel_id=1, source_target_pairs={{0,16},{8,24},{16,0},{24,8},{1,17},{9,25},{17,1},{25,9},{2,18},{10... | collective-permute-start | bytes 196616 | tf_op jit(solution)/shard_map/ppermute | solution.py:11
  140.5 6.2 %collective-permute-start.7 = (f32[2,8,1,2,512]{4,3,2,1,0:T(2,128)S(1)}, f32[2,8,1,2,512]{4,3,2,1,0:T(2,128)S(1)}, u32[]{:S(2)}, u32[]{:S(2)}) collective-permute-start(f32[2,8,1,2,512]{4,3,2,1,0:T(2,128)S(1)} %add.48), channel_id=1, source_target_pairs={{0,32},{32,0},{64,96},{96,64},{128,160},{160,128},{192,224},{224,1... | collective-permute-start | bytes 196616 | tf_op jit(solution)/shard_map/ppermute | solution.py:11
  146.7 5.3 %collective-permute-start.8 = (f32[2,8,1,2,512]{4,3,2,1,0:T(2,128)S(1)}, f32[2,8,1,2,512]{4,3,2,1,0:T(2,128)S(1)}, u32[]{:S(2)}, u32[]{:S(2)}) collective-permute-start(f32[2,8,1,2,512]{4,3,2,1,0:T(2,128)S(1)} %add.49), channel_id=1, source_target_pairs={{0,64},{32,96},{64,0},{96,32},{128,192},{160,224},{192,128},{224,1... | collective-permute-start | bytes 196616 | tf_op jit(solution)/shard_map/ppermute | solution.py:11
  152.0 8.8 %collective-permute-start.9 = (f32[2,8,1,2,512]{4,3,2,1,0:T(2,128)S(1)}, f32[2,8,1,2,512]{4,3,2,1,0:T(2,128)S(1)}, u32[]{:S(2)}, u32[]{:S(2)}) collective-permute-start(f32[2,8,1,2,512]{4,3,2,1,0:T(2,128)S(1)} %add.50), channel_id=1, source_target_pairs={{0,128},{32,160},{64,192},{96,224},{128,0},{160,32},{192,64},{224,... | collective-permute-start | bytes 196616 | tf_op jit(solution)/shard_map/ppermute | solution.py:11

commit v3 on v2

--- a/solution.py
+++ b/solution.py
@@ -51,11 +51,9 @@
     blocks = partial_s.shape[1] // RB
     own_count = RB // n_sl
     q = partial_s.reshape(2, blocks, n_sl, own_count, partial_s.shape[2])
-    q = halving(q, "sl", 2)
-    q = doubling(q, "sb")
-    q = doubling(q, "sa")
-    group = lax.axis_index("sa") * lax.axis_size("sb") + lax.axis_index("sb")
-    chosen = jnp.take(q[:, :, 0], group_rows[group], axis=1)
+    q = lax.all_to_all(q, "sl", 2, 2, tiled=True).sum(axis=2)
+    wanted = jnp.take(q, group_rows, axis=1)
+    chosen = lax.all_to_all(wanted, ("sa", "sb"), 1, 1, tiled=True).sum(axis=1)
     gates = final_gates.astype(jnp.float32)
     out_real, out_imag = complex_dot(chosen[0], chosen[1], gates, precision=lax.Precision.HIGHEST)
     return jnp.concatenate([out_real, out_imag], axis=1)

time: 163 us -> 152 us (0.933)
  blocking collectives: 0 us -> 21.1 us
  waiting for transfers between devices: 116 us -> 101 us
  starting transfers between devices: 26.6 us -> 14.8 us
  matrix products: 14.2 us -> 8.7 us
  between operations: 2.11 us -> 0.12 us
    ppermute x10 -> x2, waiting for transfers between devices: 116 us -> 92.6 us  [swapped(): lax.ppermute(shard, axis, [(i, i ^ 1 << apart) for i in range(lax.axis_si...]
    all_to_all x0 -> x1, blocking collectives: none -> 21.1 us  [local(): chosen = lax.all_to_all(wanted, ('sa', 'sb'), 1, 1, tiled=True).sum(axis=1)]
    ppermute x10 -> x2, starting transfers between devices: 26.6 us -> 7.37 us  [swapped(): lax.ppermute(shard, axis, [(i, i ^ 1 << apart) for i in range(lax.axis_si...]
    all_to_all x0 -> x1, waiting for transfers between devices: none -> 8.19 us  [local(): q = lax.all_to_all(q, 'sl', 2, 2, tiled=True).sum(axis=2)]
    all_to_all x0 -> x1, starting transfers between devices: none -> 7.46 us  [local(): q = lax.all_to_all(q, 'sl', 2, 2, tiled=True).sum(axis=2)]
    dot_general x8, matrix products: 14.2 us -> 8.7 us  [complex_dot(): jnp.dot(a, b, preferred_element_type=jnp.float32, precision=precision)]
  transfers between devices with their start and end apart: 10 -> 3, of which waited for: 10 -> 3; matrix products, arithmetic and copies ran while one was open for 0% -> 0% of each run, Pallas kernels for 0% -> 0%
where the time goes in v3:
time: 152 us; the launch traced here: 151 us
  waiting for transfers between devices  101 us (66%)
  blocking collectives  21.1 us (14%)
  starting transfers between devices  14.8 us (10%)
  matrix products  8.7 us (6%)
  local copies, waits for them, and re-layouts  2.81 us (2%)
  other arithmetic  2.39 us (2%)
    ppermute x2, waiting for transfers between devices, swapped(): lax.ppermute(shard, axis, [(i, i ^ 1 << apart) for i in range(lax.axis_si...  92.6 us
    all_to_all x1, blocking collectives, local(): chosen = lax.all_to_all(wanted, ('sa', 'sb'), 1, 1, tiled=True).sum(axis=1)  21.1 us
    dot_general x8, matrix products, complex_dot(): jnp.dot(a, b, preferred_element_type=jnp.float32, precision=precision)  8.7 us
    all_to_all x1, waiting for transfers between devices, local(): q = lax.all_to_all(q, 'sl', 2, 2, tiled=True).sum(axis=2)  8.19 us
    all_to_all x1, starting transfers between devices, local(): q = lax.all_to_all(q, 'sl', 2, 2, tiled=True).sum(axis=2)  7.46 us
    ppermute x2, starting transfers between devices, swapped(): lax.ppermute(shard, axis, [(i, i ^ 1 << apart) for i in range(lax.axis_si...  7.37 us
  transfers between devices with their start and end apart: 3, of which 3 were waited for; matrix products, arithmetic and copies ran while one was open for 0% of the time, Pallas kernels for 0%

profile of v3, /device:TPU:2, one launch (start us, length us, event | category | flops | bytes accessed | tf_op | source)
XLA Modules:
  0.0 150.7 jit_solution(8966428822578499863)
XLA Ops:
  0.0 1.8 %fusion.34 = (bf16[2,64,4096]{2,1,0:T(8,128)(2,1)S(1)}, bf16[2,64,4096]{2,1,0:T(8,128)(2,1)S(1)}) fusion(bf16[2,128,4096]{2,1,0:T(8,128)(2,1)} %bitcast.47), kind=kLoop, calls=%fused_computation.41 | loop fusion | bytes 4194304 | tf_op jit(solution)/shard_map/slice | solution.py:44
  1.9 0.1 collective-permute-start
  2.0 2.6 %collective-permute-done = bf16[2,64,4096]{2,1,0:T(8,128)(2,1)S(1)} collective-permute-done((bf16[2,64,4096]{2,1,0:T(8,128)(2,1)S(1)}, bf16[2,64,4096]{2,1,0:T(8,128)(2,1)S(1)}, u32[]{:S(2)}, u32[]{:S(2)}) %collective-permute-start) | collective-permute-done | bytes 1048608 | tf_op jit(solution)/shard_map/ppermute | solution.py:11
  4.6 0.2 pad_maximum_fusion
  4.8 7.3 %collective-permute-start.1 = (bf16[2,128,4096]{2,1,0:T(8,128)(2,1)S(1)}, bf16[2,128,4096]{2,1,0:T(8,128)(2,1)S(1)}, u32[]{:S(2)}, u32[]{:S(2)}) collective-permute-start(bf16[2,128,4096]{2,1,0:T(8,128)(2,1)S(1)} %pad_maximum_fusion), channel_id=1, source_target_pairs={{0,128},{32,160},{64,192},{96,224},{128,0},{160,32},{192,64},{224,... | collective-permute-start | bytes 6291464 | tf_op jit(solution)/shard_map/ppermute | solution.py:11
  12.1 89.9 %collective-permute-done.1 = bf16[2,128,4096]{2,1,0:T(8,128)(2,1)S(1)} collective-permute-done((bf16[2,128,4096]{2,1,0:T(8,128)(2,1)S(1)}, bf16[2,128,4096]{2,1,0:T(8,128)(2,1)S(1)}, u32[]{:S(2)}, u32[]{:S(2)}) %collective-permute-start.1) | collective-permute-done | bytes 2097184 | tf_op jit(solution)/shard_map/ppermute | solution.py:11
  102.0 0.8 fusion.2
  102.8 0.8 fusion.21
  103.6 0.1 stack.9
  103.6 2.9 %fusion.4 = f32[128,512]{1,0:T(8,128)S(1)} fusion(bf16[1,2,4096,512]{3,2,1,0:T(8,128)(2,1)} %param.5, bf16[2,128,4096]{2,1,0:T(8,128)(2,1)S(1)} %collective-permute-done.1), kind=kOutput, calls=%fused_computation.5 | convolution fusion | flops 536870912 | bytes 5505024 | tf_op jit(solution)/shard_map/dot_general | solution.py:15
  106.6 3.0 %fusion.18 = bf16[128,512]{1,0:T(8,128)(2,1)S(1)} fusion(f32[128,512]{1,0:T(8,128)S(1)} %fusion.4, bf16[1,2,4096,512]{3,2,1,0:T(8,128)(2,1)} %param.5, bf16[2,128,4096]{2,1,0:T(8,128)(2,1)S(1)} %collective-permute-done.1), kind=kOutput, calls=%fused_computation.16 | convolution fusion | flops 537001984 | bytes 5636096 | tf_op jit(solution)/shard_map/dot_general | solution.py:15
  109.6 1.1 copy_convert_fusion
  110.7 7.5 %all-to-all-start = ((f32[2,8,8,2,512]{4,3,1,0,2:T(2,128)}), f32[2,8,8,2,512]{4,3,1,0,2:T(2,128)S(1)}, u32[]{:S(2)}, u32[]{:S(2)}) async-start(f32[2,8,8,2,512]{4,3,1,0,2:T(2,128)} %copy_convert_fusion), calls=%async_computation | async-start | bytes 1048576 | tf_op jit(solution)/shard_map/all_to_all | solution.py:54
  118.2 8.2 %all-to-all-done = f32[2,8,8,2,512]{4,3,1,0,2:T(2,128)S(1)} async-done(((f32[2,8,8,2,512]{4,3,1,0,2:T(2,128)}), f32[2,8,8,2,512]{4,3,1,0,2:T(2,128)S(1)}, u32[]{:S(2)}, u32[]{:S(2)}) %all-to-all-start) | async-done | bytes 524320 | tf_op jit(solution)/shard_map/all_to_all | solution.py:54
  126.4 0.2 reduce_sum.18
  126.6 0.8 gather_fusion
  127.4 0.2 select_bitcast_fusion
  127.6 21.1 %all_to_all.10 = f32[2,32,2,512]{3,2,0,1:T(2,128)S(1)} all-to-all(f32[2,32,2,512]{3,2,0,1:T(2,128)S(1)} %select_bitcast_fusion), channel_id=1, replica_groups=mesh['sa'=8,'sb'=4,'sl'=8] {'sa','sb'}, dimensions={1} | all-to-all | bytes 524288 | tf_op jit(solution)/shard_map/all_to_all | solution.py:56
  148.8 0.1 reduce_sum.19
  148.9 0.3 fusion.28
  149.2 0.3 fusion.24
  149.5 0.3 convolution_subtract_fusion
  149.8 0.3 convolution_add_fusion
  150.1 0.6 pad_maximum_fusion.2
  (10 shorter events, 0.1 us)
Async XLA Ops:
  0.0 102.0 %copy-start.1 = (bf16[1,2,4096,512]{3,2,1,0:T(8,128)(2,1)S(1)}, bf16[1,2,4096,512]{3,2,1,0:T(8,128)(2,1)}, u32[]{:S(2)}) copy-start(bf16[1,2,4096,512]{3,2,1,0:T(8,128)(2,1)} %param.5) | copy-start | bytes 25165828
  1.9 2.7 %collective-permute-start = (bf16[2,64,4096]{2,1,0:T(8,128)(2,1)S(1)}, bf16[2,64,4096]{2,1,0:T(8,128)(2,1)S(1)}, u32[]{:S(2)}, u32[]{:S(2)}) collective-permute-start(bf16[2,64,4096]{2,1,0:T(8,128)(2,1)S(1)} %get-tuple-element.6), channel_id=1, source_target_pairs={{0,8},{8,0},{16,24},{24,16},{1,9},{9,1},{17,25},{25,17},{2,10},{10... | collective-permute-start | bytes 3145736 | tf_op jit(solution)/shard_map/ppermute | solution.py:11
  4.8 97.2 %collective-permute-start.1 = (bf16[2,128,4096]{2,1,0:T(8,128)(2,1)S(1)}, bf16[2,128,4096]{2,1,0:T(8,128)(2,1)S(1)}, u32[]{:S(2)}, u32[]{:S(2)}) collective-permute-start(bf16[2,128,4096]{2,1,0:T(8,128)(2,1)S(1)} %pad_maximum_fusion), channel_id=1, source_target_pairs={{0,128},{32,160},{64,192},{96,224},{128,0},{160,32},{192,64},{224,... | collective-permute-start | bytes 6291464 | tf_op jit(solution)/shard_map/ppermute | solution.py:11
  106.5 11.6 %copy-start.2 = (s32[32]{0:T(128)S(1)}, s32[32]{0:T(128)}, u32[]{:S(2)}) copy-start(s32[32]{0:T(128)} %param.7) | copy-start | bytes 388
  106.6 42.3 %copy-start = (bf16[2,512,512]{2,1,0:T(8,128)(2,1)S(1)}, bf16[2,512,512]{2,1,0:T(8,128)(2,1)}, u32[]{:S(2)}) copy-start(bf16[2,512,512]{2,1,0:T(8,128)(2,1)} %param.6) | copy-start | bytes 3145732
  110.7 15.7 %all-to-all-start = ((f32[2,8,8,2,512]{4,3,1,0,2:T(2,128)}), f32[2,8,8,2,512]{4,3,1,0,2:T(2,128)S(1)}, u32[]{:S(2)}, u32[]{:S(2)}) async-start(f32[2,8,8,2,512]{4,3,1,0,2:T(2,128)} %copy_convert_fusion), calls=%async_computation | async-start | bytes 1048576 | tf_op jit(solution)/shard_map/all_to_all | solution.py:54

commit v4 on v1

v4 whole, which is shorter than its diff:
```python
import jax
import jax.numpy as jnp
from jax import lax
from jax.sharding import PartitionSpec as P

RB = 16
ALL = ("sa", "sb", "sl")


def complex_dot(left_real, left_imag, right, precision=None):
    dot = lambda a, b: jnp.dot(a, b, preferred_element_type=jnp.float32, precision=precision)
    real = dot(left_real, right[0]) - dot(left_imag, right[1])
    imag = dot(left_real, right[1]) + dot(left_imag, right[0])
    return (real, imag)


def stacked_dot(stem, subtree):
    rows = stem.shape[1]
    left = jnp.concatenate(
        [jnp.concatenate([stem[0], -stem[1]], axis=1), jnp.concatenate([stem[1], stem[0]], axis=1)], axis=0
    )
    right = subtree.reshape(-1, subtree.shape[-1])
    out = jnp.dot(left, right, preferred_element_type=jnp.float32)
    return out.reshape(2, rows, out.shape[-1])


def pair_sums(partial_s, n_sl):
    blocks = partial_s.shape[1] // RB
    q = partial_s.astype(jnp.bfloat16).astype(jnp.float32)
    q = q.reshape(2, blocks, n_sl, RB // n_sl, partial_s.shape[2])
    return lax.all_to_all(q, "sl", 2, 2, tiled=True).sum(axis=2)


def local(stem_cache, subtree_cache, final_gates, group_rows):
    stem = stem_cache[0]
    subtree = subtree_cache[0]
    half = stem.shape[1] // 2
    n_sa, n_sb, n_sl = lax.axis_size("sa"), lax.axis_size("sb"), lax.axis_size("sl")
    flip = n_sa // 2
    lower = lax.ppermute(stem[:, :half], "sa", [(i, i ^ flip) for i in range(n_sa)])
    upper_src, _ = lax.optimization_barrier((stem[:, half:], lower))
    upper = lax.ppermute(
        upper_src,
        ("sa", "sb"),
        [(a * n_sb + b, (a ^ flip) * n_sb + (b ^ 1)) for a in range(n_sa) for b in range(n_sb)],
    )
    q_lower = pair_sums(stacked_dot(lower, subtree), n_sl)
    q_upper = pair_sums(stacked_dot(upper, subtree), n_sl)
    q = jnp.concatenate([q_lower, q_upper], axis=1)
    wanted = jnp.take(q, group_rows, axis=1)
    chosen = lax.all_to_all(wanted, ("sa", "sb"), 1, 1, tiled=True).sum(axis=1)
    gates = final_gates.astype(jnp.float32)
    out_real, out_imag = complex_dot(chosen[0], chosen[1], gates, precision=lax.Precision.HIGHEST)
    return jnp.concatenate([out_real, out_imag], axis=1)


def solution(mesh):
    return jax.shard_map(
        local,
        mesh=mesh,
        in_specs=(
            P(ALL, None, None, None),
            P(ALL, None, None, None),
            P(),
            P(),
        ),
        out_specs=P(ALL, None),
        check_vma=False,
    )
```

time: 390 us -> 147 us (0.38)
  waiting for transfers between devices: 350 us -> 70.5 us
  blocking collectives: 0 us -> 39 us
  starting transfers between devices: 7.37 us -> 22.2 us
  between operations: 13.5 us -> 0.15 us
  matrix products: 13.3 us -> 7.24 us
    psum x1 -> x0, waiting for transfers between devices: 258 us -> none  [local(): summed = lax.psum(partial_s, ALL)]
    all_to_all x0 -> x1, blocking collectives: none -> 39 us  [local(): chosen = lax.all_to_all(wanted, ('sa', 'sb'), 1, 1, tiled=True).sum(axis=1)]
    ppermute x2, waiting for transfers between devices: 91.9 us -> 63 us  [the longest x1 44.4 us: local(): lax.ppermute(stem[:, :half], 'sa', [(i, i ^ flip) for i in range(n_sa)])]
    all_to_all x0 -> x2, starting transfers between devices: none -> 14.9 us  [pair_sums(): return lax.all_to_all(q, 'sl', 2, 2, tiled=True).sum(axis=2)]
    dot_general x8 -> x4, matrix products: 13.3 us -> 1.26 us  [complex_dot(): jnp.dot(a, b, preferred_element_type=jnp.float32, precision=precision)]
    all_to_all x0 -> x2, waiting for transfers between devices: none -> 7.49 us  [pair_sums(): return lax.all_to_all(q, 'sl', 2, 2, tiled=True).sum(axis=2)]
    dot_general x0 -> x2, matrix products: none -> 5.98 us  [stacked_dot(): out = jnp.dot(left, right, preferred_element_type=jnp.float32)]
  transfers between devices with their start and end apart: 3 -> 4, of which waited for: 3 -> 3; matrix products, arithmetic and copies ran while one was open for 0% -> 6% of each run, Pallas kernels for 0% -> 0%
where the time goes in v4:
time: 147 us; the launch traced here: 145 us
  waiting for transfers between devices  70.5 us (48%)
  blocking collectives  39 us (27%)
  starting transfers between devices  22.2 us (15%)
  matrix products  7.24 us (5%)
  local copies, waits for them, and re-layouts  4.55 us (3%)
  other arithmetic  1.56 us (1%)
    ppermute x1, waiting for transfers between devices, local(): lax.ppermute(stem[:, :half], 'sa', [(i, i ^ flip) for i in range(n_sa)])  44.4 us
    all_to_all x1, blocking collectives, local(): chosen = lax.all_to_all(wanted, ('sa', 'sb'), 1, 1, tiled=True).sum(axis=1)  39 us
    ppermute x1, waiting for transfers between devices, local(): lax.ppermute(upper_src, ('sa', 'sb'), [(a * n_sb + b, (a ^ flip) * n_sb +...  18.7 us
    all_to_all x2, starting transfers between devices, pair_sums(): return lax.all_to_all(q, 'sl', 2, 2, tiled=True).sum(axis=2)  14.9 us
    all_to_all x2, waiting for transfers between devices, pair_sums(): return lax.all_to_all(q, 'sl', 2, 2, tiled=True).sum(axis=2)  7.49 us
    ppermute x1, starting transfers between devices, local(): lax.ppermute(stem[:, :half], 'sa', [(i, i ^ flip) for i in range(n_sa)])  7.28 us
    dot_general x2, matrix products, stacked_dot(): out = jnp.dot(left, right, preferred_element_type=jnp.float32)  5.98 us
  transfers between devices with their start and end apart: 4, of which 3 were waited for; matrix products, arithmetic and copies ran while one was open for 6% of the time, Pallas kernels for 0%

profile of v4, /device:TPU:2, one launch (start us, length us, event | category | flops | bytes accessed | tf_op | source)
XLA Modules:
  0.0 145.2 jit_solution(3992822391631107913)
XLA Ops:
  0.0 1.8 %fusion.14 = (bf16[2,64,4096]{2,1,0:T(8,128)(2,1)S(1)}, bf16[2,64,4096]{2,1,0:T(8,128)(2,1)S(1)}) fusion(bf16[2,128,4096]{2,1,0:T(8,128)(2,1)} %bitcast.46), kind=kLoop, calls=%fused_computation.33 | loop fusion | bytes 4194304 | tf_op jit(solution)/shard_map/slice | solution.py:40
  1.8 7.3 %collective-permute-start = (bf16[2,64,4096]{2,1,0:T(8,128)(2,1)S(1)}, bf16[2,64,4096]{2,1,0:T(8,128)(2,1)S(1)}, u32[]{:S(2)}, u32[]{:S(2)}) collective-permute-start(bf16[2,64,4096]{2,1,0:T(8,128)(2,1)S(1)} %get-tuple-element.7), channel_id=1, source_target_pairs={{0,128},{32,160},{64,192},{96,224},{128,0},{160,32},{192,64},{224,... | collective-permute-start | bytes 3145736 | tf_op jit(solution)/shard_map/ppermute | solution.py:40
  9.1 44.4 %collective-permute-done = bf16[2,64,4096]{2,1,0:T(8,128)(2,1)S(1)} collective-permute-done((bf16[2,64,4096]{2,1,0:T(8,128)(2,1)S(1)}, bf16[2,64,4096]{2,1,0:T(8,128)(2,1)S(1)}, u32[]{:S(2)}, u32[]{:S(2)}) %collective-permute-start) | collective-permute-done | bytes 1048608 | tf_op jit(solution)/shard_map/ppermute | solution.py:40
  53.6 0.2 maximum_maximum_fusion
  53.8 1.3 fusion.1
  55.1 0.1 reshape.26
  55.3 0.7 copy.9
  56.0 7.5 %all-to-all-start = ((f32[2,4,8,2,512]{4,3,1,0,2:T(2,128)}), f32[2,4,8,2,512]{4,3,1,0,2:T(2,128)S(1)}, u32[]{:S(2)}, u32[]{:S(2)}) async-start(f32[2,4,8,2,512]{4,3,1,0,2:T(2,128)} %copy.9), calls=%async_computation | async-start | bytes 524288 | tf_op jit(solution)/shard_map/all_to_all | solution.py:31
  63.4 18.7 %collective-permute-done.1 = bf16[2,64,4096]{2,1,0:T(8,128)(2,1)S(1)} collective-permute-done((bf16[2,64,4096]{2,1,0:T(8,128)(2,1)S(1)}, bf16[2,64,4096]{2,1,0:T(8,128)(2,1)S(1)}, u32[]{:S(2)}, u32[]{:S(2)}) %collective-permute-start.1) | collective-permute-done | bytes 1048608 | tf_op jit(solution)/shard_map/ppermute | solution.py:42
  82.2 0.2 maximum_maximum_fusion.1
  82.4 4.7 %fusion = f32[2,64,512]{2,1,0:T(8,128)S(1)} fusion(bf16[2,64,8192]{2,1,0:T(8,128)(2,1)S(1)} %bitcast.45, bf16[8192,512,1]{1,0,2:T(8,128)(2,1)} %bitcast.42), kind=kOutput, calls=%fused_computation.4 | convolution fusion | flops 1073872896 | bytes 10747904 | tf_op jit(solution)/shard_map/dot_general | solution.py:23
  87.1 0.1 reshape.28
  87.3 0.7 copy.10
  88.0 7.5 %all-to-all-start.1 = ((f32[2,4,8,2,512]{4,3,1,0,2:T(2,128)}), f32[2,4,8,2,512]{4,3,1,0,2:T(2,128)S(1)}, u32[]{:S(2)}, u32[]{:S(2)}) async-start(f32[2,4,8,2,512]{4,3,1,0,2:T(2,128)} %copy.10), calls=%async_computation.1 | async-start | bytes 524288 | tf_op jit(solution)/shard_map/all_to_all | solution.py:31
  95.6 7.5 %all-to-all-done.1 = f32[2,4,8,2,512]{4,3,1,0,2:T(2,128)S(1)} async-done(((f32[2,4,8,2,512]{4,3,1,0,2:T(2,128)}), f32[2,4,8,2,512]{4,3,1,0,2:T(2,128)S(1)}, u32[]{:S(2)}, u32[]{:S(2)}) %all-to-all-start.1) | async-done | bytes 262176 | tf_op jit(solution)/shard_map/all_to_all | solution.py:31
  103.2 0.8 gather_fusion
  104.1 0.2 select_bitcast_fusion
  104.2 39.0 %all_to_all.15 = f32[2,32,2,512]{3,2,0,1:T(2,128)S(1)} all-to-all(f32[2,32,2,512]{3,2,0,1:T(2,128)S(1)} %select_bitcast_fusion), channel_id=1, replica_groups=mesh['sa'=8,'sb'=4,'sl'=8] {'sa','sb'}, dimensions={1} | all-to-all | bytes 524288 | tf_op jit(solution)/shard_map/all_to_all | solution.py:51
  143.2 0.1 reduce_sum.29
  143.3 0.3 fusion.6
  143.6 0.3 fusion.2
  144.0 0.3 convolution_subtract_fusion
  144.3 0.3 convolution_add_fusion
  144.6 0.6 pad_maximum_fusion.1
  (18 shorter events, 0.5 us)
Async XLA Ops:
  0.0 9.1 %copy-start.2 = (s32[32]{0:T(128)S(1)}, s32[32]{0:T(128)}, u32[]{:S(2)}) copy-start(s32[32]{0:T(128)} %param.7) | copy-start | bytes 388
  0.0 53.8 %copy-start = (bf16[1,2,4096,512]{3,2,1,0:T(8,128)(2,1)S(1)}, bf16[1,2,4096,512]{3,2,1,0:T(8,128)(2,1)}, u32[]{:S(2)}) copy-start(bf16[1,2,4096,512]{3,2,1,0:T(8,128)(2,1)} %param.5) | copy-start | bytes 25165828
  1.8 51.7 %collective-permute-start = (bf16[2,64,4096]{2,1,0:T(8,128)(2,1)S(1)}, bf16[2,64,4096]{2,1,0:T(8,128)(2,1)S(1)}, u32[]{:S(2)}, u32[]{:S(2)}) collective-permute-start(bf16[2,64,4096]{2,1,0:T(8,128)(2,1)S(1)} %get-tuple-element.7), channel_id=1, source_target_pairs={{0,128},{32,160},{64,192},{96,224},{128,0},{160,32},{192,64},{224,... | collective-permute-start | bytes 3145736 | tf_op jit(solution)/shard_map/ppermute | solution.py:40
  53.5 28.6 %collective-permute-start.1 = (bf16[2,64,4096]{2,1,0:T(8,128)(2,1)S(1)}, bf16[2,64,4096]{2,1,0:T(8,128)(2,1)S(1)}, u32[]{:S(2)}, u32[]{:S(2)}) collective-permute-start(bf16[2,64,4096]{2,1,0:T(8,128)(2,1)S(1)} %get-tuple-element.6), channel_id=1, source_target_pairs={{0,136},{8,128},{16,152},{24,144},{32,168},{40,160},{48,184},{56,1... | collective-permute-start | bytes 3145736 | tf_op jit(solution)/shard_map/ppermute | solution.py:42
  56.0 32.1 %all-to-all-start = ((f32[2,4,8,2,512]{4,3,1,0,2:T(2,128)}), f32[2,4,8,2,512]{4,3,1,0,2:T(2,128)S(1)}, u32[]{:S(2)}, u32[]{:S(2)}) async-start(f32[2,4,8,2,512]{4,3,1,0,2:T(2,128)} %copy.9), calls=%async_computation | async-start | bytes 524288 | tf_op jit(solution)/shard_map/all_to_all | solution.py:31
  82.4 60.9 %copy-start.1 = (bf16[2,512,512]{2,1,0:T(8,128)(2,1)S(1)}, bf16[2,512,512]{2,1,0:T(8,128)(2,1)}, u32[]{:S(2)}) copy-start(bf16[2,512,512]{2,1,0:T(8,128)(2,1)} %param.6) | copy-start | bytes 3145732
  88.0 15.1 %all-to-all-start.1 = ((f32[2,4,8,2,512]{4,3,1,0,2:T(2,128)}), f32[2,4,8,2,512]{4,3,1,0,2:T(2,128)S(1)}, u32[]{:S(2)}, u32[]{:S(2)}) async-start(f32[2,4,8,2,512]{4,3,1,0,2:T(2,128)} %copy.10), calls=%async_computation.1 | async-start | bytes 524288 | tf_op jit(solution)/shard_map/all_to_all | solution.py:31

commit v5 on v4

--- a/solution.py
+++ b/solution.py
@@ -26,7 +26,7 @@
 
 def pair_sums(partial_s, n_sl):
     blocks = partial_s.shape[1] // RB
-    q = partial_s.astype(jnp.bfloat16).astype(jnp.float32)
+    q = lax.reduce_precision(partial_s, exponent_bits=8, mantissa_bits=7)
     q = q.reshape(2, blocks, n_sl, RB // n_sl, partial_s.shape[2])
     return lax.all_to_all(q, "sl", 2, 2, tiled=True).sum(axis=2)
 

time: 147 us -> 147 us (level)
  no operation moved by 1% of the time
where the time goes in v5:
time: 147 us; the launch traced here: 145 us
  waiting for transfers between devices  70.5 us (48%)
  blocking collectives  39 us (27%)
  starting transfers between devices  22.2 us (15%)
  matrix products  7.25 us (5%)
  local copies, waits for them, and re-layouts  4.55 us (3%)
  other arithmetic  1.56 us (1%)
    ppermute x1, waiting for transfers between devices, local(): lax.ppermute(stem[:, :half], 'sa', [(i, i ^ flip) for i in range(n_sa)])  44.4 us
    all_to_all x1, blocking collectives, local(): chosen = lax.all_to_all(wanted, ('sa', 'sb'), 1, 1, tiled=True).sum(axis=1)  39 us
    ppermute x1, waiting for transfers between devices, local(): lax.ppermute(upper_src, ('sa', 'sb'), [(a * n_sb + b, (a ^ flip) * n_sb +...  18.6 us
    all_to_all x2, starting transfers between devices, pair_sums(): return lax.all_to_all(q, 'sl', 2, 2, tiled=True).sum(axis=2)  14.9 us
    all_to_all x2, waiting for transfers between devices, pair_sums(): return lax.all_to_all(q, 'sl', 2, 2, tiled=True).sum(axis=2)  7.49 us
    ppermute x1, starting transfers between devices, local(): lax.ppermute(stem[:, :half], 'sa', [(i, i ^ flip) for i in range(n_sa)])  7.28 us
    dot_general x2, matrix products, stacked_dot(): out = jnp.dot(left, right, preferred_element_type=jnp.float32)  5.99 us
  transfers between devices with their start and end apart: 4, of which 3 were waited for; matrix products, arithmetic and copies ran while one was open for 6% of the time, Pallas kernels for 0%

profile of v5, /device:TPU:2, one launch (start us, length us, event | category | flops | bytes accessed | tf_op | source)
XLA Modules:
  0.0 145.2 jit_solution(10907885915113096323)
XLA Ops:
  0.0 1.8 %fusion.12 = (bf16[2,64,4096]{2,1,0:T(8,128)(2,1)S(1)}, bf16[2,64,4096]{2,1,0:T(8,128)(2,1)S(1)}) fusion(bf16[2,128,4096]{2,1,0:T(8,128)(2,1)} %bitcast.46), kind=kLoop, calls=%fused_computation.31 | loop fusion | bytes 4194304 | tf_op jit(solution)/shard_map/slice | solution.py:40
  1.8 7.3 %collective-permute-start = (bf16[2,64,4096]{2,1,0:T(8,128)(2,1)S(1)}, bf16[2,64,4096]{2,1,0:T(8,128)(2,1)S(1)}, u32[]{:S(2)}, u32[]{:S(2)}) collective-permute-start(bf16[2,64,4096]{2,1,0:T(8,128)(2,1)S(1)} %get-tuple-element.7), channel_id=1, source_target_pairs={{0,128},{32,160},{64,192},{96,224},{128,0},{160,32},{192,64},{224,... | collective-permute-start | bytes 3145736 | tf_op jit(solution)/shard_map/ppermute | solution.py:40
  9.1 44.4 %collective-permute-done = bf16[2,64,4096]{2,1,0:T(8,128)(2,1)S(1)} collective-permute-done((bf16[2,64,4096]{2,1,0:T(8,128)(2,1)S(1)}, bf16[2,64,4096]{2,1,0:T(8,128)(2,1)S(1)}, u32[]{:S(2)}, u32[]{:S(2)}) %collective-permute-start) | collective-permute-done | bytes 1048608 | tf_op jit(solution)/shard_map/ppermute | solution.py:40
  53.6 0.2 maximum_maximum_fusion
  53.8 1.3 convolution_reduce-precision_fusion.1
  55.1 0.1 reshape.15
  55.3 0.7 copy.9
  56.0 7.5 %all-to-all-start = ((f32[2,4,8,2,512]{4,3,1,0,2:T(2,128)}), f32[2,4,8,2,512]{4,3,1,0,2:T(2,128)S(1)}, u32[]{:S(2)}, u32[]{:S(2)}) async-start(f32[2,4,8,2,512]{4,3,1,0,2:T(2,128)} %copy.9), calls=%async_computation | async-start | bytes 524288 | tf_op jit(solution)/shard_map/all_to_all | solution.py:31
  63.4 18.6 %collective-permute-done.1 = bf16[2,64,4096]{2,1,0:T(8,128)(2,1)S(1)} collective-permute-done((bf16[2,64,4096]{2,1,0:T(8,128)(2,1)S(1)}, bf16[2,64,4096]{2,1,0:T(8,128)(2,1)S(1)}, u32[]{:S(2)}, u32[]{:S(2)}) %collective-permute-start.1) | collective-permute-done | bytes 1048608 | tf_op jit(solution)/shard_map/ppermute | solution.py:42
  82.2 0.2 maximum_maximum_fusion.1
  82.4 4.7 %convolution_reduce-precision_fusion = f32[2,64,512]{2,1,0:T(8,128)S(1)} fusion(bf16[2,64,8192]{2,1,0:T(8,128)(2,1)S(1)} %bitcast.45, bf16[8192,512,1]{1,0,2:T(8,128)(2,1)} %bitcast.42), kind=kOutput, calls=%fused_computation.3 | convolution fusion | flops 1073807360 | bytes 10747904 | tf_op jit(solution)/shard_map/dot_general | solution.py:23
  87.2 0.1 reshape.16
  87.3 0.7 copy.10
  88.0 7.5 %all-to-all-start.1 = ((f32[2,4,8,2,512]{4,3,1,0,2:T(2,128)}), f32[2,4,8,2,512]{4,3,1,0,2:T(2,128)S(1)}, u32[]{:S(2)}, u32[]{:S(2)}) async-start(f32[2,4,8,2,512]{4,3,1,0,2:T(2,128)} %copy.10), calls=%async_computation.1 | async-start | bytes 524288 | tf_op jit(solution)/shard_map/all_to_all | solution.py:31
  95.6 7.5 %all-to-all-done.1 = f32[2,4,8,2,512]{4,3,1,0,2:T(2,128)S(1)} async-done(((f32[2,4,8,2,512]{4,3,1,0,2:T(2,128)}), f32[2,4,8,2,512]{4,3,1,0,2:T(2,128)S(1)}, u32[]{:S(2)}, u32[]{:S(2)}) %all-to-all-start.1) | async-done | bytes 262176 | tf_op jit(solution)/shard_map/all_to_all | solution.py:31
  103.2 0.8 gather_fusion
  104.1 0.2 select_bitcast_fusion
  104.2 39.0 %all_to_all.15 = f32[2,32,2,512]{3,2,0,1:T(2,128)S(1)} all-to-all(f32[2,32,2,512]{3,2,0,1:T(2,128)S(1)} %select_bitcast_fusion), channel_id=1, replica_groups=mesh['sa'=8,'sb'=4,'sl'=8] {'sa','sb'}, dimensions={1} | all-to-all | bytes 524288 | tf_op jit(solution)/shard_map/all_to_all | solution.py:51
  143.2 0.1 reduce_sum.29
  143.3 0.3 fusion.4
  143.6 0.3 fusion
  144.0 0.3 convolution_subtract_fusion
  144.3 0.3 convolution_add_fusion
  144.6 0.6 pad_maximum_fusion.1
  (18 shorter events, 0.5 us)
Async XLA Ops:
  0.0 9.1 %copy-start.2 = (s32[32]{0:T(128)S(1)}, s32[32]{0:T(128)}, u32[]{:S(2)}) copy-start(s32[32]{0:T(128)} %param.7) | copy-start | bytes 388
  0.0 53.8 %copy-start = (bf16[1,2,4096,512]{3,2,1,0:T(8,128)(2,1)S(1)}, bf16[1,2,4096,512]{3,2,1,0:T(8,128)(2,1)}, u32[]{:S(2)}) copy-start(bf16[1,2,4096,512]{3,2,1,0:T(8,128)(2,1)} %param.5) | copy-start | bytes 25165828
  1.8 51.7 %collective-permute-start = (bf16[2,64,4096]{2,1,0:T(8,128)(2,1)S(1)}, bf16[2,64,4096]{2,1,0:T(8,128)(2,1)S(1)}, u32[]{:S(2)}, u32[]{:S(2)}) collective-permute-start(bf16[2,64,4096]{2,1,0:T(8,128)(2,1)S(1)} %get-tuple-element.7), channel_id=1, source_target_pairs={{0,128},{32,160},{64,192},{96,224},{128,0},{160,32},{192,64},{224,... | collective-permute-start | bytes 3145736 | tf_op jit(solution)/shard_map/ppermute | solution.py:40
  53.5 28.6 %collective-permute-start.1 = (bf16[2,64,4096]{2,1,0:T(8,128)(2,1)S(1)}, bf16[2,64,4096]{2,1,0:T(8,128)(2,1)S(1)}, u32[]{:S(2)}, u32[]{:S(2)}) collective-permute-start(bf16[2,64,4096]{2,1,0:T(8,128)(2,1)S(1)} %get-tuple-element.6), channel_id=1, source_target_pairs={{0,136},{8,128},{16,152},{24,144},{32,168},{40,160},{48,184},{56,1... | collective-permute-start | bytes 3145736 | tf_op jit(solution)/shard_map/ppermute | solution.py:42
  56.0 32.1 %all-to-all-start = ((f32[2,4,8,2,512]{4,3,1,0,2:T(2,128)}), f32[2,4,8,2,512]{4,3,1,0,2:T(2,128)S(1)}, u32[]{:S(2)}, u32[]{:S(2)}) async-start(f32[2,4,8,2,512]{4,3,1,0,2:T(2,128)} %copy.9), calls=%async_computation | async-start | bytes 524288 | tf_op jit(solution)/shard_map/all_to_all | solution.py:31
  82.4 60.9 %copy-start.1 = (bf16[2,512,512]{2,1,0:T(8,128)(2,1)S(1)}, bf16[2,512,512]{2,1,0:T(8,128)(2,1)}, u32[]{:S(2)}) copy-start(bf16[2,512,512]{2,1,0:T(8,128)(2,1)} %param.6) | copy-start | bytes 3145732
  88.0 15.1 %all-to-all-start.1 = ((f32[2,4,8,2,512]{4,3,1,0,2:T(2,128)}), f32[2,4,8,2,512]{4,3,1,0,2:T(2,128)S(1)}, u32[]{:S(2)}, u32[]{:S(2)}) async-start(f32[2,4,8,2,512]{4,3,1,0,2:T(2,128)} %copy.10), calls=%async_computation.1 | async-start | bytes 524288 | tf_op jit(solution)/shard_map/all_to_all | solution.py:31

commit v6 on v5

--- a/solution.py
+++ b/solution.py
@@ -34,19 +34,21 @@
 def local(stem_cache, subtree_cache, final_gates, group_rows):
     stem = stem_cache[0]
     subtree = subtree_cache[0]
-    half = stem.shape[1] // 2
+    rows = stem.shape[1]
+    half = rows // 2
     n_sa, n_sb, n_sl = lax.axis_size("sa"), lax.axis_size("sb"), lax.axis_size("sl")
     flip = n_sa // 2
-    lower = lax.ppermute(stem[:, :half], "sa", [(i, i ^ flip) for i in range(n_sa)])
-    upper_src, _ = lax.optimization_barrier((stem[:, half:], lower))
-    upper = lax.ppermute(
-        upper_src,
-        ("sa", "sb"),
-        [(a * n_sb + b, (a ^ flip) * n_sb + (b ^ 1)) for a in range(n_sa) for b in range(n_sb)],
-    )
-    q_lower = pair_sums(stacked_dot(lower, subtree), n_sl)
-    q_upper = pair_sums(stacked_dot(upper, subtree), n_sl)
-    q = jnp.concatenate([q_lower, q_upper], axis=1)
+    straight = [(i, i ^ flip) for i in range(n_sa)]
+    diagonal = [(a * n_sb + b, (a ^ flip) * n_sb + (b ^ 1)) for a in range(n_sa) for b in range(n_sb)]
+    cut = rows - rows // 4
+    lower = lax.ppermute(stem[:, :half], "sa", straight)
+    middle = lax.ppermute(stem[:, half:cut], ("sa", "sb"), diagonal)
+    last_src, _, _ = lax.optimization_barrier((stem[:, cut:], lower, middle))
+    last = lax.ppermute(last_src, ("sa", "sb"), diagonal)
+    first = jnp.concatenate([lower, middle], axis=1)
+    q_first = pair_sums(stacked_dot(first, subtree), n_sl)
+    q_last = pair_sums(stacked_dot(last, subtree), n_sl)
+    q = jnp.concatenate([q_first, q_last], axis=1)
     wanted = jnp.take(q, group_rows, axis=1)
     chosen = lax.all_to_all(wanted, ("sa", "sb"), 1, 1, tiled=True).sum(axis=1)
     gates = final_gates.astype(jnp.float32)

time: 147 us -> 145 us (0.986)
  blocking collectives: 39 us -> 15.3 us
  other arithmetic: 1.56 us -> 13.9 us
  starting transfers between devices: 22.2 us -> 26.9 us
  waiting for transfers between devices: 70.5 us -> 73.3 us
    all_to_all x1, blocking collectives: 39 us -> 15.3 us  [local(): chosen = lax.all_to_all(wanted, ('sa', 'sb'), 1, 1, tiled=True).sum(axis=1)]
    concatenate x2, other arithmetic: 0.37 us -> 12.7 us  [stacked_dot(): jnp.concatenate([jnp.concatenate([stem[0], -stem[1]], axis=1), jnp.concat...]
    ppermute x2 -> x3, starting transfers between devices: 7.28 us -> 13.7 us  [the longest x1 7.28 us: local(): lower = lax.ppermute(stem[:, :half], 'sa', straight)]
    ppermute x2 -> x3, waiting for transfers between devices: 63 us -> 65.6 us  [the longest x1 37 us: local(): middle = lax.ppermute(stem[:, half:cut], ('sa', 'sb'), diagonal)]
    all_to_all x2, starting transfers between devices: 14.9 us -> 13.2 us  [pair_sums(): return lax.all_to_all(q, 'sl', 2, 2, tiled=True).sum(axis=2)]
  transfers between devices with their start and end apart: 4 -> 5, of which waited for: 3 -> 4; matrix products, arithmetic and copies ran while one was open for 6% -> 16% of each run, Pallas kernels for 0% -> 0%
where the time goes in v6:
time: 145 us; the launch traced here: 143 us
  waiting for transfers between devices  73.3 us (51%)
  starting transfers between devices  26.9 us (19%)
  blocking collectives  15.3 us (11%)
  other arithmetic  13.9 us (10%)
  matrix products  7.99 us (6%)
  local copies, waits for them, and re-layouts  5.57 us (4%)
    ppermute x1, waiting for transfers between devices, local(): middle = lax.ppermute(stem[:, half:cut], ('sa', 'sb'), diagonal)  37 us
    ppermute x1, waiting for transfers between devices, local(): lower = lax.ppermute(stem[:, :half], 'sa', straight)  28.6 us
    all_to_all x1, blocking collectives, local(): chosen = lax.all_to_all(wanted, ('sa', 'sb'), 1, 1, tiled=True).sum(axis=1)  15.3 us
    all_to_all x2, starting transfers between devices, pair_sums(): return lax.all_to_all(q, 'sl', 2, 2, tiled=True).sum(axis=2)  13.2 us
    concatenate x2, other arithmetic, stacked_dot(): jnp.concatenate([jnp.concatenate([stem[0], -stem[1]], axis=1), jnp.concat...  12.7 us
    all_to_all x2, waiting for transfers between devices, pair_sums(): return lax.all_to_all(q, 'sl', 2, 2, tiled=True).sum(axis=2)  7.73 us
    ppermute x1, starting transfers between devices, local(): lower = lax.ppermute(stem[:, :half], 'sa', straight)  7.28 us
    dot_general x2, matrix products, stacked_dot(): out = jnp.dot(left, right, preferred_element_type=jnp.float32)  6.73 us
  transfers between devices with their start and end apart: 5, of which 4 were waited for; matrix products, arithmetic and copies ran while one was open for 16% of the time, Pallas kernels for 0%

profile of v6, /device:TPU:2, one launch (start us, length us, event | category | flops | bytes accessed | tf_op | source)
XLA Modules:
  0.0 143.2 jit_solution(6443140254697444658)
XLA Ops:
  0.0 1.3 slice.52
  1.3 7.3 %collective-permute-start = (bf16[2,64,4096]{2,1,0:T(8,128)(2,1)S(1)}, bf16[2,64,4096]{2,1,0:T(8,128)(2,1)S(1)}, u32[]{:S(2)}, u32[]{:S(2)}) collective-permute-start(bf16[2,64,4096]{2,1,0:T(8,128)(2,1)S(1)} %slice.52), channel_id=1, source_target_pairs={{0,128},{32,160},{64,192},{96,224},{128,0},{160,32},{192,64},{224,... | collective-permute-start | bytes 3145736 | tf_op jit(solution)/shard_map/ppermute | solution.py:44
  8.6 1.4 fusion.12
  10.1 28.6 %collective-permute-done = bf16[2,64,4096]{2,1,0:T(8,128)(2,1)S(1)} collective-permute-done((bf16[2,64,4096]{2,1,0:T(8,128)(2,1)S(1)}, bf16[2,64,4096]{2,1,0:T(8,128)(2,1)S(1)}, u32[]{:S(2)}, u32[]{:S(2)}) %collective-permute-start) | collective-permute-done | bytes 1048608 | tf_op jit(solution)/shard_map/ppermute | solution.py:44
  38.8 37.0 %collective-permute-done.1 = bf16[2,32,4096]{2,1,0:T(8,128)(2,1)S(1)} collective-permute-done((bf16[2,32,4096]{2,1,0:T(8,128)(2,1)S(1)}, bf16[2,32,4096]{2,1,0:T(8,128)(2,1)S(1)}, u32[]{:S(2)}, u32[]{:S(2)}) %collective-permute-start.1) | collective-permute-done | bytes 524320 | tf_op jit(solution)/shard_map/ppermute | solution.py:45
  76.0 6.3 %collective-permute-start.2 = (bf16[2,32,4096]{2,1,0:T(8,128)(2,1)S(1)}, bf16[2,32,4096]{2,1,0:T(8,128)(2,1)S(1)}, u32[]{:S(2)}, u32[]{:S(2)}) collective-permute-start(bf16[2,32,4096]{2,1,0:T(8,128)(2,1)S(1)} %get-tuple-element.6), channel_id=1, source_target_pairs={{0,136},{8,128},{16,152},{24,144},{32,168},{40,160},{48,184},{56,1... | collective-permute-start | bytes 1572872 | tf_op jit(solution)/shard_map/ppermute | solution.py:47
  82.3 12.7 %maximum_maximum_fusion = bf16[192,8192]{1,0:T(8,128)(2,1)S(1)} fusion(bf16[96,4096]{1,0:T(8,128)(2,1)S(1)} %get-tuple-element.10, bf16[96,4096]{1,0:T(8,128)(2,1)S(1)} %get-tuple-element.9, bf16[96,4096]{1,0:T(8,128)(2,1)S(1)} %fusion.11), kind=kLoop, calls=%fused_computation.1 | loop fusion | flops 12582912 | bytes 5505024 | tf_op jit(solution)/shard_map/concatenate | solution.py:19
  95.0 1.8 %convolution_reduce-precision_fusion = f32[2,96,512]{2,1,0:T(8,128)S(1)} fusion(bf16[2,96,8192]{2,1,0:T(8,128)(2,1)S(1)} %bitcast.47, bf16[8192,512,1]{1,0,2:T(8,128)(2,1)S(1)} %bitcast.45), kind=kOutput, calls=%fused_computation.2 | convolution fusion | flops 1610711040 | bytes 11927552 | tf_op jit(solution)/shard_map/dot_general | solution.py:23
  96.8 0.2 reshape.15
  97.1 0.8 copy.9
  97.9 7.5 %all-to-all-start = ((f32[2,6,8,2,512]{4,3,1,0,2:T(2,128)}), f32[2,6,8,2,512]{4,3,1,0,2:T(2,128)S(1)}, u32[]{:S(2)}, u32[]{:S(2)}) async-start(f32[2,6,8,2,512]{4,3,1,0,2:T(2,128)} %copy.9), calls=%async_computation | async-start | bytes 786432 | tf_op jit(solution)/shard_map/all_to_all | solution.py:31
  105.5 4.9 %convolution_reduce-precision_fusion.1 = f32[2,32,512]{2,1,0:T(8,128)S(1)} fusion(bf16[2,32,8192]{2,1,0:T(8,128)(2,1)S(1)} %bitcast.46, bf16[8192,512,1]{1,0,2:T(8,128)(2,1)} %bitcast.42), kind=kOutput, calls=%fused_computation.3 | convolution fusion | flops 536903680 | bytes 9568256 | tf_op jit(solution)/shard_map/dot_general | solution.py:23
  110.5 0.7 copy.10
  111.2 1.5 %all-to-all-done = f32[2,6,8,2,512]{4,3,1,0,2:T(2,128)S(1)} async-done(((f32[2,6,8,2,512]{4,3,1,0,2:T(2,128)}), f32[2,6,8,2,512]{4,3,1,0,2:T(2,128)S(1)}, u32[]{:S(2)}, u32[]{:S(2)}) %all-to-all-start) | async-done | bytes 393248 | tf_op jit(solution)/shard_map/all_to_all | solution.py:31
  112.7 5.7 %all-to-all-start.1 = ((f32[2,2,8,2,512]{4,3,1,0,2:T(2,128)}), f32[2,2,8,2,512]{4,3,1,0,2:T(2,128)S(1)}, u32[]{:S(2)}, u32[]{:S(2)}) async-start(f32[2,2,8,2,512]{4,3,1,0,2:T(2,128)} %copy.10), calls=%async_computation.1 | async-start | bytes 262144 | tf_op jit(solution)/shard_map/all_to_all | solution.py:31
  118.5 6.2 %all-to-all-done.1 = f32[2,2,8,2,512]{4,3,1,0,2:T(2,128)S(1)} async-done(((f32[2,2,8,2,512]{4,3,1,0,2:T(2,128)}), f32[2,2,8,2,512]{4,3,1,0,2:T(2,128)S(1)}, u32[]{:S(2)}, u32[]{:S(2)}) %all-to-all-start.1) | async-done | bytes 131104 | tf_op jit(solution)/shard_map/all_to_all | solution.py:31
  124.9 0.8 gather_fusion
  125.7 0.2 select_bitcast_fusion
  125.9 15.3 %all_to_all.15 = f32[2,32,2,512]{3,2,0,1:T(2,128)S(1)} all-to-all(f32[2,32,2,512]{3,2,0,1:T(2,128)S(1)} %select_bitcast_fusion), channel_id=1, replica_groups=mesh['sa'=8,'sb'=4,'sl'=8] {'sa','sb'}, dimensions={1} | all-to-all | bytes 524288 | tf_op jit(solution)/shard_map/all_to_all | solution.py:53
  141.3 0.3 fusion.4
  141.6 0.3 fusion
  141.9 0.3 convolution_subtract_fusion
  142.3 0.3 convolution_add_fusion
  142.6 0.6 pad_maximum_fusion.1
  (26 shorter events, 0.9 us)
Async XLA Ops:
  0.0 10.1 %copy-start.1 = (s32[32]{0:T(128)S(1)}, s32[32]{0:T(128)}, u32[]{:S(2)}) copy-start(s32[32]{0:T(128)} %param.7) | copy-start | bytes 388
  1.3 37.4 %collective-permute-start = (bf16[2,64,4096]{2,1,0:T(8,128)(2,1)S(1)}, bf16[2,64,4096]{2,1,0:T(8,128)(2,1)S(1)}, u32[]{:S(2)}, u32[]{:S(2)}) collective-permute-start(bf16[2,64,4096]{2,1,0:T(8,128)(2,1)S(1)} %slice.52), channel_id=1, source_target_pairs={{0,128},{32,160},{64,192},{96,224},{128,0},{160,32},{192,64},{224,... | collective-permute-start | bytes 3145736 | tf_op jit(solution)/shard_map/ppermute | solution.py:44
  8.6 86.4 %slice-start = ((s8[8388608]{0:T(1024)(128)(4,1)}), s8[4194304]{0:T(1024)(128)(4,1)S(1)}, s32[]{:S(2)}) async-start(s8[8388608]{0:T(1024)(128)(4,1)} %bitcast.43), calls=%async_computation.3 | async-start | bytes 8388608
  10.0 65.7 %collective-permute-start.1 = (bf16[2,32,4096]{2,1,0:T(8,128)(2,1)S(1)}, bf16[2,32,4096]{2,1,0:T(8,128)(2,1)S(1)}, u32[]{:S(2)}, u32[]{:S(2)}) collective-permute-start(bf16[2,32,4096]{2,1,0:T(8,128)(2,1)S(1)} %get-tuple-element.7), channel_id=1, source_target_pairs={{0,136},{8,128},{16,152},{24,144},{32,168},{40,160},{48,184},{56,1... | collective-permute-start | bytes 1572872 | tf_op jit(solution)/shard_map/ppermute | solution.py:45
  75.8 19.2 %slice-start.1 = ((s8[8388608]{0:T(1024)(128)(4,1)}), s8[4194304]{0:T(1024)(128)(4,1)S(1)}, s32[]{:S(2)}) async-start(s8[8388608]{0:T(1024)(128)(4,1)} %bitcast.43), calls=%async_computation.4 | async-start | bytes 8388608
  76.0 29.3 %collective-permute-start.2 = (bf16[2,32,4096]{2,1,0:T(8,128)(2,1)S(1)}, bf16[2,32,4096]{2,1,0:T(8,128)(2,1)S(1)}, u32[]{:S(2)}, u32[]{:S(2)}) collective-permute-start(bf16[2,32,4096]{2,1,0:T(8,128)(2,1)S(1)} %get-tuple-element.6), channel_id=1, source_target_pairs={{0,136},{8,128},{16,152},{24,144},{32,168},{40,160},{48,184},{56,1... | collective-permute-start | bytes 1572872 | tf_op jit(solution)/shard_map/ppermute | solution.py:47
  97.9 14.8 %all-to-all-start = ((f32[2,6,8,2,512]{4,3,1,0,2:T(2,128)}), f32[2,6,8,2,512]{4,3,1,0,2:T(2,128)S(1)}, u32[]{:S(2)}, u32[]{:S(2)}) async-start(f32[2,6,8,2,512]{4,3,1,0,2:T(2,128)} %copy.9), calls=%async_computation | async-start | bytes 786432 | tf_op jit(solution)/shard_map/all_to_all | solution.py:31
  110.4 30.9 %copy-start = (bf16[2,512,512]{2,1,0:T(8,128)(2,1)S(1)}, bf16[2,512,512]{2,1,0:T(8,128)(2,1)}, u32[]{:S(2)}) copy-start(bf16[2,512,512]{2,1,0:T(8,128)(2,1)} %param.6) | copy-start | bytes 3145732
  112.7 12.1 %all-to-all-start.1 = ((f32[2,2,8,2,512]{4,3,1,0,2:T(2,128)}), f32[2,2,8,2,512]{4,3,1,0,2:T(2,128)S(1)}, u32[]{:S(2)}, u32[]{:S(2)}) async-start(f32[2,2,8,2,512]{4,3,1,0,2:T(2,128)} %copy.10), calls=%async_computation.1 | async-start | bytes 262144 | tf_op jit(solution)/shard_map/all_to_all | solution.py:31

commit v7 on v6

--- a/solution.py
+++ b/solution.py
@@ -45,10 +45,10 @@
     middle = lax.ppermute(stem[:, half:cut], ("sa", "sb"), diagonal)
     last_src, _, _ = lax.optimization_barrier((stem[:, cut:], lower, middle))
     last = lax.ppermute(last_src, ("sa", "sb"), diagonal)
-    first = jnp.concatenate([lower, middle], axis=1)
-    q_first = pair_sums(stacked_dot(first, subtree), n_sl)
-    q_last = pair_sums(stacked_dot(last, subtree), n_sl)
-    q = jnp.concatenate([q_first, q_last], axis=1)
+    partial_s = jnp.concatenate(
+        [stacked_dot(lower, subtree), stacked_dot(middle, subtree), stacked_dot(last, subtree)], axis=1
+    )
+    q = pair_sums(partial_s, n_sl)
     wanted = jnp.take(q, group_rows, axis=1)
     chosen = lax.all_to_all(wanted, ("sa", "sb"), 1, 1, tiled=True).sum(axis=1)
     gates = final_gates.astype(jnp.float32)

time: 145 us -> 151 us (1.041)
  waiting for transfers between devices: 73.3 us -> 92 us
  other arithmetic: 13.9 us -> 1.56 us
  blocking collectives: 15.3 us -> 21.6 us
  starting transfers between devices: 26.9 us -> 21.3 us
  local copies, waits for them, and re-layouts: 5.57 us -> 3.65 us
    ppermute x1, waiting for transfers between devices: 37 us -> 13.4 us  [local(): middle = lax.ppermute(stem[:, half:cut], ('sa', 'sb'), diagonal)]
    ppermute x1, waiting for transfers between devices: 0.01 us -> 21.5 us  [local(): last = lax.ppermute(last_src, ('sa', 'sb'), diagonal)]
    ppermute x1, waiting for transfers between devices: 28.6 us -> 48.9 us  [local(): lower = lax.ppermute(stem[:, :half], 'sa', straight)]
    concatenate x2 -> x3, other arithmetic: 12.7 us -> 0.34 us  [stacked_dot(): jnp.concatenate([jnp.concatenate([stem[0], -stem[1]], axis=1), jnp.concat...]
    ppermute x1, starting transfers between devices: 0.09 us -> 6.72 us  [local(): middle = lax.ppermute(stem[:, half:cut], ('sa', 'sb'), diagonal)]
    ppermute x1, starting transfers between devices: 7.28 us -> 1.03 us  [local(): lower = lax.ppermute(stem[:, :half], 'sa', straight)]
    all_to_all x1, blocking collectives: 15.3 us -> 21.6 us  [local(): chosen = lax.all_to_all(wanted, ('sa', 'sb'), 1, 1, tiled=True).sum(axis=1)]
    all_to_all x2 -> x1, starting transfers between devices: 13.2 us -> 7.46 us  [pair_sums(): return lax.all_to_all(q, 'sl', 2, 2, tiled=True).sum(axis=2)]
  transfers between devices with their start and end apart: 5 -> 4, of which waited for: 4 -> 4; matrix products, arithmetic and copies ran while one was open for 16% -> 5% of each run, Pallas kernels for 0% -> 0%
where the time goes in v7:
time: 151 us; the launch traced here: 149 us
  waiting for transfers between devices  92 us (61%)
  blocking collectives  21.6 us (14%)
  starting transfers between devices  21.3 us (14%)
  matrix products  9.15 us (6%)
  local copies, waits for them, and re-layouts  3.65 us (2%)
  other arithmetic  1.56 us (1%)
    ppermute x1, waiting for transfers between devices, local(): lower = lax.ppermute(stem[:, :half], 'sa', straight)  48.9 us
    all_to_all x1, blocking collectives, local(): chosen = lax.all_to_all(wanted, ('sa', 'sb'), 1, 1, tiled=True).sum(axis=1)  21.6 us
    ppermute x1, waiting for transfers between devices, local(): last = lax.ppermute(last_src, ('sa', 'sb'), diagonal)  21.5 us
    ppermute x1, waiting for transfers between devices, local(): middle = lax.ppermute(stem[:, half:cut], ('sa', 'sb'), diagonal)  13.4 us
    all_to_all x1, waiting for transfers between devices, pair_sums(): return lax.all_to_all(q, 'sl', 2, 2, tiled=True).sum(axis=2)  8.19 us
    dot_general x3, matrix products, stacked_dot(): out = jnp.dot(left, right, preferred_element_type=jnp.float32)  7.89 us
    all_to_all x1, starting transfers between devices, pair_sums(): return lax.all_to_all(q, 'sl', 2, 2, tiled=True).sum(axis=2)  7.46 us
    ppermute x1, starting transfers between devices, local(): middle = lax.ppermute(stem[:, half:cut], ('sa', 'sb'), diagonal)  6.72 us
  transfers between devices with their start and end apart: 4, of which 4 were waited for; matrix products, arithmetic and copies ran while one was open for 5% of the time, Pallas kernels for 0%

profile of v7, /device:TPU:2, one launch (start us, length us, event | category | flops | bytes accessed | tf_op | source)
XLA Modules:
  0.0 149.4 jit_solution(8976932393058661378)
XLA Ops:
  0.0 1.4 fusion.13
  1.4 6.7 %collective-permute-start.1 = (bf16[2,32,4096]{2,1,0:T(8,128)(2,1)S(1)}, bf16[2,32,4096]{2,1,0:T(8,128)(2,1)S(1)}, u32[]{:S(2)}, u32[]{:S(2)}) collective-permute-start(bf16[2,32,4096]{2,1,0:T(8,128)(2,1)S(1)} %get-tuple-element.7), channel_id=1, source_target_pairs={{0,136},{8,128},{16,152},{24,144},{32,168},{40,160},{48,184},{56,1... | collective-permute-start | bytes 1572872 | tf_op jit(solution)/shard_map/ppermute | solution.py:45
  8.2 1.0 collective-permute-start
  9.3 13.4 %collective-permute-done.1 = bf16[2,32,4096]{2,1,0:T(8,128)(2,1)S(1)} collective-permute-done((bf16[2,32,4096]{2,1,0:T(8,128)(2,1)S(1)}, bf16[2,32,4096]{2,1,0:T(8,128)(2,1)S(1)}, u32[]{:S(2)}, u32[]{:S(2)}) %collective-permute-start.1) | collective-permute-done | bytes 524320 | tf_op jit(solution)/shard_map/ppermute | solution.py:45
  22.9 5.1 %fusion.15 = f32[2,32,512]{2,1,0:T(8,128)S(1)} fusion(bf16[2,32,8192]{2,1,0:T(8,128)(2,1)S(1)} %bitcast.57, bf16[8192,512,1]{1,0,2:T(8,128)(2,1)} %bitcast.51), kind=kOutput, calls=%fused_computation.35 | convolution fusion | flops 536870912 | bytes 9568256 | tf_op jit(solution)/shard_map/dot_general | solution.py:23
  28.0 48.9 %collective-permute-done = bf16[2,64,4096]{2,1,0:T(8,128)(2,1)S(1)} collective-permute-done((bf16[2,64,4096]{2,1,0:T(8,128)(2,1)S(1)}, bf16[2,64,4096]{2,1,0:T(8,128)(2,1)S(1)}, u32[]{:S(2)}, u32[]{:S(2)}) %collective-permute-start) | collective-permute-done | bytes 1048608 | tf_op jit(solution)/shard_map/ppermute | solution.py:44
  76.8 6.1 %collective-permute-start.2 = (bf16[2,32,4096]{2,1,0:T(8,128)(2,1)S(1)}, bf16[2,32,4096]{2,1,0:T(8,128)(2,1)S(1)}, u32[]{:S(2)}, u32[]{:S(2)}) collective-permute-start(bf16[2,32,4096]{2,1,0:T(8,128)(2,1)S(1)} %get-tuple-element.6), channel_id=1, source_target_pairs={{0,136},{8,128},{16,152},{24,144},{32,168},{40,160},{48,184},{56,1... | collective-permute-start | bytes 1572872 | tf_op jit(solution)/shard_map/ppermute | solution.py:47
  83.0 0.2 maximum_maximum_fusion
  83.2 1.3 fusion.14
  84.5 21.5 %collective-permute-done.2 = bf16[2,32,4096]{2,1,0:T(8,128)(2,1)S(1)} collective-permute-done((bf16[2,32,4096]{2,1,0:T(8,128)(2,1)S(1)}, bf16[2,32,4096]{2,1,0:T(8,128)(2,1)S(1)}, u32[]{:S(2)}, u32[]{:S(2)}) %collective-permute-start.2) | collective-permute-done | bytes 524320 | tf_op jit(solution)/shard_map/ppermute | solution.py:47
  106.1 1.6 %fusion.16 = f32[2,32,512]{2,1,0:T(8,128)S(1)} fusion(bf16[2,32,8192]{2,1,0:T(8,128)(2,1)S(1)} %bitcast.58, bf16[8192,512,1]{1,0,2:T(8,128)(2,1)S(1)} %bitcast.55), kind=kOutput, calls=%fused_computation.36 | convolution fusion | flops 536870912 | bytes 9568256 | tf_op jit(solution)/shard_map/dot_general | solution.py:23
  107.8 0.3 reduce_precision.8
  108.1 0.8 copy.7
  108.9 7.5 %all-to-all-start = ((f32[2,8,8,2,512]{4,3,1,0,2:T(2,128)}), f32[2,8,8,2,512]{4,3,1,0,2:T(2,128)S(1)}, u32[]{:S(2)}, u32[]{:S(2)}) async-start(f32[2,8,8,2,512]{4,3,1,0,2:T(2,128)} %copy.7), calls=%async_computation | async-start | bytes 1048576 | tf_op jit(solution)/shard_map/all_to_all | solution.py:31
  116.4 8.2 %all-to-all-done = f32[2,8,8,2,512]{4,3,1,0,2:T(2,128)S(1)} async-done(((f32[2,8,8,2,512]{4,3,1,0,2:T(2,128)}), f32[2,8,8,2,512]{4,3,1,0,2:T(2,128)S(1)}, u32[]{:S(2)}, u32[]{:S(2)}) %all-to-all-start) | async-done | bytes 524320 | tf_op jit(solution)/shard_map/all_to_all | solution.py:31
  124.6 0.2 reduce_sum.18
  124.8 0.8 gather_fusion
  125.7 0.2 select_bitcast_fusion
  125.8 21.6 %all_to_all.10 = f32[2,32,2,512]{3,2,0,1:T(2,128)S(1)} all-to-all(f32[2,32,2,512]{3,2,0,1:T(2,128)S(1)} %select_bitcast_fusion), channel_id=1, replica_groups=mesh['sa'=8,'sb'=4,'sl'=8] {'sa','sb'}, dimensions={1} | all-to-all | bytes 524288 | tf_op jit(solution)/shard_map/all_to_all | solution.py:53
  147.5 0.3 fusion.4
  147.8 0.3 fusion
  148.1 0.3 convolution_subtract_fusion
  148.4 0.3 convolution_add_fusion
  148.8 0.6 pad_maximum_fusion
  (25 shorter events, 0.6 us)
Async XLA Ops:
  0.0 8.2 %copy-start.1 = (bf16[1,2,128,4096]{3,2,1,0:T(8,128)(2,1)S(1)}, bf16[1,2,128,4096]{3,2,1,0:T(8,128)(2,1)}, u32[]{:S(2)}) copy-start(bf16[1,2,128,4096]{3,2,1,0:T(8,128)(2,1)} %param.4) | copy-start | bytes 6291460
  1.4 21.3 %collective-permute-start.1 = (bf16[2,32,4096]{2,1,0:T(8,128)(2,1)S(1)}, bf16[2,32,4096]{2,1,0:T(8,128)(2,1)S(1)}, u32[]{:S(2)}, u32[]{:S(2)}) collective-permute-start(bf16[2,32,4096]{2,1,0:T(8,128)(2,1)S(1)} %get-tuple-element.7), channel_id=1, source_target_pairs={{0,136},{8,128},{16,152},{24,144},{32,168},{40,160},{48,184},{56,1... | collective-permute-start | bytes 1572872 | tf_op jit(solution)/shard_map/ppermute | solution.py:45
  8.2 68.6 %collective-permute-start = (bf16[2,64,4096]{2,1,0:T(8,128)(2,1)S(1)}, bf16[2,64,4096]{2,1,0:T(8,128)(2,1)S(1)}, u32[]{:S(2)}, u32[]{:S(2)}) collective-permute-start(bf16[2,64,4096]{2,1,0:T(8,128)(2,1)S(1)} %slice.62), channel_id=1, source_target_pairs={{0,128},{32,160},{64,192},{96,224},{128,0},{160,32},{192,64},{224,... | collective-permute-start | bytes 3145736 | tf_op jit(solution)/shard_map/ppermute | solution.py:44
  22.8 60.4 %slice-start = ((s8[8388608]{0:T(1024)(128)(4,1)}), s8[4194304]{0:T(1024)(128)(4,1)S(1)}, s32[]{:S(2)}) async-start(s8[8388608]{0:T(1024)(128)(4,1)} %bitcast.52), calls=%async_computation.2 | async-start | bytes 8388608
  22.8 60.4 %slice-start.1 = ((s8[8388608]{0:T(1024)(128)(4,1)}), s8[4194304]{0:T(1024)(128)(4,1)S(1)}, s32[]{:S(2)}) async-start(s8[8388608]{0:T(1024)(128)(4,1)} %bitcast.52), calls=%async_computation.3 | async-start | bytes 8388608
  76.8 29.2 %collective-permute-start.2 = (bf16[2,32,4096]{2,1,0:T(8,128)(2,1)S(1)}, bf16[2,32,4096]{2,1,0:T(8,128)(2,1)S(1)}, u32[]{:S(2)}, u32[]{:S(2)}) collective-permute-start(bf16[2,32,4096]{2,1,0:T(8,128)(2,1)S(1)} %get-tuple-element.6), channel_id=1, source_target_pairs={{0,136},{8,128},{16,152},{24,144},{32,168},{40,160},{48,184},{56,1... | collective-permute-start | bytes 1572872 | tf_op jit(solution)/shard_map/ppermute | solution.py:47
  107.7 8.7 %copy-start.2 = (s32[32]{0:T(128)S(1)}, s32[32]{0:T(128)}, u32[]{:S(2)}) copy-start(s32[32]{0:T(128)} %param.7) | copy-start | bytes 388
  108.1 39.4 %copy-start = (bf16[2,512,512]{2,1,0:T(8,128)(2,1)S(1)}, bf16[2,512,512]{2,1,0:T(8,128)(2,1)}, u32[]{:S(2)}) copy-start(bf16[2,512,512]{2,1,0:T(8,128)(2,1)} %param.6) | copy-start | bytes 3145732
  108.9 15.7 %all-to-all-start = ((f32[2,8,8,2,512]{4,3,1,0,2:T(2,128)}), f32[2,8,8,2,512]{4,3,1,0,2:T(2,128)S(1)}, u32[]{:S(2)}, u32[]{:S(2)}) async-start(f32[2,8,8,2,512]{4,3,1,0,2:T(2,128)} %copy.7), calls=%async_computation | async-start | bytes 1048576 | tf_op jit(solution)/shard_map/all_to_all | solution.py:31

commit v8 on v6

--- a/solution.py
+++ b/solution.py
@@ -45,8 +45,8 @@
     middle = lax.ppermute(stem[:, half:cut], ("sa", "sb"), diagonal)
     last_src, _, _ = lax.optimization_barrier((stem[:, cut:], lower, middle))
     last = lax.ppermute(last_src, ("sa", "sb"), diagonal)
-    first = jnp.concatenate([lower, middle], axis=1)
-    q_first = pair_sums(stacked_dot(first, subtree), n_sl)
+    first = jnp.concatenate([stacked_dot(lower, subtree), stacked_dot(middle, subtree)], axis=1)
+    q_first = pair_sums(first, n_sl)
     q_last = pair_sums(stacked_dot(last, subtree), n_sl)
     q = jnp.concatenate([q_first, q_last], axis=1)
     wanted = jnp.take(q, group_rows, axis=1)

time: 145 us -> 151 us (1.041)
  other arithmetic: 13.9 us -> 1.55 us
  waiting for transfers between devices: 73.3 us -> 81.5 us
  blocking collectives: 15.3 us -> 20.1 us
  matrix products: 7.99 us -> 12.5 us
  starting transfers between devices: 26.9 us -> 28.8 us
    ppermute x1, waiting for transfers between devices: 37 us -> 13.4 us  [local(): middle = lax.ppermute(stem[:, half:cut], ('sa', 'sb'), diagonal)]
    ppermute x1, waiting for transfers between devices: 28.6 us -> 48.9 us  [local(): lower = lax.ppermute(stem[:, :half], 'sa', straight)]
    ppermute x1, waiting for transfers between devices: 0.01 us -> 13 us  [local(): last = lax.ppermute(last_src, ('sa', 'sb'), diagonal)]
    concatenate x2 -> x3, other arithmetic: 12.7 us -> 0.33 us  [stacked_dot(): jnp.concatenate([jnp.concatenate([stem[0], -stem[1]], axis=1), jnp.concat...]
    ppermute x1, starting transfers between devices: 0.09 us -> 6.72 us  [local(): middle = lax.ppermute(stem[:, half:cut], ('sa', 'sb'), diagonal)]
    ppermute x1, starting transfers between devices: 7.28 us -> 1.04 us  [local(): lower = lax.ppermute(stem[:, :half], 'sa', straight)]
    all_to_all x1, blocking collectives: 15.3 us -> 20.1 us  [local(): chosen = lax.all_to_all(wanted, ('sa', 'sb'), 1, 1, tiled=True).sum(axis=1)]
    dot_general x2 -> x3, matrix products: 6.73 us -> 11.3 us  [stacked_dot(): out = jnp.dot(left, right, preferred_element_type=jnp.float32)]
  transfers between devices with their start and end apart: 5 -> 5, of which waited for: 4 -> 4; matrix products, arithmetic and copies ran while one was open for 16% -> 9% of each run, Pallas kernels for 0% -> 0%
where the time goes in v8:
time: 151 us; the launch traced here: 149 us
  waiting for transfers between devices  81.5 us (54%)
  starting transfers between devices  28.8 us (19%)
  blocking collectives  20.1 us (13%)
  matrix products  12.5 us (8%)
  local copies, waits for them, and re-layouts  4.21 us (3%)
  other arithmetic  1.55 us (1%)
    ppermute x1, waiting for transfers between devices, local(): lower = lax.ppermute(stem[:, :half], 'sa', straight)  48.9 us
    all_to_all x1, blocking collectives, local(): chosen = lax.all_to_all(wanted, ('sa', 'sb'), 1, 1, tiled=True).sum(axis=1)  20.1 us
    all_to_all x2, starting transfers between devices, pair_sums(): return lax.all_to_all(q, 'sl', 2, 2, tiled=True).sum(axis=2)  14.9 us
    ppermute x1, waiting for transfers between devices, local(): middle = lax.ppermute(stem[:, half:cut], ('sa', 'sb'), diagonal)  13.4 us
    ppermute x1, waiting for transfers between devices, local(): last = lax.ppermute(last_src, ('sa', 'sb'), diagonal)  13 us
    dot_general x3, matrix products, stacked_dot(): out = jnp.dot(left, right, preferred_element_type=jnp.float32)  11.3 us
    ppermute x1, starting transfers between devices, local(): middle = lax.ppermute(stem[:, half:cut], ('sa', 'sb'), diagonal)  6.72 us
    all_to_all x2, waiting for transfers between devices, pair_sums(): return lax.all_to_all(q, 'sl', 2, 2, tiled=True).sum(axis=2)  6.24 us
  transfers between devices with their start and end apart: 5, of which 4 were waited for; matrix products, arithmetic and copies ran while one was open for 9% of the time, Pallas kernels for 0%

profile of v8, /device:TPU:2, one launch (start us, length us, event | category | flops | bytes accessed | tf_op | source)
XLA Modules:
  0.0 148.9 jit_solution(15095593855607709451)
XLA Ops:
  0.0 1.4 fusion.13
  1.4 6.7 %collective-permute-start.1 = (bf16[2,32,4096]{2,1,0:T(8,128)(2,1)S(1)}, bf16[2,32,4096]{2,1,0:T(8,128)(2,1)S(1)}, u32[]{:S(2)}, u32[]{:S(2)}) collective-permute-start(bf16[2,32,4096]{2,1,0:T(8,128)(2,1)S(1)} %get-tuple-element.7), channel_id=1, source_target_pairs={{0,136},{8,128},{16,152},{24,144},{32,168},{40,160},{48,184},{56,1... | collective-permute-start | bytes 1572872 | tf_op jit(solution)/shard_map/ppermute | solution.py:45
  8.2 1.0 collective-permute-start
  9.3 13.4 %collective-permute-done.1 = bf16[2,32,4096]{2,1,0:T(8,128)(2,1)S(1)} collective-permute-done((bf16[2,32,4096]{2,1,0:T(8,128)(2,1)S(1)}, bf16[2,32,4096]{2,1,0:T(8,128)(2,1)S(1)}, u32[]{:S(2)}, u32[]{:S(2)}) %collective-permute-start.1) | collective-permute-done | bytes 524320 | tf_op jit(solution)/shard_map/ppermute | solution.py:45
  22.9 5.1 %fusion.15 = f32[2,32,512]{2,1,0:T(8,128)S(1)} fusion(bf16[2,32,8192]{2,1,0:T(8,128)(2,1)S(1)} %bitcast.57, bf16[8192,512,1]{1,0,2:T(8,128)(2,1)} %bitcast.51), kind=kOutput, calls=%fused_computation.37 | convolution fusion | flops 536870912 | bytes 9568256 | tf_op jit(solution)/shard_map/dot_general | solution.py:23
  27.9 48.9 %collective-permute-done = bf16[2,64,4096]{2,1,0:T(8,128)(2,1)S(1)} collective-permute-done((bf16[2,64,4096]{2,1,0:T(8,128)(2,1)S(1)}, bf16[2,64,4096]{2,1,0:T(8,128)(2,1)S(1)}, u32[]{:S(2)}, u32[]{:S(2)}) %collective-permute-start) | collective-permute-done | bytes 1048608 | tf_op jit(solution)/shard_map/ppermute | solution.py:44
  76.8 6.1 %collective-permute-start.2 = (bf16[2,32,4096]{2,1,0:T(8,128)(2,1)S(1)}, bf16[2,32,4096]{2,1,0:T(8,128)(2,1)S(1)}, u32[]{:S(2)}, u32[]{:S(2)}) collective-permute-start(bf16[2,32,4096]{2,1,0:T(8,128)(2,1)S(1)} %get-tuple-element.6), channel_id=1, source_target_pairs={{0,136},{8,128},{16,152},{24,144},{32,168},{40,160},{48,184},{56,1... | collective-permute-start | bytes 1572872 | tf_op jit(solution)/shard_map/ppermute | solution.py:47
  83.0 0.2 maximum_maximum_fusion
  83.2 1.3 fusion.14
  84.5 0.2 reduce_precision.11
  84.8 0.8 copy.9
  85.5 7.5 %all-to-all-start = ((f32[2,6,8,2,512]{4,3,1,0,2:T(2,128)}), f32[2,6,8,2,512]{4,3,1,0,2:T(2,128)S(1)}, u32[]{:S(2)}, u32[]{:S(2)}) async-start(f32[2,6,8,2,512]{4,3,1,0,2:T(2,128)} %copy.9), calls=%async_computation | async-start | bytes 786432 | tf_op jit(solution)/shard_map/all_to_all | solution.py:31
  93.0 13.0 %collective-permute-done.2 = bf16[2,32,4096]{2,1,0:T(8,128)(2,1)S(1)} collective-permute-done((bf16[2,32,4096]{2,1,0:T(8,128)(2,1)S(1)}, bf16[2,32,4096]{2,1,0:T(8,128)(2,1)S(1)}, u32[]{:S(2)}, u32[]{:S(2)}) %collective-permute-start.2) | collective-permute-done | bytes 524320 | tf_op jit(solution)/shard_map/ppermute | solution.py:47
  106.1 4.9 %convolution_reduce-precision_fusion = f32[2,32,512]{2,1,0:T(8,128)S(1)} fusion(bf16[2,32,8192]{2,1,0:T(8,128)(2,1)S(1)} %bitcast.58, bf16[8192,512,1]{1,0,2:T(8,128)(2,1)} %bitcast.52), kind=kOutput, calls=%fused_computation.2 | convolution fusion | flops 536903680 | bytes 9568256 | tf_op jit(solution)/shard_map/dot_general | solution.py:23
  111.2 0.7 copy.10
  111.8 7.5 %all-to-all-start.1 = ((f32[2,2,8,2,512]{4,3,1,0,2:T(2,128)}), f32[2,2,8,2,512]{4,3,1,0,2:T(2,128)S(1)}, u32[]{:S(2)}, u32[]{:S(2)}) async-start(f32[2,2,8,2,512]{4,3,1,0,2:T(2,128)} %copy.10), calls=%async_computation.1 | async-start | bytes 262144 | tf_op jit(solution)/shard_map/all_to_all | solution.py:31
  119.5 6.2 %all-to-all-done.1 = f32[2,2,8,2,512]{4,3,1,0,2:T(2,128)S(1)} async-done(((f32[2,2,8,2,512]{4,3,1,0,2:T(2,128)}), f32[2,2,8,2,512]{4,3,1,0,2:T(2,128)S(1)}, u32[]{:S(2)}, u32[]{:S(2)}) %all-to-all-start.1) | async-done | bytes 131104 | tf_op jit(solution)/shard_map/all_to_all | solution.py:31
  125.8 0.8 gather_fusion
  126.8 20.1 %all_to_all.15 = f32[2,32,2,512]{3,2,0,1:T(2,128)S(1)} all-to-all(f32[2,32,2,512]{3,2,0,1:T(2,128)S(1)} %select_bitcast_fusion), channel_id=1, replica_groups=mesh['sa'=8,'sb'=4,'sl'=8] {'sa','sb'}, dimensions={1} | all-to-all | bytes 524288 | tf_op jit(solution)/shard_map/all_to_all | solution.py:53
  147.1 0.3 fusion.4
  147.4 0.3 fusion
  147.7 0.3 convolution_subtract_fusion
  148.0 0.3 convolution_add_fusion
  148.3 0.6 pad_maximum_fusion.1
  (31 shorter events, 1.1 us)
Async XLA Ops:
  0.0 8.1 %copy-start.1 = (bf16[1,2,128,4096]{3,2,1,0:T(8,128)(2,1)S(1)}, bf16[1,2,128,4096]{3,2,1,0:T(8,128)(2,1)}, u32[]{:S(2)}) copy-start(bf16[1,2,128,4096]{3,2,1,0:T(8,128)(2,1)} %param.4) | copy-start | bytes 6291460
  0.0 9.3 %copy-start.2 = (s32[32]{0:T(128)S(1)}, s32[32]{0:T(128)}, u32[]{:S(2)}) copy-start(s32[32]{0:T(128)} %param.7) | copy-start | bytes 388
  1.4 21.3 %collective-permute-start.1 = (bf16[2,32,4096]{2,1,0:T(8,128)(2,1)S(1)}, bf16[2,32,4096]{2,1,0:T(8,128)(2,1)S(1)}, u32[]{:S(2)}, u32[]{:S(2)}) collective-permute-start(bf16[2,32,4096]{2,1,0:T(8,128)(2,1)S(1)} %get-tuple-element.7), channel_id=1, source_target_pairs={{0,136},{8,128},{16,152},{24,144},{32,168},{40,160},{48,184},{56,1... | collective-permute-start | bytes 1572872 | tf_op jit(solution)/shard_map/ppermute | solution.py:45
  8.2 68.6 %collective-permute-start = (bf16[2,64,4096]{2,1,0:T(8,128)(2,1)S(1)}, bf16[2,64,4096]{2,1,0:T(8,128)(2,1)S(1)}, u32[]{:S(2)}, u32[]{:S(2)}) collective-permute-start(bf16[2,64,4096]{2,1,0:T(8,128)(2,1)S(1)} %slice.62), channel_id=1, source_target_pairs={{0,128},{32,160},{64,192},{96,224},{128,0},{160,32},{192,64},{224,... | collective-permute-start | bytes 3145736 | tf_op jit(solution)/shard_map/ppermute | solution.py:44
  22.7 60.4 %slice-start = ((s8[8388608]{0:T(1024)(128)(4,1)}), s8[4194304]{0:T(1024)(128)(4,1)S(1)}, s32[]{:S(2)}) async-start(s8[8388608]{0:T(1024)(128)(4,1)} %bitcast.53), calls=%async_computation.3 | async-start | bytes 8388608
  22.8 60.4 %slice-start.1 = ((s8[8388608]{0:T(1024)(128)(4,1)}), s8[4194304]{0:T(1024)(128)(4,1)S(1)}, s32[]{:S(2)}) async-start(s8[8388608]{0:T(1024)(128)(4,1)} %bitcast.53), calls=%async_computation.4 | async-start | bytes 8388608
  76.8 29.2 %collective-permute-start.2 = (bf16[2,32,4096]{2,1,0:T(8,128)(2,1)S(1)}, bf16[2,32,4096]{2,1,0:T(8,128)(2,1)S(1)}, u32[]{:S(2)}, u32[]{:S(2)}) collective-permute-start(bf16[2,32,4096]{2,1,0:T(8,128)(2,1)S(1)} %get-tuple-element.6), channel_id=1, source_target_pairs={{0,136},{8,128},{16,152},{24,144},{32,168},{40,160},{48,184},{56,1... | collective-permute-start | bytes 1572872 | tf_op jit(solution)/shard_map/ppermute | solution.py:47
  85.5 26.3 %all-to-all-start = ((f32[2,6,8,2,512]{4,3,1,0,2:T(2,128)}), f32[2,6,8,2,512]{4,3,1,0,2:T(2,128)S(1)}, u32[]{:S(2)}, u32[]{:S(2)}) async-start(f32[2,6,8,2,512]{4,3,1,0,2:T(2,128)} %copy.9), calls=%async_computation | async-start | bytes 786432 | tf_op jit(solution)/shard_map/all_to_all | solution.py:31
  111.1 36.0 %copy-start = (bf16[2,512,512]{2,1,0:T(8,128)(2,1)S(1)}, bf16[2,512,512]{2,1,0:T(8,128)(2,1)}, u32[]{:S(2)}) copy-start(bf16[2,512,512]{2,1,0:T(8,128)(2,1)} %param.6) | copy-start | bytes 3145732
  111.8 13.9 %all-to-all-start.1 = ((f32[2,2,8,2,512]{4,3,1,0,2:T(2,128)}), f32[2,2,8,2,512]{4,3,1,0,2:T(2,128)S(1)}, u32[]{:S(2)}, u32[]{:S(2)}) async-start(f32[2,2,8,2,512]{4,3,1,0,2:T(2,128)} %copy.10), calls=%async_computation.1 | async-start | bytes 262144 | tf_op jit(solution)/shard_map/all_to_all | solution.py:31

commit v9 on v8

--- a/solution.py
+++ b/solution.py
@@ -40,13 +40,14 @@
     flip = n_sa // 2
     straight = [(i, i ^ flip) for i in range(n_sa)]
     diagonal = [(a * n_sb + b, (a ^ flip) * n_sb + (b ^ 1)) for a in range(n_sa) for b in range(n_sb)]
-    cut = rows - rows // 4
+    cut = rows - RB
     lower = lax.ppermute(stem[:, :half], "sa", straight)
     middle = lax.ppermute(stem[:, half:cut], ("sa", "sb"), diagonal)
     last_src, _, _ = lax.optimization_barrier((stem[:, cut:], lower, middle))
     last = lax.ppermute(last_src, ("sa", "sb"), diagonal)
     first = jnp.concatenate([stacked_dot(lower, subtree), stacked_dot(middle, subtree)], axis=1)
     q_first = pair_sums(first, n_sl)
+    last, q_first = lax.optimization_barrier((last, q_first))
     q_last = pair_sums(stacked_dot(last, subtree), n_sl)
     q = jnp.concatenate([q_first, q_last], axis=1)
     wanted = jnp.take(q, group_rows, axis=1)

time: 151 us -> 153 us (1.013)
  waiting for transfers between devices: 81.5 us -> 90.4 us
  matrix products: 12.5 us -> 8.96 us
  starting transfers between devices: 28.8 us -> 26.3 us
  blocking collectives: 20.1 us -> 17.8 us
  local copies, waits for them, and re-layouts: 4.21 us -> 6.34 us
    ppermute x1, waiting for transfers between devices: 13 us -> 0.01 us  [local(): last = lax.ppermute(last_src, ('sa', 'sb'), diagonal)]
    all_to_all x2, waiting for transfers between devices: 6.24 us -> 15.4 us  [pair_sums(): return lax.all_to_all(q, 'sl', 2, 2, tiled=True).sum(axis=2)]
    ppermute x1, waiting for transfers between devices: 48.9 us -> 55.5 us  [local(): lower = lax.ppermute(stem[:, :half], 'sa', straight)]
    ppermute x1, waiting for transfers between devices: 13.4 us -> 19.5 us  [local(): middle = lax.ppermute(stem[:, half:cut], ('sa', 'sb'), diagonal)]
    dot_general x3, matrix products: 11.3 us -> 7.7 us  [stacked_dot(): out = jnp.dot(left, right, preferred_element_type=jnp.float32)]
    all_to_all x1, blocking collectives: 20.1 us -> 17.8 us  [local(): chosen = lax.all_to_all(wanted, ('sa', 'sb'), 1, 1, tiled=True).sum(axis=1)]
    all_to_all x2, starting transfers between devices: 14.9 us -> 12.6 us  [pair_sums(): return lax.all_to_all(q, 'sl', 2, 2, tiled=True).sum(axis=2)]
  transfers between devices with their start and end apart: 5 -> 5, of which waited for: 4 -> 4; matrix products, arithmetic and copies ran while one was open for 9% -> 4% of each run, Pallas kernels for 0% -> 0%
where the time goes in v9:
time: 153 us; the launch traced here: 152 us
  waiting for transfers between devices  90.4 us (59%)
  starting transfers between devices  26.3 us (17%)
  blocking collectives  17.8 us (12%)
  matrix products  8.96 us (6%)
  local copies, waits for them, and re-layouts  6.34 us (4%)
  other arithmetic  1.57 us (1%)
    ppermute x1, waiting for transfers between devices, local(): lower = lax.ppermute(stem[:, :half], 'sa', straight)  55.5 us
    ppermute x1, waiting for transfers between devices, local(): middle = lax.ppermute(stem[:, half:cut], ('sa', 'sb'), diagonal)  19.5 us
    all_to_all x1, blocking collectives, local(): chosen = lax.all_to_all(wanted, ('sa', 'sb'), 1, 1, tiled=True).sum(axis=1)  17.8 us
    all_to_all x2, waiting for transfers between devices, pair_sums(): return lax.all_to_all(q, 'sl', 2, 2, tiled=True).sum(axis=2)  15.4 us
    all_to_all x2, starting transfers between devices, pair_sums(): return lax.all_to_all(q, 'sl', 2, 2, tiled=True).sum(axis=2)  12.6 us
    dot_general x3, matrix products, stacked_dot(): out = jnp.dot(left, right, preferred_element_type=jnp.float32)  7.7 us
    ppermute x1, starting transfers between devices, local(): middle = lax.ppermute(stem[:, half:cut], ('sa', 'sb'), diagonal)  6.72 us
    ppermute x1, starting transfers between devices, local(): last = lax.ppermute(last_src, ('sa', 'sb'), diagonal)  6.08 us
  transfers between devices with their start and end apart: 5, of which 4 were waited for; matrix products, arithmetic and copies ran while one was open for 4% of the time, Pallas kernels for 0%

profile of v9, /device:TPU:2, one launch (start us, length us, event | category | flops | bytes accessed | tf_op | source)
XLA Modules:
  0.0 151.6 jit_solution(8399494789937065103)
XLA Ops:
  0.0 1.3 slice.64
  1.3 6.7 %collective-permute-start.1 = (bf16[2,48,4096]{2,1,0:T(8,128)(2,1)S(1)}, bf16[2,48,4096]{2,1,0:T(8,128)(2,1)S(1)}, u32[]{:S(2)}, u32[]{:S(2)}) collective-permute-start(bf16[2,48,4096]{2,1,0:T(8,128)(2,1)S(1)} %slice.64), channel_id=1, source_target_pairs={{0,136},{8,128},{16,152},{24,144},{32,168},{40,160},{48,184},{56,1... | collective-permute-start | bytes 2359304 | tf_op jit(solution)/shard_map/ppermute | solution.py:45
  8.1 1.3 slice.63
  9.4 1.0 collective-permute-start
  10.3 1.0 slice.62
  11.3 19.5 %collective-permute-done.1 = bf16[2,48,4096]{2,1,0:T(8,128)(2,1)S(1)} collective-permute-done((bf16[2,48,4096]{2,1,0:T(8,128)(2,1)S(1)}, bf16[2,48,4096]{2,1,0:T(8,128)(2,1)S(1)}, u32[]{:S(2)}, u32[]{:S(2)}) %collective-permute-start.1) | collective-permute-done | bytes 786464 | tf_op jit(solution)/shard_map/ppermute | solution.py:45
  31.0 1.5 fusion.14
  32.5 55.5 %collective-permute-done = bf16[2,64,4096]{2,1,0:T(8,128)(2,1)S(1)} collective-permute-done((bf16[2,64,4096]{2,1,0:T(8,128)(2,1)S(1)}, bf16[2,64,4096]{2,1,0:T(8,128)(2,1)S(1)}, u32[]{:S(2)}, u32[]{:S(2)}) %collective-permute-start) | collective-permute-done | bytes 1048608 | tf_op jit(solution)/shard_map/ppermute | solution.py:44
  88.0 6.1 %collective-permute-start.2 = (bf16[2,16,4096]{2,1,0:T(8,128)(2,1)S(1)}, bf16[2,16,4096]{2,1,0:T(8,128)(2,1)S(1)}, u32[]{:S(2)}, u32[]{:S(2)}) collective-permute-start(bf16[2,16,4096]{2,1,0:T(8,128)(2,1)S(1)} %slice.62), channel_id=1, source_target_pairs={{0,136},{8,128},{16,152},{24,144},{32,168},{40,160},{48,184},{56,1... | collective-permute-start | bytes 786440 | tf_op jit(solution)/shard_map/ppermute | solution.py:47
  94.4 1.3 fusion.13
  96.0 0.8 copy.9
  96.8 7.5 %all-to-all-start = ((f32[2,7,8,2,512]{4,3,1,0,2:T(2,128)}), f32[2,7,8,2,512]{4,3,1,0,2:T(2,128)S(1)}, u32[]{:S(2)}, u32[]{:S(2)}) async-start(f32[2,7,8,2,512]{4,3,1,0,2:T(2,128)} %copy.9), calls=%async_computation | async-start | bytes 917504 | tf_op jit(solution)/shard_map/all_to_all | solution.py:31
  104.3 9.1 %all-to-all-done = f32[2,7,8,2,512]{4,3,1,0,2:T(2,128)S(1)} async-done(((f32[2,7,8,2,512]{4,3,1,0,2:T(2,128)}), f32[2,7,8,2,512]{4,3,1,0,2:T(2,128)S(1)}, u32[]{:S(2)}, u32[]{:S(2)}) %all-to-all-start) | async-done | bytes 458784 | tf_op jit(solution)/shard_map/all_to_all | solution.py:31
  113.6 5.0 %convolution_reduce-precision_fusion = f32[2,16,512]{2,1,0:T(8,128)S(1)} fusion(bf16[2,16,8192]{2,1,0:T(8,128)(2,1)S(1)} %bitcast.57, bf16[8192,512,1]{1,0,2:T(8,128)(2,1)} %bitcast.52), kind=kOutput, calls=%fused_computation.3 | convolution fusion | flops 268451840 | bytes 8978432 | tf_op jit(solution)/shard_map/dot_general | solution.py:23
  118.7 0.6 copy.10
  119.3 5.1 %all-to-all-start.1 = ((f32[2,1,8,2,512]{4,3,0,1,2:T(2,128)}), f32[2,1,8,2,512]{4,3,0,1,2:T(2,128)S(1)}, u32[]{:S(2)}, u32[]{:S(2)}) async-start(f32[2,1,8,2,512]{4,3,0,1,2:T(2,128)} %copy.10), calls=%async_computation.1 | async-start | bytes 131072 | tf_op jit(solution)/shard_map/all_to_all | solution.py:31
  124.4 6.3 %all-to-all-done.1 = f32[2,1,8,2,512]{4,3,0,1,2:T(2,128)S(1)} async-done(((f32[2,1,8,2,512]{4,3,0,1,2:T(2,128)}), f32[2,1,8,2,512]{4,3,0,1,2:T(2,128)S(1)}, u32[]{:S(2)}, u32[]{:S(2)}) %all-to-all-start.1) | async-done | bytes 65568 | tf_op jit(solution)/shard_map/all_to_all | solution.py:31
  130.8 0.8 gather_fusion
  131.8 17.8 %all_to_all.15 = f32[2,32,2,512]{3,2,0,1:T(2,128)S(1)} all-to-all(f32[2,32,2,512]{3,2,0,1:T(2,128)S(1)} %select_bitcast_fusion), channel_id=1, replica_groups=mesh['sa'=8,'sb'=4,'sl'=8] {'sa','sb'}, dimensions={1} | all-to-all | bytes 524288 | tf_op jit(solution)/shard_map/all_to_all | solution.py:54
  149.7 0.3 fusion
  150.0 0.3 fusion.4
  150.4 0.3 convolution_add_fusion
  150.7 0.3 convolution_subtract_fusion
  151.0 0.6 pad_maximum_fusion.1
  (27 shorter events, 1.4 us)
Async XLA Ops:
  0.0 31.0 %copy-start = (bf16[1,2,4096,512]{3,2,1,0:T(8,128)(2,1)S(1)}, bf16[1,2,4096,512]{3,2,1,0:T(8,128)(2,1)}, u32[]{:S(2)}) copy-start(bf16[1,2,4096,512]{3,2,1,0:T(8,128)(2,1)} %param.5) | copy-start | bytes 25165828
  1.3 29.4 %collective-permute-start.1 = (bf16[2,48,4096]{2,1,0:T(8,128)(2,1)S(1)}, bf16[2,48,4096]{2,1,0:T(8,128)(2,1)S(1)}, u32[]{:S(2)}, u32[]{:S(2)}) collective-permute-start(bf16[2,48,4096]{2,1,0:T(8,128)(2,1)S(1)} %slice.64), channel_id=1, source_target_pairs={{0,136},{8,128},{16,152},{24,144},{32,168},{40,160},{48,184},{56,1... | collective-permute-start | bytes 2359304 | tf_op jit(solution)/shard_map/ppermute | solution.py:45
  9.4 78.6 %collective-permute-start = (bf16[2,64,4096]{2,1,0:T(8,128)(2,1)S(1)}, bf16[2,64,4096]{2,1,0:T(8,128)(2,1)S(1)}, u32[]{:S(2)}, u32[]{:S(2)}) collective-permute-start(bf16[2,64,4096]{2,1,0:T(8,128)(2,1)S(1)} %slice.63), channel_id=1, source_target_pairs={{0,128},{32,160},{64,192},{96,224},{128,0},{160,32},{192,64},{224,... | collective-permute-start | bytes 3145736 | tf_op jit(solution)/shard_map/ppermute | solution.py:44
  88.0 25.5 %collective-permute-start.2 = (bf16[2,16,4096]{2,1,0:T(8,128)(2,1)S(1)}, bf16[2,16,4096]{2,1,0:T(8,128)(2,1)S(1)}, u32[]{:S(2)}, u32[]{:S(2)}) collective-permute-start(bf16[2,16,4096]{2,1,0:T(8,128)(2,1)S(1)} %slice.62), channel_id=1, source_target_pairs={{0,136},{8,128},{16,152},{24,144},{32,168},{40,160},{48,184},{56,1... | collective-permute-start | bytes 786440 | tf_op jit(solution)/shard_map/ppermute | solution.py:47
  95.6 8.6 %copy-start.2 = (s32[32]{0:T(128)S(1)}, s32[32]{0:T(128)}, u32[]{:S(2)}) copy-start(s32[32]{0:T(128)} %param.7) | copy-start | bytes 388
  96.8 16.6 %all-to-all-start = ((f32[2,7,8,2,512]{4,3,1,0,2:T(2,128)}), f32[2,7,8,2,512]{4,3,1,0,2:T(2,128)S(1)}, u32[]{:S(2)}, u32[]{:S(2)}) async-start(f32[2,7,8,2,512]{4,3,1,0,2:T(2,128)} %copy.9), calls=%async_computation | async-start | bytes 917504 | tf_op jit(solution)/shard_map/all_to_all | solution.py:31
  113.6 36.1 %copy-start.1 = (bf16[2,512,512]{2,1,0:T(8,128)(2,1)S(1)}, bf16[2,512,512]{2,1,0:T(8,128)(2,1)}, u32[]{:S(2)}) copy-start(bf16[2,512,512]{2,1,0:T(8,128)(2,1)} %param.6) | copy-start | bytes 3145732
  119.3 11.4 %all-to-all-start.1 = ((f32[2,1,8,2,512]{4,3,0,1,2:T(2,128)}), f32[2,1,8,2,512]{4,3,0,1,2:T(2,128)S(1)}, u32[]{:S(2)}, u32[]{:S(2)}) async-start(f32[2,1,8,2,512]{4,3,0,1,2:T(2,128)} %copy.10), calls=%async_computation.1 | async-start | bytes 131072 | tf_op jit(solution)/shard_map/all_to_all | solution.py:31

commit v10 on v8

--- a/solution.py
+++ b/solution.py
@@ -43,12 +43,13 @@
     cut = rows - rows // 4
     lower = lax.ppermute(stem[:, :half], "sa", straight)
     middle = lax.ppermute(stem[:, half:cut], ("sa", "sb"), diagonal)
-    last_src, _, _ = lax.optimization_barrier((stem[:, cut:], lower, middle))
-    last = lax.ppermute(last_src, ("sa", "sb"), diagonal)
-    first = jnp.concatenate([stacked_dot(lower, subtree), stacked_dot(middle, subtree)], axis=1)
-    q_first = pair_sums(first, n_sl)
-    q_last = pair_sums(stacked_dot(last, subtree), n_sl)
-    q = jnp.concatenate([q_first, q_last], axis=1)
+    end_src, _ = lax.optimization_barrier((stem[:, cut:], middle))
+    end = lax.ppermute(end_src, ("sa", "sb"), diagonal)
+    q_middle = pair_sums(stacked_dot(middle, subtree), n_sl)
+    lower, end, q_middle = lax.optimization_barrier((lower, end, q_middle))
+    q_rest = pair_sums(jnp.concatenate([stacked_dot(lower, subtree), stacked_dot(end, subtree)], axis=1), n_sl)
+    blocks_lower = half // RB
+    q = jnp.concatenate([q_rest[:, :blocks_lower], q_middle, q_rest[:, blocks_lower:]], axis=1)
     wanted = jnp.take(q, group_rows, axis=1)
     chosen = lax.all_to_all(wanted, ("sa", "sb"), 1, 1, tiled=True).sum(axis=1)
     gates = final_gates.astype(jnp.float32)

time: 151 us -> 149 us (0.987)
  blocking collectives: 20.1 us -> 34 us
  waiting for transfers between devices: 81.5 us -> 73.4 us
  starting transfers between devices: 28.8 us -> 21.3 us
    ppermute x1, waiting for transfers between devices: 48.9 us -> 7.1 us  [local(): lower = lax.ppermute(stem[:, :half], 'sa', straight)]
    ppermute x1, waiting for transfers between devices: 13 us -> 44.6 us  [local(): end = lax.ppermute(end_src, ('sa', 'sb'), diagonal)]
    all_to_all x0 -> x1, blocking collectives: none -> 13.7 us  [pair_sums(): return lax.all_to_all(q, 'sl', 2, 2, tiled=True).sum(axis=2)]
    all_to_all x2 -> x1, starting transfers between devices: 14.9 us -> 7.46 us  [pair_sums(): return lax.all_to_all(q, 'sl', 2, 2, tiled=True).sum(axis=2)]
    all_to_all x2 -> x1, waiting for transfers between devices: 6.24 us -> 8.25 us  [pair_sums(): return lax.all_to_all(q, 'sl', 2, 2, tiled=True).sum(axis=2)]
  transfers between devices with their start and end apart: 5 -> 4, of which waited for: 4 -> 4; matrix products, arithmetic and copies ran while one was open for 9% -> 4% of each run, Pallas kernels for 0% -> 0%
where the time goes in v10:
time: 149 us; the launch traced here: 147 us
  waiting for transfers between devices  73.4 us (49%)
  blocking collectives  34 us (23%)
  starting transfers between devices  21.3 us (14%)
  matrix products  12.5 us (8%)
  local copies, waits for them, and re-layouts  4.14 us (3%)
  other arithmetic  1.56 us (1%)
    ppermute x1, waiting for transfers between devices, local(): end = lax.ppermute(end_src, ('sa', 'sb'), diagonal)  44.6 us
    all_to_all x1, blocking collectives, local(): chosen = lax.all_to_all(wanted, ('sa', 'sb'), 1, 1, tiled=True).sum(axis=1)  20.3 us
    all_to_all x1, blocking collectives, pair_sums(): return lax.all_to_all(q, 'sl', 2, 2, tiled=True).sum(axis=2)  13.7 us
    ppermute x1, waiting for transfers between devices, local(): middle = lax.ppermute(stem[:, half:cut], ('sa', 'sb'), diagonal)  13.4 us
    dot_general x3, matrix products, stacked_dot(): out = jnp.dot(left, right, preferred_element_type=jnp.float32)  11.3 us
    all_to_all x1, waiting for transfers between devices, pair_sums(): return lax.all_to_all(q, 'sl', 2, 2, tiled=True).sum(axis=2)  8.25 us
    all_to_all x1, starting transfers between devices, pair_sums(): return lax.all_to_all(q, 'sl', 2, 2, tiled=True).sum(axis=2)  7.46 us
    ppermute x1, waiting for transfers between devices, local(): lower = lax.ppermute(stem[:, :half], 'sa', straight)  7.1 us
  transfers between devices with their start and end apart: 4, of which 4 were waited for; matrix products, arithmetic and copies ran while one was open for 4% of the time, Pallas kernels for 0%

profile of v10, /device:TPU:2, one launch (start us, length us, event | category | flops | bytes accessed | tf_op | source)
XLA Modules:
  0.0 147.2 jit_solution(13957736258632857883)
XLA Ops:
  0.0 1.4 fusion.13
  1.4 6.7 %collective-permute-start.1 = (bf16[2,32,4096]{2,1,0:T(8,128)(2,1)S(1)}, bf16[2,32,4096]{2,1,0:T(8,128)(2,1)S(1)}, u32[]{:S(2)}, u32[]{:S(2)}) collective-permute-start(bf16[2,32,4096]{2,1,0:T(8,128)(2,1)S(1)} %get-tuple-element.13), channel_id=1, source_target_pairs={{0,136},{8,128},{16,152},{24,144},{32,168},{40,160},{48,184},{56,1... | collective-permute-start | bytes 1572872 | tf_op jit(solution)/shard_map/ppermute | solution.py:45
  8.2 1.0 collective-permute-start
  9.3 13.4 %collective-permute-done.1 = bf16[2,32,4096]{2,1,0:T(8,128)(2,1)S(1)} collective-permute-done((bf16[2,32,4096]{2,1,0:T(8,128)(2,1)S(1)}, bf16[2,32,4096]{2,1,0:T(8,128)(2,1)S(1)}, u32[]{:S(2)}, u32[]{:S(2)}) %collective-permute-start.1) | collective-permute-done | bytes 524320 | tf_op jit(solution)/shard_map/ppermute | solution.py:45
  22.7 6.1 %collective-permute-start.2 = (bf16[2,32,4096]{2,1,0:T(8,128)(2,1)S(1)}, bf16[2,32,4096]{2,1,0:T(8,128)(2,1)S(1)}, u32[]{:S(2)}, u32[]{:S(2)}) collective-permute-start(bf16[2,32,4096]{2,1,0:T(8,128)(2,1)S(1)} %get-tuple-element.9), channel_id=1, source_target_pairs={{0,136},{8,128},{16,152},{24,144},{32,168},{40,160},{48,184},{56,1... | collective-permute-start | bytes 1572872 | tf_op jit(solution)/shard_map/ppermute | solution.py:47
  28.9 4.9 %convolution_reduce-precision_fusion = f32[2,32,512]{2,1,0:T(8,128)S(1)} fusion(bf16[2,32,8192]{2,1,0:T(8,128)(2,1)S(1)} %bitcast.57, bf16[8192,512,1]{1,0,2:T(8,128)(2,1)} %bitcast.51), kind=kOutput, calls=%fused_computation.2 | convolution fusion | flops 536903680 | bytes 9568256 | tf_op jit(solution)/shard_map/dot_general | solution.py:23
  34.0 13.7 %all_to_all.15 = f32[2,2,8,2,512]{4,3,1,0,2:T(2,128)S(1)} all-to-all(f32[2,2,8,2,512]{4,3,1,0,2:T(2,128)S(1)} %copy.9), channel_id=1, replica_groups=mesh['sa'=8,'sb'=4,'sl'=8] {'sl'}, dimensions={2} | all-to-all | bytes 262144 | tf_op jit(solution)/shard_map/all_to_all | solution.py:31
  47.7 7.1 %collective-permute-done = bf16[2,64,4096]{2,1,0:T(8,128)(2,1)S(1)} collective-permute-done((bf16[2,64,4096]{2,1,0:T(8,128)(2,1)S(1)}, bf16[2,64,4096]{2,1,0:T(8,128)(2,1)S(1)}, u32[]{:S(2)}, u32[]{:S(2)}) %collective-permute-start) | collective-permute-done | bytes 1048608 | tf_op jit(solution)/shard_map/ppermute | solution.py:44
  54.8 44.6 %collective-permute-done.2 = bf16[2,32,4096]{2,1,0:T(8,128)(2,1)S(1)} collective-permute-done((bf16[2,32,4096]{2,1,0:T(8,128)(2,1)S(1)}, bf16[2,32,4096]{2,1,0:T(8,128)(2,1)S(1)}, u32[]{:S(2)}, u32[]{:S(2)}) %collective-permute-start.2) | collective-permute-done | bytes 524320 | tf_op jit(solution)/shard_map/ppermute | solution.py:47
  99.7 5.1 %fusion.15 = f32[2,32,512]{2,1,0:T(8,128)S(1)} fusion(bf16[2,32,8192]{2,1,0:T(8,128)(2,1)S(1)} %bitcast.58, bf16[8192,512,1]{1,0,2:T(8,128)(2,1)} %bitcast.52), kind=kOutput, calls=%fused_computation.37 | convolution fusion | flops 536870912 | bytes 9568256 | tf_op jit(solution)/shard_map/dot_general | solution.py:23
  104.8 0.2 maximum_maximum_fusion
  105.0 0.5 slice-done.1
  105.5 1.3 fusion.14
  106.8 0.2 reduce_precision.12
  107.1 0.8 copy.10
  107.9 7.5 %all-to-all-start.1 = ((f32[2,6,8,2,512]{4,3,1,0,2:T(2,128)}), f32[2,6,8,2,512]{4,3,1,0,2:T(2,128)S(1)}, u32[]{:S(2)}, u32[]{:S(2)}) async-start(f32[2,6,8,2,512]{4,3,1,0,2:T(2,128)} %copy.10), calls=%async_computation.1 | async-start | bytes 786432 | tf_op jit(solution)/shard_map/all_to_all | solution.py:31
  115.4 8.3 %all-to-all-done.1 = f32[2,6,8,2,512]{4,3,1,0,2:T(2,128)S(1)} async-done(((f32[2,6,8,2,512]{4,3,1,0,2:T(2,128)}), f32[2,6,8,2,512]{4,3,1,0,2:T(2,128)S(1)}, u32[]{:S(2)}, u32[]{:S(2)}) %all-to-all-start.1) | async-done | bytes 393248 | tf_op jit(solution)/shard_map/all_to_all | solution.py:31
  123.8 0.8 gather_fusion
  124.8 20.3 %all_to_all.16 = f32[2,32,2,512]{3,2,0,1:T(2,128)S(1)} all-to-all(f32[2,32,2,512]{3,2,0,1:T(2,128)S(1)} %select_bitcast_fusion), channel_id=1, replica_groups=mesh['sa'=8,'sb'=4,'sl'=8] {'sa','sb'}, dimensions={1} | all-to-all | bytes 524288 | tf_op jit(solution)/shard_map/all_to_all | solution.py:54
  145.3 0.3 fusion
  145.6 0.3 fusion.4
  145.9 0.3 convolution_add_fusion
  146.2 0.3 convolution_subtract_fusion
  146.5 0.6 pad_maximum_fusion.1
  (32 shorter events, 1.1 us)
Async XLA Ops:
  0.0 8.1 %copy-start.1 = (bf16[1,2,128,4096]{3,2,1,0:T(8,128)(2,1)S(1)}, bf16[1,2,128,4096]{3,2,1,0:T(8,128)(2,1)}, u32[]{:S(2)}) copy-start(bf16[1,2,128,4096]{3,2,1,0:T(8,128)(2,1)} %param.4) | copy-start | bytes 6291460
  1.4 21.3 %collective-permute-start.1 = (bf16[2,32,4096]{2,1,0:T(8,128)(2,1)S(1)}, bf16[2,32,4096]{2,1,0:T(8,128)(2,1)S(1)}, u32[]{:S(2)}, u32[]{:S(2)}) collective-permute-start(bf16[2,32,4096]{2,1,0:T(8,128)(2,1)S(1)} %get-tuple-element.13), channel_id=1, source_target_pairs={{0,136},{8,128},{16,152},{24,144},{32,168},{40,160},{48,184},{56,1... | collective-permute-start | bytes 1572872 | tf_op jit(solution)/shard_map/ppermute | solution.py:45
  8.2 46.5 %collective-permute-start = (bf16[2,64,4096]{2,1,0:T(8,128)(2,1)S(1)}, bf16[2,64,4096]{2,1,0:T(8,128)(2,1)S(1)}, u32[]{:S(2)}, u32[]{:S(2)}) collective-permute-start(bf16[2,64,4096]{2,1,0:T(8,128)(2,1)S(1)} %slice.70), channel_id=1, source_target_pairs={{0,128},{32,160},{64,192},{96,224},{128,0},{160,32},{192,64},{224,... | collective-permute-start | bytes 3145736 | tf_op jit(solution)/shard_map/ppermute | solution.py:44
  22.7 76.7 %collective-permute-start.2 = (bf16[2,32,4096]{2,1,0:T(8,128)(2,1)S(1)}, bf16[2,32,4096]{2,1,0:T(8,128)(2,1)S(1)}, u32[]{:S(2)}, u32[]{:S(2)}) collective-permute-start(bf16[2,32,4096]{2,1,0:T(8,128)(2,1)S(1)} %get-tuple-element.9), channel_id=1, source_target_pairs={{0,136},{8,128},{16,152},{24,144},{32,168},{40,160},{48,184},{56,1... | collective-permute-start | bytes 1572872 | tf_op jit(solution)/shard_map/ppermute | solution.py:47
  99.7 5.3 %slice-start = ((s8[8388608]{0:T(1024)(128)(4,1)}), s8[4194304]{0:T(1024)(128)(4,1)S(1)}, s32[]{:S(2)}) async-start(s8[8388608]{0:T(1024)(128)(4,1)} %bitcast.53), calls=%async_computation.3 | async-start | bytes 8388608
  99.7 5.8 %slice-start.1 = ((s8[8388608]{0:T(1024)(128)(4,1)}), s8[4194304]{0:T(1024)(128)(4,1)S(1)}, s32[]{:S(2)}) async-start(s8[8388608]{0:T(1024)(128)(4,1)} %bitcast.53), calls=%async_computation.4 | async-start | bytes 8388608
  106.8 8.5 %copy-start.2 = (s32[32]{0:T(128)S(1)}, s32[32]{0:T(128)}, u32[]{:S(2)}) copy-start(s32[32]{0:T(128)} %param.7) | copy-start | bytes 388
  107.1 38.2 %copy-start = (bf16[2,512,512]{2,1,0:T(8,128)(2,1)S(1)}, bf16[2,512,512]{2,1,0:T(8,128)(2,1)}, u32[]{:S(2)}) copy-start(bf16[2,512,512]{2,1,0:T(8,128)(2,1)} %param.6) | copy-start | bytes 3145732
  107.9 15.8 %all-to-all-start.1 = ((f32[2,6,8,2,512]{4,3,1,0,2:T(2,128)}), f32[2,6,8,2,512]{4,3,1,0,2:T(2,128)S(1)}, u32[]{:S(2)}, u32[]{:S(2)}) async-start(f32[2,6,8,2,512]{4,3,1,0,2:T(2,128)} %copy.10), calls=%async_computation.1 | async-start | bytes 786432 | tf_op jit(solution)/shard_map/all_to_all | solution.py:31

commit v11 on v10

--- a/solution.py
+++ b/solution.py
@@ -46,10 +46,10 @@
     end_src, _ = lax.optimization_barrier((stem[:, cut:], middle))
     end = lax.ppermute(end_src, ("sa", "sb"), diagonal)
     q_middle = pair_sums(stacked_dot(middle, subtree), n_sl)
-    lower, end, q_middle = lax.optimization_barrier((lower, end, q_middle))
-    q_rest = pair_sums(jnp.concatenate([stacked_dot(lower, subtree), stacked_dot(end, subtree)], axis=1), n_sl)
-    blocks_lower = half // RB
-    q = jnp.concatenate([q_rest[:, :blocks_lower], q_middle, q_rest[:, blocks_lower:]], axis=1)
+    q_lower = pair_sums(stacked_dot(lower, subtree), n_sl)
+    end, q_lower = lax.optimization_barrier((end, q_lower))
+    q_end = pair_sums(stacked_dot(end, subtree), n_sl)
+    q = jnp.concatenate([q_lower, q_middle, q_end], axis=1)
     wanted = jnp.take(q, group_rows, axis=1)
     chosen = lax.all_to_all(wanted, ("sa", "sb"), 1, 1, tiled=True).sum(axis=1)
     gates = final_gates.astype(jnp.float32)

time: 149 us -> 153 us (1.027)
  starting transfers between devices: 21.3 us -> 34.9 us
  waiting for transfers between devices: 73.4 us -> 68.3 us
  blocking collectives: 34 us -> 29.5 us
    ppermute x1, waiting for transfers between devices: 44.6 us -> 21.7 us  [local(): end = lax.ppermute(end_src, ('sa', 'sb'), diagonal)]
    ppermute x1, waiting for transfers between devices: 7.1 us -> 25.8 us  [local(): lower = lax.ppermute(stem[:, :half], 'sa', straight)]
    all_to_all x1 -> x0, blocking collectives: 13.7 us -> none  [pair_sums(): return lax.all_to_all(q, 'sl', 2, 2, tiled=True).sum(axis=2)]
    all_to_all x1 -> x3, starting transfers between devices: 7.46 us -> 21.1 us  [pair_sums(): return lax.all_to_all(q, 'sl', 2, 2, tiled=True).sum(axis=2)]
    all_to_all x1, blocking collectives: 20.3 us -> 29.5 us  [local(): chosen = lax.all_to_all(wanted, ('sa', 'sb'), 1, 1, tiled=True).sum(axis=1)]
    reshape x2 -> x6, local copies, waits for them, and re-layouts: 0.08 us -> 2.33 us  [pair_sums(): q = q.reshape(2, blocks, n_sl, RB // n_sl, partial_s.shape[2])]
    all_to_all x1 -> x3, waiting for transfers between devices: 8.25 us -> 7.37 us  [pair_sums(): return lax.all_to_all(q, 'sl', 2, 2, tiled=True).sum(axis=2)]
  transfers between devices with their start and end apart: 4 -> 6, of which waited for: 4 -> 5; matrix products, arithmetic and copies ran while one was open for 4% -> 9% of each run, Pallas kernels for 0% -> 0%
where the time goes in v11:
time: 153 us; the launch traced here: 152 us
  waiting for transfers between devices  68.3 us (45%)
  starting transfers between devices  34.9 us (23%)
  blocking collectives  29.5 us (19%)
  matrix products  12.4 us (8%)
  local copies, waits for them, and re-layouts  4.82 us (3%)
  other arithmetic  1.53 us (1%)
    all_to_all x1, blocking collectives, local(): chosen = lax.all_to_all(wanted, ('sa', 'sb'), 1, 1, tiled=True).sum(axis=1)  29.5 us
    ppermute x1, waiting for transfers between devices, local(): lower = lax.ppermute(stem[:, :half], 'sa', straight)  25.8 us
    ppermute x1, waiting for transfers between devices, local(): end = lax.ppermute(end_src, ('sa', 'sb'), diagonal)  21.7 us
    all_to_all x3, starting transfers between devices, pair_sums(): return lax.all_to_all(q, 'sl', 2, 2, tiled=True).sum(axis=2)  21.1 us
    ppermute x1, waiting for transfers between devices, local(): middle = lax.ppermute(stem[:, half:cut], ('sa', 'sb'), diagonal)  13.4 us
    dot_general x3, matrix products, stacked_dot(): out = jnp.dot(left, right, preferred_element_type=jnp.float32)  11.1 us
    all_to_all x3, waiting for transfers between devices, pair_sums(): return lax.all_to_all(q, 'sl', 2, 2, tiled=True).sum(axis=2)  7.37 us
    ppermute x1, starting transfers between devices, local(): middle = lax.ppermute(stem[:, half:cut], ('sa', 'sb'), diagonal)  6.72 us
  transfers between devices with their start and end apart: 6, of which 5 were waited for; matrix products, arithmetic and copies ran while one was open for 9% of the time, Pallas kernels for 0%

profile of v11, /device:TPU:2, one launch (start us, length us, event | category | flops | bytes accessed | tf_op | source)
XLA Modules:
  0.0 151.7 jit_solution(9428043932349721257)
XLA Ops:
  0.0 1.4 fusion.13
  1.4 6.7 %collective-permute-start = (bf16[2,32,4096]{2,1,0:T(8,128)(2,1)S(1)}, bf16[2,32,4096]{2,1,0:T(8,128)(2,1)S(1)}, u32[]{:S(2)}, u32[]{:S(2)}) collective-permute-start(bf16[2,32,4096]{2,1,0:T(8,128)(2,1)S(1)} %get-tuple-element.11), channel_id=1, source_target_pairs={{0,136},{8,128},{16,152},{24,144},{32,168},{40,160},{48,184},{56,1... | collective-permute-start | bytes 1572872 | tf_op jit(solution)/shard_map/ppermute | solution.py:45
  8.2 1.0 collective-permute-start.2
  9.3 13.4 %collective-permute-done = bf16[2,32,4096]{2,1,0:T(8,128)(2,1)S(1)} collective-permute-done((bf16[2,32,4096]{2,1,0:T(8,128)(2,1)S(1)}, bf16[2,32,4096]{2,1,0:T(8,128)(2,1)S(1)}, u32[]{:S(2)}, u32[]{:S(2)}) %collective-permute-start) | collective-permute-done | bytes 524320 | tf_op jit(solution)/shard_map/ppermute | solution.py:45
  22.7 6.1 %collective-permute-start.1 = (bf16[2,32,4096]{2,1,0:T(8,128)(2,1)S(1)}, bf16[2,32,4096]{2,1,0:T(8,128)(2,1)S(1)}, u32[]{:S(2)}, u32[]{:S(2)}) collective-permute-start(bf16[2,32,4096]{2,1,0:T(8,128)(2,1)S(1)} %get-tuple-element.8), channel_id=1, source_target_pairs={{0,136},{8,128},{16,152},{24,144},{32,168},{40,160},{48,184},{56,1... | collective-permute-start | bytes 1572872 | tf_op jit(solution)/shard_map/ppermute | solution.py:47
  28.9 25.8 %collective-permute-done.2 = bf16[2,64,4096]{2,1,0:T(8,128)(2,1)S(1)} collective-permute-done((bf16[2,64,4096]{2,1,0:T(8,128)(2,1)S(1)}, bf16[2,64,4096]{2,1,0:T(8,128)(2,1)S(1)}, u32[]{:S(2)}, u32[]{:S(2)}) %collective-permute-start.2) | collective-permute-done | bytes 1048608 | tf_op jit(solution)/shard_map/ppermute | solution.py:44
  55.1 1.3 convolution_reduce-precision_fusion
  56.5 0.7 copy.11
  57.2 7.5 %all-to-all-start = ((f32[2,4,8,2,512]{4,3,1,0,2:T(2,128)}), f32[2,4,8,2,512]{4,3,1,0,2:T(2,128)S(1)}, u32[]{:S(2)}, u32[]{:S(2)}) async-start(f32[2,4,8,2,512]{4,3,1,0,2:T(2,128)} %copy.11), calls=%async_computation | async-start | bytes 524288 | tf_op jit(solution)/shard_map/all_to_all | solution.py:31
  64.7 4.9 %convolution_reduce-precision_fusion.2 = f32[2,32,512]{2,1,0:T(8,128)S(1)} fusion(bf16[2,32,8192]{2,1,0:T(8,128)(2,1)S(1)} %bitcast.55, bf16[8192,512,1]{1,0,2:T(8,128)(2,1)} %bitcast.51), kind=kOutput, calls=%fused_computation.4 | convolution fusion | flops 536903680 | bytes 9568256 | tf_op jit(solution)/shard_map/dot_general | solution.py:23
  69.7 0.7 copy.12
  70.4 1.0 all-to-all-done
  71.4 6.2 %all-to-all-start.1 = ((f32[2,2,8,2,512]{4,3,1,0,2:T(2,128)}), f32[2,2,8,2,512]{4,3,1,0,2:T(2,128)S(1)}, u32[]{:S(2)}, u32[]{:S(2)}) async-start(f32[2,2,8,2,512]{4,3,1,0,2:T(2,128)} %copy.12), calls=%async_computation.1 | async-start | bytes 262144 | tf_op jit(solution)/shard_map/all_to_all | solution.py:31
  77.7 21.7 %collective-permute-done.1 = bf16[2,32,4096]{2,1,0:T(8,128)(2,1)S(1)} collective-permute-done((bf16[2,32,4096]{2,1,0:T(8,128)(2,1)S(1)}, bf16[2,32,4096]{2,1,0:T(8,128)(2,1)S(1)}, u32[]{:S(2)}, u32[]{:S(2)}) %collective-permute-start.1) | collective-permute-done | bytes 524320 | tf_op jit(solution)/shard_map/ppermute | solution.py:47
  99.5 4.9 %convolution_reduce-precision_fusion.1 = f32[2,32,512]{2,1,0:T(8,128)S(1)} fusion(bf16[2,32,8192]{2,1,0:T(8,128)(2,1)S(1)} %bitcast.56, bf16[8192,512,1]{1,0,2:T(8,128)(2,1)} %bitcast.52), kind=kOutput, calls=%fused_computation.3 | convolution fusion | flops 536903680 | bytes 9568256 | tf_op jit(solution)/shard_map/dot_general | solution.py:23
  104.6 0.7 copy.13
  105.2 7.5 %all-to-all-start.2 = ((f32[2,2,8,2,512]{4,3,1,0,2:T(2,128)}), f32[2,2,8,2,512]{4,3,1,0,2:T(2,128)S(1)}, u32[]{:S(2)}, u32[]{:S(2)}) async-start(f32[2,2,8,2,512]{4,3,1,0,2:T(2,128)} %copy.13), calls=%async_computation.2 | async-start | bytes 262144 | tf_op jit(solution)/shard_map/all_to_all | solution.py:31
  112.8 6.3 %all-to-all-done.2 = f32[2,2,8,2,512]{4,3,1,0,2:T(2,128)S(1)} async-done(((f32[2,2,8,2,512]{4,3,1,0,2:T(2,128)}), f32[2,2,8,2,512]{4,3,1,0,2:T(2,128)S(1)}, u32[]{:S(2)}, u32[]{:S(2)}) %all-to-all-start.2) | async-done | bytes 131104 | tf_op jit(solution)/shard_map/all_to_all | solution.py:31
  119.2 0.8 gather_fusion
  120.2 29.5 %all_to_all.20 = f32[2,32,2,512]{3,2,0,1:T(2,128)S(1)} all-to-all(f32[2,32,2,512]{3,2,0,1:T(2,128)S(1)} %select_bitcast_fusion), channel_id=1, replica_groups=mesh['sa'=8,'sb'=4,'sl'=8] {'sa','sb'}, dimensions={1} | all-to-all | bytes 524288 | tf_op jit(solution)/shard_map/all_to_all | solution.py:54
  150.2 0.3 fusion
  150.5 0.3 convolution_subtract_fusion
  150.8 0.3 convolution_add_fusion
  151.1 0.6 pad_maximum_fusion.1
  (32 shorter events, 1.7 us)
Async XLA Ops:
  0.0 8.1 %copy-start.2 = (bf16[1,2,128,4096]{3,2,1,0:T(8,128)(2,1)S(1)}, bf16[1,2,128,4096]{3,2,1,0:T(8,128)(2,1)}, u32[]{:S(2)}) copy-start(bf16[1,2,128,4096]{3,2,1,0:T(8,128)(2,1)} %param.4) | copy-start | bytes 6291460
  0.0 9.3 %copy-start.3 = (s32[32]{0:T(128)S(1)}, s32[32]{0:T(128)}, u32[]{:S(2)}) copy-start(s32[32]{0:T(128)} %param.7) | copy-start | bytes 388
  1.4 21.3 %collective-permute-start = (bf16[2,32,4096]{2,1,0:T(8,128)(2,1)S(1)}, bf16[2,32,4096]{2,1,0:T(8,128)(2,1)S(1)}, u32[]{:S(2)}, u32[]{:S(2)}) collective-permute-start(bf16[2,32,4096]{2,1,0:T(8,128)(2,1)S(1)} %get-tuple-element.11), channel_id=1, source_target_pairs={{0,136},{8,128},{16,152},{24,144},{32,168},{40,160},{48,184},{56,1... | collective-permute-start | bytes 1572872 | tf_op jit(solution)/shard_map/ppermute | solution.py:45
  8.2 46.5 %collective-permute-start.2 = (bf16[2,64,4096]{2,1,0:T(8,128)(2,1)S(1)}, bf16[2,64,4096]{2,1,0:T(8,128)(2,1)S(1)}, u32[]{:S(2)}, u32[]{:S(2)}) collective-permute-start(bf16[2,64,4096]{2,1,0:T(8,128)(2,1)S(1)} %slice.64), channel_id=1, source_target_pairs={{0,128},{32,160},{64,192},{96,224},{128,0},{160,32},{192,64},{224,... | collective-permute-start | bytes 3145736 | tf_op jit(solution)/shard_map/ppermute | solution.py:44
  22.7 76.7 %collective-permute-start.1 = (bf16[2,32,4096]{2,1,0:T(8,128)(2,1)S(1)}, bf16[2,32,4096]{2,1,0:T(8,128)(2,1)S(1)}, u32[]{:S(2)}, u32[]{:S(2)}) collective-permute-start(bf16[2,32,4096]{2,1,0:T(8,128)(2,1)S(1)} %get-tuple-element.8), channel_id=1, source_target_pairs={{0,136},{8,128},{16,152},{24,144},{32,168},{40,160},{48,184},{56,1... | collective-permute-start | bytes 1572872 | tf_op jit(solution)/shard_map/ppermute | solution.py:47
  28.8 26.2 %copy-start = (bf16[1,2,4096,512]{3,2,1,0:T(8,128)(2,1)S(1)}, bf16[1,2,4096,512]{3,2,1,0:T(8,128)(2,1)}, u32[]{:S(2)}) copy-start(bf16[1,2,4096,512]{3,2,1,0:T(8,128)(2,1)} %param.5) | copy-start | bytes 25165828
  57.2 14.2 %all-to-all-start = ((f32[2,4,8,2,512]{4,3,1,0,2:T(2,128)}), f32[2,4,8,2,512]{4,3,1,0,2:T(2,128)S(1)}, u32[]{:S(2)}, u32[]{:S(2)}) async-start(f32[2,4,8,2,512]{4,3,1,0,2:T(2,128)} %copy.11), calls=%async_computation | async-start | bytes 524288 | tf_op jit(solution)/shard_map/all_to_all | solution.py:31
  71.4 33.8 %all-to-all-start.1 = ((f32[2,2,8,2,512]{4,3,1,0,2:T(2,128)}), f32[2,2,8,2,512]{4,3,1,0,2:T(2,128)S(1)}, u32[]{:S(2)}, u32[]{:S(2)}) async-start(f32[2,2,8,2,512]{4,3,1,0,2:T(2,128)} %copy.12), calls=%async_computation.1 | async-start | bytes 262144 | tf_op jit(solution)/shard_map/all_to_all | solution.py:31
  104.5 45.4 %copy-start.1 = (bf16[2,512,512]{2,1,0:T(8,128)(2,1)S(1)}, bf16[2,512,512]{2,1,0:T(8,128)(2,1)}, u32[]{:S(2)}) copy-start(bf16[2,512,512]{2,1,0:T(8,128)(2,1)} %param.6) | copy-start | bytes 3145732
  105.2 13.9 %all-to-all-start.2 = ((f32[2,2,8,2,512]{4,3,1,0,2:T(2,128)}), f32[2,2,8,2,512]{4,3,1,0,2:T(2,128)S(1)}, u32[]{:S(2)}, u32[]{:S(2)}) async-start(f32[2,2,8,2,512]{4,3,1,0,2:T(2,128)} %copy.13), calls=%async_computation.2 | async-start | bytes 262144 | tf_op jit(solution)/shard_map/all_to_all | solution.py:31

commit v12 on v6

--- a/solution.py
+++ b/solution.py
@@ -2,6 +2,7 @@
 import jax.numpy as jnp
 from jax import lax
 from jax.sharding import PartitionSpec as P
+from jax.experimental import pallas as pl
 
 RB = 16
 ALL = ("sa", "sb", "sl")
@@ -14,13 +15,39 @@
     return (real, imag)
 
 
-def stacked_dot(stem, subtree):
+def _acc_kernel(left_ref, right_ref, out_ref):
+    @pl.when(pl.program_id(0) == 0)
+    def _():
+        out_ref[...] = jnp.zeros_like(out_ref)
+
+    out_ref[...] += jnp.dot(left_ref[...], right_ref[...], preferred_element_type=jnp.float32)
+
+
+def streamed_dot(left, right, block_k=1024):
+    m, k = left.shape
+    n = right.shape[1]
+    return pl.pallas_call(
+        _acc_kernel,
+        grid=(k // block_k,),
+        in_specs=[
+            pl.BlockSpec((m, block_k), lambda i: (0, i)),
+            pl.BlockSpec((block_k, n), lambda i: (i, 0)),
+        ],
+        out_specs=pl.BlockSpec((m, n), lambda i: (0, 0)),
+        out_shape=jax.ShapeDtypeStruct((m, n), jnp.float32),
+    )(left, right)
+
+
+def stacked_dot(stem, subtree, dot=None):
     rows = stem.shape[1]
     left = jnp.concatenate(
         [jnp.concatenate([stem[0], -stem[1]], axis=1), jnp.concatenate([stem[1], stem[0]], axis=1)], axis=0
     )
     right = subtree.reshape(-1, subtree.shape[-1])
-    out = jnp.dot(left, right, preferred_element_type=jnp.float32)
+    if dot is None:
+        out = jnp.dot(left, right, preferred_element_type=jnp.float32)
+    else:
+        out = dot(left, right)
     return out.reshape(2, rows, out.shape[-1])
 
 
@@ -47,7 +74,7 @@
     last = lax.ppermute(last_src, ("sa", "sb"), diagonal)
     first = jnp.concatenate([lower, middle], axis=1)
     q_first = pair_sums(stacked_dot(first, subtree), n_sl)
-    q_last = pair_sums(stacked_dot(last, subtree), n_sl)
+    q_last = pair_sums(stacked_dot(last, subtree, streamed_dot), n_sl)
     q = jnp.concatenate([q_first, q_last], axis=1)
     wanted = jnp.take(q, group_rows, axis=1)
     chosen = lax.all_to_all(wanted, ("sa", "sb"), 1, 1, tiled=True).sum(axis=1)

time: 145 us -> 150 us (1.034)
  Pallas kernels: 0 us -> 7.57 us
  matrix products: 7.99 us -> 3.05 us
  other arithmetic: 13.9 us -> 15.9 us
  starting transfers between devices: 26.9 us -> 28.4 us
  waiting for transfers between devices: 73.3 us -> 71.8 us
    pallas_call x0 -> x1, Pallas kernels: none -> 7.57 us  [streamed_dot(): pl.pallas_call(_acc_kernel, grid=(k // block_k,), in_specs=[pl.BlockSpec(...]
    dot_general x2 -> x1, matrix products: 6.73 us -> 1.79 us  [stacked_dot(): out = jnp.dot(left, right, preferred_element_type=jnp.float32)]
  transfers between devices with their start and end apart: 5 -> 5, of which waited for: 4 -> 3; matrix products, arithmetic and copies ran while one was open for 16% -> 14% of each run, Pallas kernels for 0% -> 5%
where the time goes in v12:
time: 150 us; the launch traced here: 148 us
  waiting for transfers between devices  71.8 us (48%)
  starting transfers between devices  28.4 us (19%)
  other arithmetic  15.9 us (11%)
  blocking collectives  15.3 us (10%)
  Pallas kernels  7.57 us (5%)
  local copies, waits for them, and re-layouts  5.6 us (4%)
  matrix products  3.05 us (2%)
    ppermute x1, waiting for transfers between devices, local(): middle = lax.ppermute(stem[:, half:cut], ('sa', 'sb'), diagonal)  37 us
    ppermute x1, waiting for transfers between devices, local(): lower = lax.ppermute(stem[:, :half], 'sa', straight)  28.6 us
    all_to_all x1, blocking collectives, local(): chosen = lax.all_to_all(wanted, ('sa', 'sb'), 1, 1, tiled=True).sum(axis=1)  15.3 us
    all_to_all x2, starting transfers between devices, pair_sums(): return lax.all_to_all(q, 'sl', 2, 2, tiled=True).sum(axis=2)  14.7 us
    concatenate x2, other arithmetic, stacked_dot(): jnp.concatenate([jnp.concatenate([stem[0], -stem[1]], axis=1), jnp.concat...  13.7 us
    pallas_call x1, Pallas kernels, streamed_dot(): pl.pallas_call(_acc_kernel, grid=(k // block_k,), in_specs=[pl.BlockSpec(...  7.57 us
    ppermute x1, starting transfers between devices, local(): lower = lax.ppermute(stem[:, :half], 'sa', straight)  7.28 us
    ppermute x1, starting transfers between devices, local(): last = lax.ppermute(last_src, ('sa', 'sb'), diagonal)  6.34 us
  transfers between devices with their start and end apart: 5, of which 3 were waited for; matrix products, arithmetic and copies ran while one was open for 14% of the time, Pallas kernels for 5%

profile of v12, /device:TPU:2, one launch (start us, length us, event | category | flops | bytes accessed | tf_op | source)
XLA Modules:
  0.0 147.8 jit_solution(14924482221303332601)
XLA Ops:
  0.0 1.3 slice.52
  1.3 7.3 %collective-permute-start = (bf16[2,64,4096]{2,1,0:T(8,128)(2,1)S(1)}, bf16[2,64,4096]{2,1,0:T(8,128)(2,1)S(1)}, u32[]{:S(2)}, u32[]{:S(2)}) collective-permute-start(bf16[2,64,4096]{2,1,0:T(8,128)(2,1)S(1)} %slice.52), channel_id=1, source_target_pairs={{0,128},{32,160},{64,192},{96,224},{128,0},{160,32},{192,64},{224,... | collective-permute-start | bytes 3145736 | tf_op jit(solution)/shard_map/ppermute | solution.py:71
  8.6 1.4 fusion.12
  10.1 28.6 %collective-permute-done = bf16[2,64,4096]{2,1,0:T(8,128)(2,1)S(1)} collective-permute-done((bf16[2,64,4096]{2,1,0:T(8,128)(2,1)S(1)}, bf16[2,64,4096]{2,1,0:T(8,128)(2,1)S(1)}, u32[]{:S(2)}, u32[]{:S(2)}) %collective-permute-start) | collective-permute-done | bytes 1048608 | tf_op jit(solution)/shard_map/ppermute | solution.py:71
  38.8 37.0 %collective-permute-done.1 = bf16[2,32,4096]{2,1,0:T(8,128)(2,1)S(1)} collective-permute-done((bf16[2,32,4096]{2,1,0:T(8,128)(2,1)S(1)}, bf16[2,32,4096]{2,1,0:T(8,128)(2,1)S(1)}, u32[]{:S(2)}, u32[]{:S(2)}) %collective-permute-start.1) | collective-permute-done | bytes 524320 | tf_op jit(solution)/shard_map/ppermute | solution.py:72
  76.0 6.3 %collective-permute-start.2 = (bf16[2,32,4096]{2,1,0:T(8,128)(2,1)S(1)}, bf16[2,32,4096]{2,1,0:T(8,128)(2,1)S(1)}, u32[]{:S(2)}, u32[]{:S(2)}) collective-permute-start(bf16[2,32,4096]{2,1,0:T(8,128)(2,1)S(1)} %get-tuple-element.6), channel_id=1, source_target_pairs={{0,136},{8,128},{16,152},{24,144},{32,168},{40,160},{48,184},{56,1... | collective-permute-start | bytes 1572872 | tf_op jit(solution)/shard_map/ppermute | solution.py:74
  82.3 12.7 %maximum_maximum_fusion = bf16[192,8192]{1,0:T(8,128)(2,1)S(1)} fusion(bf16[96,4096]{1,0:T(8,128)(2,1)S(1)} %get-tuple-element.10, bf16[96,4096]{1,0:T(8,128)(2,1)S(1)} %get-tuple-element.9, bf16[96,4096]{1,0:T(8,128)(2,1)S(1)} %fusion.11), kind=kLoop, calls=%fused_computation.1 | loop fusion | flops 12582912 | bytes 5505024 | tf_op jit(solution)/shard_map/concatenate | solution.py:43
  95.0 1.8 %convolution_reduce-precision_fusion = f32[2,96,512]{2,1,0:T(8,128)S(1)} fusion(bf16[2,96,8192]{2,1,0:T(8,128)(2,1)S(1)} %bitcast.43, bf16[8192,512,1]{1,0,2:T(8,128)(2,1)S(1)} %bitcast.42), kind=kOutput, calls=%fused_computation.2 | convolution fusion | flops 1610711040 | bytes 11927552 | tf_op jit(solution)/shard_map/dot_general | solution.py:48
  96.8 0.2 reshape.14
  97.1 0.8 copy.9
  97.9 7.5 %all-to-all-start = ((f32[2,6,8,2,512]{4,3,1,0,2:T(2,128)}), f32[2,6,8,2,512]{4,3,1,0,2:T(2,128)S(1)}, u32[]{:S(2)}, u32[]{:S(2)}) async-start(f32[2,6,8,2,512]{4,3,1,0,2:T(2,128)} %copy.9), calls=%async_computation | async-start | bytes 786432 | tf_op jit(solution)/shard_map/all_to_all | solution.py:58
  105.4 1.0 maximum_maximum_fusion.1.left_ref
  106.5 7.6 %shard_map.46 = f32[64,512]{1,0:T(8,128)} custom-call(bf16[64,8192]{1,0:T(8,128)(2,1)} %maximum_maximum_fusion.1.left_ref, bf16[8192,512]{1,0:T(8,128)(2,1)} %bitcast.39), custom_call_target="tpu_custom_call" | custom-call | tf_op jit(solution)/shard_map/pallas_call | solution.py:29
  114.0 1.0 reduce_precision.11
  115.1 0.7 copy.10
  115.8 7.2 %all-to-all-start.1 = ((f32[2,2,8,2,512]{4,3,1,0,2:T(2,128)}), f32[2,2,8,2,512]{4,3,1,0,2:T(2,128)S(1)}, u32[]{:S(2)}, u32[]{:S(2)}) async-start(f32[2,2,8,2,512]{4,3,1,0,2:T(2,128)} %copy.10), calls=%async_computation.1 | async-start | bytes 262144 | tf_op jit(solution)/shard_map/all_to_all | solution.py:58
  123.2 6.2 %all-to-all-done.1 = f32[2,2,8,2,512]{4,3,1,0,2:T(2,128)S(1)} async-done(((f32[2,2,8,2,512]{4,3,1,0,2:T(2,128)}), f32[2,2,8,2,512]{4,3,1,0,2:T(2,128)S(1)}, u32[]{:S(2)}, u32[]{:S(2)}) %all-to-all-start.1) | async-done | bytes 131104 | tf_op jit(solution)/shard_map/all_to_all | solution.py:58
  129.5 0.8 gather_fusion
  130.5 15.3 %all_to_all.15 = f32[2,32,2,512]{3,2,0,1:T(2,128)S(1)} all-to-all(f32[2,32,2,512]{3,2,0,1:T(2,128)S(1)} %select_bitcast_fusion), channel_id=1, replica_groups=mesh['sa'=8,'sb'=4,'sl'=8] {'sa','sb'}, dimensions={1} | all-to-all | bytes 524288 | tf_op jit(solution)/shard_map/all_to_all | solution.py:80
  145.9 0.3 fusion.4
  146.2 0.3 fusion
  146.6 0.3 convolution_subtract_fusion
  146.9 0.3 convolution_add_fusion
  147.2 0.6 pad_maximum_fusion.1
  (27 shorter events, 1.0 us)
Async XLA Ops:
  0.0 10.1 %copy-start.1 = (s32[32]{0:T(128)S(1)}, s32[32]{0:T(128)}, u32[]{:S(2)}) copy-start(s32[32]{0:T(128)} %param.7) | copy-start | bytes 388
  1.3 37.4 %collective-permute-start = (bf16[2,64,4096]{2,1,0:T(8,128)(2,1)S(1)}, bf16[2,64,4096]{2,1,0:T(8,128)(2,1)S(1)}, u32[]{:S(2)}, u32[]{:S(2)}) collective-permute-start(bf16[2,64,4096]{2,1,0:T(8,128)(2,1)S(1)} %slice.52), channel_id=1, source_target_pairs={{0,128},{32,160},{64,192},{96,224},{128,0},{160,32},{192,64},{224,... | collective-permute-start | bytes 3145736 | tf_op jit(solution)/shard_map/ppermute | solution.py:71
  8.6 86.4 %slice-start = ((s8[8388608]{0:T(1024)(128)(4,1)}), s8[4194304]{0:T(1024)(128)(4,1)S(1)}, s32[]{:S(2)}) async-start(s8[8388608]{0:T(1024)(128)(4,1)} %bitcast.40), calls=%async_computation.3 | async-start | bytes 8388608
  10.0 65.7 %collective-permute-start.1 = (bf16[2,32,4096]{2,1,0:T(8,128)(2,1)S(1)}, bf16[2,32,4096]{2,1,0:T(8,128)(2,1)S(1)}, u32[]{:S(2)}, u32[]{:S(2)}) collective-permute-start(bf16[2,32,4096]{2,1,0:T(8,128)(2,1)S(1)} %get-tuple-element.7), channel_id=1, source_target_pairs={{0,136},{8,128},{16,152},{24,144},{32,168},{40,160},{48,184},{56,1... | collective-permute-start | bytes 1572872 | tf_op jit(solution)/shard_map/ppermute | solution.py:72
  75.8 19.2 %slice-start.1 = ((s8[8388608]{0:T(1024)(128)(4,1)}), s8[4194304]{0:T(1024)(128)(4,1)S(1)}, s32[]{:S(2)}) async-start(s8[8388608]{0:T(1024)(128)(4,1)} %bitcast.40), calls=%async_computation.4 | async-start | bytes 8388608
  76.0 29.3 %collective-permute-start.2 = (bf16[2,32,4096]{2,1,0:T(8,128)(2,1)S(1)}, bf16[2,32,4096]{2,1,0:T(8,128)(2,1)S(1)}, u32[]{:S(2)}, u32[]{:S(2)}) collective-permute-start(bf16[2,32,4096]{2,1,0:T(8,128)(2,1)S(1)} %get-tuple-element.6), channel_id=1, source_target_pairs={{0,136},{8,128},{16,152},{24,144},{32,168},{40,160},{48,184},{56,1... | collective-permute-start | bytes 1572872 | tf_op jit(solution)/shard_map/ppermute | solution.py:74
  97.9 17.9 %all-to-all-start = ((f32[2,6,8,2,512]{4,3,1,0,2:T(2,128)}), f32[2,6,8,2,512]{4,3,1,0,2:T(2,128)S(1)}, u32[]{:S(2)}, u32[]{:S(2)}) async-start(f32[2,6,8,2,512]{4,3,1,0,2:T(2,128)} %copy.9), calls=%async_computation | async-start | bytes 786432 | tf_op jit(solution)/shard_map/all_to_all | solution.py:58
  114.0 31.9 %copy-start = (bf16[2,512,512]{2,1,0:T(8,128)(2,1)S(1)}, bf16[2,512,512]{2,1,0:T(8,128)(2,1)}, u32[]{:S(2)}) copy-start(bf16[2,512,512]{2,1,0:T(8,128)(2,1)} %param.6) | copy-start | bytes 3145732
  115.8 13.6 %all-to-all-start.1 = ((f32[2,2,8,2,512]{4,3,1,0,2:T(2,128)}), f32[2,2,8,2,512]{4,3,1,0,2:T(2,128)S(1)}, u32[]{:S(2)}, u32[]{:S(2)}) async-start(f32[2,2,8,2,512]{4,3,1,0,2:T(2,128)} %copy.10), calls=%async_computation.1 | async-start | bytes 262144 | tf_op jit(solution)/shard_map/all_to_all | solution.py:58

commit v13 on v6

--- a/solution.py
+++ b/solution.py
@@ -52,8 +52,11 @@
     wanted = jnp.take(q, group_rows, axis=1)
     chosen = lax.all_to_all(wanted, ("sa", "sb"), 1, 1, tiled=True).sum(axis=1)
     gates = final_gates.astype(jnp.float32)
-    out_real, out_imag = complex_dot(chosen[0], chosen[1], gates, precision=lax.Precision.HIGHEST)
-    return jnp.concatenate([out_real, out_imag], axis=1)
+    block = jnp.concatenate(
+        [jnp.concatenate([gates[0], gates[1]], axis=1), jnp.concatenate([-gates[1], gates[0]], axis=1)], axis=0
+    )
+    left = jnp.concatenate([chosen[0], chosen[1]], axis=1)
+    return jnp.dot(left, block, preferred_element_type=jnp.float32, precision=lax.Precision.HIGHEST)
 
 
 def solution(mesh):

time: 145 us -> 150 us (1.034)
  blocking collectives: 15.3 us -> 0 us
  waiting for transfers between devices: 73.3 us -> 83.8 us
  starting transfers between devices: 26.9 us -> 30.8 us
  matrix products: 7.99 us -> 11.3 us
    all_to_all x1 -> x0, blocking collectives: 15.3 us -> none  [local(): chosen = lax.all_to_all(wanted, ('sa', 'sb'), 1, 1, tiled=True).sum(axis=1)]
    all_to_all x0 -> x1, waiting for transfers between devices: none -> 10.7 us  [local(): chosen = lax.all_to_all(wanted, ('sa', 'sb'), 1, 1, tiled=True).sum(axis=1)]
    all_to_all x0 -> x1, starting transfers between devices: none -> 3.87 us  [local(): chosen = lax.all_to_all(wanted, ('sa', 'sb'), 1, 1, tiled=True).sum(axis=1)]
    dot_general x4 -> x1, matrix products: 1.26 us -> 4.54 us  [local(): jnp.dot(left, block, preferred_element_type=jnp.float32, precision=lax.Pr...]
    squeeze x0 -> x2, local copies, waits for them, and re-layouts: none -> 1.51 us  [the longest x1 1.5 us: local(): gates[1]]
  transfers between devices with their start and end apart: 5 -> 6, of which waited for: 4 -> 5; matrix products, arithmetic and copies ran while one was open for 16% -> 17% of each run, Pallas kernels for 0% -> 0%
where the time goes in v13:
time: 150 us; the launch traced here: 149 us
  waiting for transfers between devices  83.8 us (56%)
  starting transfers between devices  30.8 us (21%)
  other arithmetic  15.3 us (10%)
  matrix products  11.3 us (8%)
  local copies, waits for them, and re-layouts  7.06 us (5%)
    ppermute x1, waiting for transfers between devices, local(): middle = lax.ppermute(stem[:, half:cut], ('sa', 'sb'), diagonal)  37 us
    ppermute x1, waiting for transfers between devices, local(): lower = lax.ppermute(stem[:, :half], 'sa', straight)  28.6 us
    all_to_all x2, starting transfers between devices, pair_sums(): return lax.all_to_all(q, 'sl', 2, 2, tiled=True).sum(axis=2)  13.3 us
    concatenate x2, other arithmetic, stacked_dot(): jnp.concatenate([jnp.concatenate([stem[0], -stem[1]], axis=1), jnp.concat...  12.7 us
    all_to_all x1, waiting for transfers between devices, local(): chosen = lax.all_to_all(wanted, ('sa', 'sb'), 1, 1, tiled=True).sum(axis=1)  10.7 us
    all_to_all x2, waiting for transfers between devices, pair_sums(): return lax.all_to_all(q, 'sl', 2, 2, tiled=True).sum(axis=2)  7.46 us
    ppermute x1, starting transfers between devices, local(): lower = lax.ppermute(stem[:, :half], 'sa', straight)  7.28 us
    dot_general x2, matrix products, stacked_dot(): out = jnp.dot(left, right, preferred_element_type=jnp.float32)  6.81 us
  transfers between devices with their start and end apart: 6, of which 5 were waited for; matrix products, arithmetic and copies ran while one was open for 17% of the time, Pallas kernels for 0%

profile of v13, /device:TPU:2, one launch (start us, length us, event | category | flops | bytes accessed | tf_op | source)
XLA Modules:
  0.0 148.5 jit_solution(16155261963589907226)
XLA Ops:
  0.0 1.3 slice.52
  1.3 7.3 %collective-permute-start = (bf16[2,64,4096]{2,1,0:T(8,128)(2,1)S(1)}, bf16[2,64,4096]{2,1,0:T(8,128)(2,1)S(1)}, u32[]{:S(2)}, u32[]{:S(2)}) collective-permute-start(bf16[2,64,4096]{2,1,0:T(8,128)(2,1)S(1)} %slice.52), channel_id=1, source_target_pairs={{0,128},{32,160},{64,192},{96,224},{128,0},{160,32},{192,64},{224,... | collective-permute-start | bytes 3145736 | tf_op jit(solution)/shard_map/ppermute | solution.py:44
  8.6 1.4 fusion.15
  10.1 28.6 %collective-permute-done = bf16[2,64,4096]{2,1,0:T(8,128)(2,1)S(1)} collective-permute-done((bf16[2,64,4096]{2,1,0:T(8,128)(2,1)S(1)}, bf16[2,64,4096]{2,1,0:T(8,128)(2,1)S(1)}, u32[]{:S(2)}, u32[]{:S(2)}) %collective-permute-start) | collective-permute-done | bytes 1048608 | tf_op jit(solution)/shard_map/ppermute | solution.py:44
  38.8 37.0 %collective-permute-done.1 = bf16[2,32,4096]{2,1,0:T(8,128)(2,1)S(1)} collective-permute-done((bf16[2,32,4096]{2,1,0:T(8,128)(2,1)S(1)}, bf16[2,32,4096]{2,1,0:T(8,128)(2,1)S(1)}, u32[]{:S(2)}, u32[]{:S(2)}) %collective-permute-start.1) | collective-permute-done | bytes 524320 | tf_op jit(solution)/shard_map/ppermute | solution.py:45
  76.0 6.3 %collective-permute-start.2 = (bf16[2,32,4096]{2,1,0:T(8,128)(2,1)S(1)}, bf16[2,32,4096]{2,1,0:T(8,128)(2,1)S(1)}, u32[]{:S(2)}, u32[]{:S(2)}) collective-permute-start(bf16[2,32,4096]{2,1,0:T(8,128)(2,1)S(1)} %get-tuple-element.6), channel_id=1, source_target_pairs={{0,136},{8,128},{16,152},{24,144},{32,168},{40,160},{48,184},{56,1... | collective-permute-start | bytes 1572872 | tf_op jit(solution)/shard_map/ppermute | solution.py:47
  82.3 12.7 %maximum_maximum_fusion = bf16[192,8192]{1,0:T(8,128)(2,1)S(1)} fusion(bf16[96,4096]{1,0:T(8,128)(2,1)S(1)} %get-tuple-element.12, bf16[96,4096]{1,0:T(8,128)(2,1)S(1)} %get-tuple-element.11, bf16[96,4096]{1,0:T(8,128)(2,1)S(1)} %fusion.14), kind=kLoop, calls=%fused_computation.9 | loop fusion | flops 12582912 | bytes 5505024 | tf_op jit(solution)/shard_map/concatenate | solution.py:19
  95.0 1.8 %convolution_reduce-precision_fusion = f32[2,96,512]{2,1,0:T(8,128)S(1)} fusion(bf16[2,96,8192]{2,1,0:T(8,128)(2,1)S(1)} %bitcast.39, bf16[8192,512,1]{1,0,2:T(8,128)(2,1)S(1)} %bitcast.37), kind=kOutput, calls=%fused_computation.10 | convolution fusion | flops 1610711040 | bytes 11927552 | tf_op jit(solution)/shard_map/dot_general | solution.py:23
  96.8 0.2 reshape.15
  97.1 0.8 copy.9
  97.8 7.5 %all-to-all-start = ((f32[2,6,8,2,512]{4,3,1,0,2:T(2,128)}), f32[2,6,8,2,512]{4,3,1,0,2:T(2,128)S(1)}, u32[]{:S(2)}, u32[]{:S(2)}) async-start(f32[2,6,8,2,512]{4,3,1,0,2:T(2,128)} %copy.9), calls=%async_computation | async-start | bytes 786432 | tf_op jit(solution)/shard_map/all_to_all | solution.py:31
  105.5 5.0 %convolution_reduce-precision_fusion.1 = f32[2,32,512]{2,1,0:T(8,128)S(1)} fusion(bf16[2,32,8192]{2,1,0:T(8,128)(2,1)S(1)} %bitcast.38, bf16[8192,512,1]{1,0,2:T(8,128)(2,1)} %bitcast.34), kind=kOutput, calls=%fused_computation.11 | convolution fusion | flops 536903680 | bytes 9568256 | tf_op jit(solution)/shard_map/dot_general | solution.py:23
  110.6 0.6 copy.10
  111.2 1.4 all-to-all-done
  112.7 5.8 %all-to-all-start.1 = ((f32[2,2,8,2,512]{4,3,1,0,2:T(2,128)}), f32[2,2,8,2,512]{4,3,1,0,2:T(2,128)}, u32[]{:S(2)}, u32[]{:S(2)}) async-start(f32[2,2,8,2,512]{4,3,1,0,2:T(2,128)} %copy.10), calls=%async_computation.1 | async-start | bytes 262144 | tf_op jit(solution)/shard_map/all_to_all | solution.py:31
  118.5 0.3 convert_element_type.3
  118.9 6.0 %all-to-all-done.1 = f32[2,2,8,2,512]{4,3,1,0,2:T(2,128)} async-done(((f32[2,2,8,2,512]{4,3,1,0,2:T(2,128)}), f32[2,2,8,2,512]{4,3,1,0,2:T(2,128)}, u32[]{:S(2)}, u32[]{:S(2)}) %all-to-all-start.1) | async-done | bytes 131104 | tf_op jit(solution)/shard_map/all_to_all | solution.py:31
  125.0 1.0 reduce_sum.28
  125.9 0.8 gather_fusion
  126.8 0.9 select_bitcast_fusion
  127.7 3.9 %all-to-all-start.2 = ((f32[2,32,2,512]{3,2,0,1:T(2,128)}), f32[2,32,2,512]{3,2,0,1:T(2,128)S(1)}, u32[]{:S(2)}, u32[]{:S(2)}) async-start(f32[2,32,2,512]{3,2,0,1:T(2,128)} %select_bitcast_fusion), calls=%async_computation.2 | async-start | bytes 524288 | tf_op jit(solution)/shard_map/all_to_all | solution.py:53
  131.6 1.5 %slice_bitcast_fusion = (f32[512,512]{1,0:T(8,128)}, f32[512,512]{1,0:T(8,128)}) fusion(f32[2,512,512]{2,1,0:T(8,128)S(1)} %convert_element_type.3), kind=kLoop, calls=%fused_computation.12 | loop fusion | bytes 4194304 | tf_op jit(solution)/shard_map/squeeze | solution.py:56
  133.1 10.7 %all-to-all-done.2 = f32[2,32,2,512]{3,2,0,1:T(2,128)S(1)} async-done(((f32[2,32,2,512]{3,2,0,1:T(2,128)}), f32[2,32,2,512]{3,2,0,1:T(2,128)S(1)}, u32[]{:S(2)}, u32[]{:S(2)}) %all-to-all-start.2) | async-done | bytes 262176 | tf_op jit(solution)/shard_map/all_to_all | solution.py:53
  144.0 4.5 %fusion = f32[2,1024]{1,0:T(2,128)} fusion(f32[512,512]{1,0:T(8,128)} %get-tuple-element.10, f32[512,512]{1,0:T(8,128)S(1)} %fusion.13, f32[512,512]{1,0:T(8,128)} %get-tuple-element.9, f32[2,512]{1,0:T(2,128)S(1)} %get-tuple-element.16, f32[2,512]{1,0:T(2,128)S(1)} %get-tuple-element.15), kind=kOutput, calls=%fused_computation.1 | convolution fusion | flops 28313600 | bytes 3162112 | tf_op jit(solution)/shard_map/dot_general | solution.py:59
  (27 shorter events, 1.0 us)
Async XLA Ops:
  0.0 10.1 %copy-start.1 = (s32[32]{0:T(128)S(1)}, s32[32]{0:T(128)}, u32[]{:S(2)}) copy-start(s32[32]{0:T(128)} %param.7) | copy-start | bytes 388
  1.3 37.4 %collective-permute-start = (bf16[2,64,4096]{2,1,0:T(8,128)(2,1)S(1)}, bf16[2,64,4096]{2,1,0:T(8,128)(2,1)S(1)}, u32[]{:S(2)}, u32[]{:S(2)}) collective-permute-start(bf16[2,64,4096]{2,1,0:T(8,128)(2,1)S(1)} %slice.52), channel_id=1, source_target_pairs={{0,128},{32,160},{64,192},{96,224},{128,0},{160,32},{192,64},{224,... | collective-permute-start | bytes 3145736 | tf_op jit(solution)/shard_map/ppermute | solution.py:44
  8.6 86.4 %slice-start = ((s8[8388608]{0:T(1024)(128)(4,1)}), s8[4194304]{0:T(1024)(128)(4,1)S(1)}, s32[]{:S(2)}) async-start(s8[8388608]{0:T(1024)(128)(4,1)} %bitcast.35), calls=%async_computation.3 | async-start | bytes 8388608
  10.0 65.7 %collective-permute-start.1 = (bf16[2,32,4096]{2,1,0:T(8,128)(2,1)S(1)}, bf16[2,32,4096]{2,1,0:T(8,128)(2,1)S(1)}, u32[]{:S(2)}, u32[]{:S(2)}) collective-permute-start(bf16[2,32,4096]{2,1,0:T(8,128)(2,1)S(1)} %get-tuple-element.7), channel_id=1, source_target_pairs={{0,136},{8,128},{16,152},{24,144},{32,168},{40,160},{48,184},{56,1... | collective-permute-start | bytes 1572872 | tf_op jit(solution)/shard_map/ppermute | solution.py:45
  75.8 19.2 %slice-start.1 = ((s8[8388608]{0:T(1024)(128)(4,1)}), s8[4194304]{0:T(1024)(128)(4,1)S(1)}, s32[]{:S(2)}) async-start(s8[8388608]{0:T(1024)(128)(4,1)} %bitcast.35), calls=%async_computation.4 | async-start | bytes 8388608
  76.0 29.3 %collective-permute-start.2 = (bf16[2,32,4096]{2,1,0:T(8,128)(2,1)S(1)}, bf16[2,32,4096]{2,1,0:T(8,128)(2,1)S(1)}, u32[]{:S(2)}, u32[]{:S(2)}) collective-permute-start(bf16[2,32,4096]{2,1,0:T(8,128)(2,1)S(1)} %get-tuple-element.6), channel_id=1, source_target_pairs={{0,136},{8,128},{16,152},{24,144},{32,168},{40,160},{48,184},{56,1... | collective-permute-start | bytes 1572872 | tf_op jit(solution)/shard_map/ppermute | solution.py:47
  97.8 14.8 %all-to-all-start = ((f32[2,6,8,2,512]{4,3,1,0,2:T(2,128)}), f32[2,6,8,2,512]{4,3,1,0,2:T(2,128)S(1)}, u32[]{:S(2)}, u32[]{:S(2)}) async-start(f32[2,6,8,2,512]{4,3,1,0,2:T(2,128)} %copy.9), calls=%async_computation | async-start | bytes 786432 | tf_op jit(solution)/shard_map/all_to_all | solution.py:31
  105.5 13.0 %copy-start = (bf16[2,512,512]{2,1,0:T(8,128)(2,1)S(1)}, bf16[2,512,512]{2,1,0:T(8,128)(2,1)}, u32[]{:S(2)}) copy-start(bf16[2,512,512]{2,1,0:T(8,128)(2,1)} %param.6) | copy-start | bytes 3145732
  112.7 12.3 %all-to-all-start.1 = ((f32[2,2,8,2,512]{4,3,1,0,2:T(2,128)}), f32[2,2,8,2,512]{4,3,1,0,2:T(2,128)}, u32[]{:S(2)}, u32[]{:S(2)}) async-start(f32[2,2,8,2,512]{4,3,1,0,2:T(2,128)} %copy.10), calls=%async_computation.1 | async-start | bytes 262144 | tf_op jit(solution)/shard_map/all_to_all | solution.py:31
  127.7 16.2 %all-to-all-start.2 = ((f32[2,32,2,512]{3,2,0,1:T(2,128)}), f32[2,32,2,512]{3,2,0,1:T(2,128)S(1)}, u32[]{:S(2)}, u32[]{:S(2)}) async-start(f32[2,32,2,512]{3,2,0,1:T(2,128)} %select_bitcast_fusion), calls=%async_computation.2 | async-start | bytes 524288 | tf_op jit(solution)/shard_map/all_to_all | solution.py:53

commit v14 on v6

--- a/solution.py
+++ b/solution.py
@@ -41,9 +41,10 @@
     straight = [(i, i ^ flip) for i in range(n_sa)]
     diagonal = [(a * n_sb + b, (a ^ flip) * n_sb + (b ^ 1)) for a in range(n_sa) for b in range(n_sb)]
     cut = rows - rows // 4
-    lower = lax.ppermute(stem[:, :half], "sa", straight)
-    middle = lax.ppermute(stem[:, half:cut], ("sa", "sb"), diagonal)
-    last_src, _, _ = lax.optimization_barrier((stem[:, cut:], lower, middle))
+    lower_parts = [lax.ppermute(stem[part, :half], "sa", straight) for part in range(2)]
+    middle_parts = [lax.ppermute(stem[part, half:cut], ("sa", "sb"), diagonal) for part in range(2)]
+    last_src, *landed = lax.optimization_barrier((stem[:, cut:], *lower_parts, *middle_parts))
+    lower, middle = jnp.stack(landed[:2]), jnp.stack(landed[2:])
     last = lax.ppermute(last_src, ("sa", "sb"), diagonal)
     first = jnp.concatenate([lower, middle], axis=1)
     q_first = pair_sums(stacked_dot(first, subtree), n_sl)

time: 145 us -> 145 us (level)
  waiting for transfers between devices: 73.3 us -> 66.8 us
  starting transfers between devices: 26.9 us -> 32.6 us
    ppermute x2 -> x4, waiting for transfers between devices: 65.6 us -> 59 us  [the longest x2 59 us: local(): lax.ppermute(stem[part, half:cut], ('sa', 'sb'), diagonal)]
    ppermute x2 -> x4, starting transfers between devices: 7.37 us -> 13.1 us  [the longest x2 7.38 us: local(): lax.ppermute(stem[part, :half], 'sa', straight)]
    squeeze x0 -> x2, local copies, waits for them, and re-layouts: none -> 2.49 us  [the longest x1 1.28 us: local(): stem[part, :half]]
    slice x2 -> x1, local copies, waits for them, and re-layouts: 2.73 us -> 1.08 us  [local(): stem[:, cut:]]
  transfers between devices with their start and end apart: 5 -> 7, of which waited for: 4 -> 4; matrix products, arithmetic and copies ran while one was open for 16% -> 17% of each run, Pallas kernels for 0% -> 0%
where the time goes in v14:
time: 145 us; the launch traced here: 143 us
  waiting for transfers between devices  66.8 us (46%)
  starting transfers between devices  32.6 us (22%)
  blocking collectives  15.3 us (11%)
  other arithmetic  14.1 us (10%)
  matrix products  7.99 us (6%)
  local copies, waits for them, and re-layouts  6.34 us (4%)
    ppermute x2, waiting for transfers between devices, local(): lax.ppermute(stem[part, half:cut], ('sa', 'sb'), diagonal)  59 us
    all_to_all x1, blocking collectives, local(): chosen = lax.all_to_all(wanted, ('sa', 'sb'), 1, 1, tiled=True).sum(axis=1)  15.3 us
    all_to_all x2, starting transfers between devices, pair_sums(): return lax.all_to_all(q, 'sl', 2, 2, tiled=True).sum(axis=2)  13.2 us
    concatenate x2, other arithmetic, stacked_dot(): jnp.concatenate([jnp.concatenate([stem[0], -stem[1]], axis=1), jnp.concat...  12.7 us
    all_to_all x2, waiting for transfers between devices, pair_sums(): return lax.all_to_all(q, 'sl', 2, 2, tiled=True).sum(axis=2)  7.73 us
    ppermute x2, starting transfers between devices, local(): lax.ppermute(stem[part, :half], 'sa', straight)  7.38 us
    dot_general x2, matrix products, stacked_dot(): out = jnp.dot(left, right, preferred_element_type=jnp.float32)  6.73 us
    ppermute x1, starting transfers between devices, local(): last = lax.ppermute(last_src, ('sa', 'sb'), diagonal)  6.34 us
  transfers between devices with their start and end apart: 7, of which 4 were waited for; matrix products, arithmetic and copies ran while one was open for 17% of the time, Pallas kernels for 0%

profile of v14, /device:TPU:2, one launch (start us, length us, event | category | flops | bytes accessed | tf_op | source)
XLA Modules:
  0.0 143.3 jit_solution(16677175973186570434)
XLA Ops:
  0.0 1.3 slice_bitcast_fusion.2
  1.3 7.3 %collective-permute-start = (bf16[64,4096]{1,0:T(8,128)(2,1)S(1)}, bf16[64,4096]{1,0:T(8,128)(2,1)S(1)}, u32[]{:S(2)}, u32[]{:S(2)}) collective-permute-start(bf16[64,4096]{1,0:T(8,128)(2,1)S(1)} %get-tuple-element.18), channel_id=1, source_target_pairs={{0,128},{32,160},{64,192},{96,224},{128,0},{160,32},{192,64},{224,... | collective-permute-start | bytes 1572872 | tf_op jit(solution)/shard_map/ppermute | solution.py:44
  8.7 1.2 slice_bitcast_fusion.6
  9.9 4.8 %collective-permute-start.2 = (bf16[32,4096]{1,0:T(8,128)(2,1)S(1)}, bf16[32,4096]{1,0:T(8,128)(2,1)S(1)}, u32[]{:S(2)}, u32[]{:S(2)}) collective-permute-start(bf16[32,4096]{1,0:T(8,128)(2,1)S(1)} %get-tuple-element.16), channel_id=1, source_target_pairs={{0,136},{8,128},{16,152},{24,144},{32,168},{40,160},{48,184},{56,1... | collective-permute-start | bytes 786440 | tf_op jit(solution)/shard_map/ppermute | solution.py:45
  14.7 0.9 collective-permute-start.3
  15.6 1.1 slice.60
  16.7 30.3 %collective-permute-done.2 = bf16[32,4096]{1,0:T(8,128)(2,1)S(1)} collective-permute-done((bf16[32,4096]{1,0:T(8,128)(2,1)S(1)}, bf16[32,4096]{1,0:T(8,128)(2,1)S(1)}, u32[]{:S(2)}, u32[]{:S(2)}) %collective-permute-start.2) | collective-permute-done | bytes 262176 | tf_op jit(solution)/shard_map/ppermute | solution.py:45
  47.0 28.7 %collective-permute-done.3 = bf16[32,4096]{1,0:T(8,128)(2,1)S(1)} collective-permute-done((bf16[32,4096]{1,0:T(8,128)(2,1)S(1)}, bf16[32,4096]{1,0:T(8,128)(2,1)S(1)}, u32[]{:S(2)}, u32[]{:S(2)}) %collective-permute-start.3) | collective-permute-done | bytes 262176 | tf_op jit(solution)/shard_map/ppermute | solution.py:45
  76.1 6.3 %collective-permute-start.4 = (bf16[2,32,4096]{2,1,0:T(8,128)(2,1)S(1)}, bf16[2,32,4096]{2,1,0:T(8,128)(2,1)S(1)}, u32[]{:S(2)}, u32[]{:S(2)}) collective-permute-start(bf16[2,32,4096]{2,1,0:T(8,128)(2,1)S(1)} %slice.60), channel_id=1, source_target_pairs={{0,136},{8,128},{16,152},{24,144},{32,168},{40,160},{48,184},{56,1... | collective-permute-start | bytes 1572872 | tf_op jit(solution)/shard_map/ppermute | solution.py:48
  82.5 12.7 %maximum_maximum_fusion = bf16[192,8192]{1,0:T(8,128)(2,1)S(1)} fusion(bf16[96,4096]{1,0:T(8,128)(2,1)S(1)} %get-tuple-element.20, bf16[96,4096]{1,0:T(8,128)(2,1)S(1)} %get-tuple-element.19, bf16[96,4096]{1,0:T(8,128)(2,1)S(1)} %fusion.11), kind=kLoop, calls=%fused_computation.1 | loop fusion | flops 12582912 | bytes 5505024 | tf_op jit(solution)/shard_map/concatenate | solution.py:19
  95.2 1.8 %convolution_reduce-precision_fusion = f32[2,96,512]{2,1,0:T(8,128)S(1)} fusion(bf16[2,96,8192]{2,1,0:T(8,128)(2,1)S(1)} %bitcast.59, bf16[8192,512,1]{1,0,2:T(8,128)(2,1)S(1)} %bitcast.57), kind=kOutput, calls=%fused_computation.3 | convolution fusion | flops 1610711040 | bytes 11927552 | tf_op jit(solution)/shard_map/dot_general | solution.py:23
  97.2 0.8 copy.9
  98.0 7.5 %all-to-all-start = ((f32[2,6,8,2,512]{4,3,1,0,2:T(2,128)}), f32[2,6,8,2,512]{4,3,1,0,2:T(2,128)S(1)}, u32[]{:S(2)}, u32[]{:S(2)}) async-start(f32[2,6,8,2,512]{4,3,1,0,2:T(2,128)} %copy.9), calls=%async_computation | async-start | bytes 786432 | tf_op jit(solution)/shard_map/all_to_all | solution.py:31
  105.6 4.9 %convolution_reduce-precision_fusion.1 = f32[2,32,512]{2,1,0:T(8,128)S(1)} fusion(bf16[2,32,8192]{2,1,0:T(8,128)(2,1)S(1)} %bitcast.58, bf16[8192,512,1]{1,0,2:T(8,128)(2,1)} %bitcast.54), kind=kOutput, calls=%fused_computation.4 | convolution fusion | flops 536903680 | bytes 9568256 | tf_op jit(solution)/shard_map/dot_general | solution.py:23
  110.6 0.7 copy.10
  111.3 1.5 %all-to-all-done = f32[2,6,8,2,512]{4,3,1,0,2:T(2,128)S(1)} async-done(((f32[2,6,8,2,512]{4,3,1,0,2:T(2,128)}), f32[2,6,8,2,512]{4,3,1,0,2:T(2,128)S(1)}, u32[]{:S(2)}, u32[]{:S(2)}) %all-to-all-start) | async-done | bytes 393248 | tf_op jit(solution)/shard_map/all_to_all | solution.py:31
  112.8 5.7 %all-to-all-start.1 = ((f32[2,2,8,2,512]{4,3,1,0,2:T(2,128)}), f32[2,2,8,2,512]{4,3,1,0,2:T(2,128)S(1)}, u32[]{:S(2)}, u32[]{:S(2)}) async-start(f32[2,2,8,2,512]{4,3,1,0,2:T(2,128)} %copy.10), calls=%async_computation.1 | async-start | bytes 262144 | tf_op jit(solution)/shard_map/all_to_all | solution.py:31
  118.7 6.2 %all-to-all-done.1 = f32[2,2,8,2,512]{4,3,1,0,2:T(2,128)S(1)} async-done(((f32[2,2,8,2,512]{4,3,1,0,2:T(2,128)}), f32[2,2,8,2,512]{4,3,1,0,2:T(2,128)S(1)}, u32[]{:S(2)}, u32[]{:S(2)}) %all-to-all-start.1) | async-done | bytes 131104 | tf_op jit(solution)/shard_map/all_to_all | solution.py:31
  125.0 0.8 gather_fusion
  126.0 15.3 %all_to_all.15 = f32[2,32,2,512]{3,2,0,1:T(2,128)S(1)} all-to-all(f32[2,32,2,512]{3,2,0,1:T(2,128)S(1)} %select_bitcast_fusion), channel_id=1, replica_groups=mesh['sa'=8,'sb'=4,'sl'=8] {'sa','sb'}, dimensions={1} | all-to-all | bytes 524288 | tf_op jit(solution)/shard_map/all_to_all | solution.py:54
  141.8 0.3 fusion.4
  142.1 0.3 convolution_add_fusion
  142.4 0.3 convolution_subtract_fusion
  142.7 0.6 pad_maximum_fusion.1
  (30 shorter events, 1.7 us)
Async XLA Ops:
  0.0 16.7 %copy-start.1 = (s32[32]{0:T(128)S(1)}, s32[32]{0:T(128)}, u32[]{:S(2)}) copy-start(s32[32]{0:T(128)} %param.7) | copy-start | bytes 388
  1.3 74.5 %collective-permute-start = (bf16[64,4096]{1,0:T(8,128)(2,1)S(1)}, bf16[64,4096]{1,0:T(8,128)(2,1)S(1)}, u32[]{:S(2)}, u32[]{:S(2)}) collective-permute-start(bf16[64,4096]{1,0:T(8,128)(2,1)S(1)} %get-tuple-element.18), channel_id=1, source_target_pairs={{0,128},{32,160},{64,192},{96,224},{128,0},{160,32},{192,64},{224,... | collective-permute-start | bytes 1572872 | tf_op jit(solution)/shard_map/ppermute | solution.py:44
  8.6 67.2 %collective-permute-start.1 = (bf16[64,4096]{1,0:T(8,128)(2,1)S(1)}, bf16[64,4096]{1,0:T(8,128)(2,1)S(1)}, u32[]{:S(2)}, u32[]{:S(2)}) collective-permute-start(bf16[64,4096]{1,0:T(8,128)(2,1)S(1)} %get-tuple-element.17), channel_id=1, source_target_pairs={{0,128},{32,160},{64,192},{96,224},{128,0},{160,32},{192,64},{224,... | collective-permute-start | bytes 1572872 | tf_op jit(solution)/shard_map/ppermute | solution.py:44
  8.7 86.5 %slice-start = ((s8[8388608]{0:T(1024)(128)(4,1)}), s8[4194304]{0:T(1024)(128)(4,1)S(1)}, s32[]{:S(2)}) async-start(s8[8388608]{0:T(1024)(128)(4,1)} %bitcast.55), calls=%async_computation.3 | async-start | bytes 8388608
  9.9 37.2 %collective-permute-start.2 = (bf16[32,4096]{1,0:T(8,128)(2,1)S(1)}, bf16[32,4096]{1,0:T(8,128)(2,1)S(1)}, u32[]{:S(2)}, u32[]{:S(2)}) collective-permute-start(bf16[32,4096]{1,0:T(8,128)(2,1)S(1)} %get-tuple-element.16), channel_id=1, source_target_pairs={{0,136},{8,128},{16,152},{24,144},{32,168},{40,160},{48,184},{56,1... | collective-permute-start | bytes 786440 | tf_op jit(solution)/shard_map/ppermute | solution.py:45
  14.7 61.1 %collective-permute-start.3 = (bf16[32,4096]{1,0:T(8,128)(2,1)S(1)}, bf16[32,4096]{1,0:T(8,128)(2,1)S(1)}, u32[]{:S(2)}, u32[]{:S(2)}) collective-permute-start(bf16[32,4096]{1,0:T(8,128)(2,1)S(1)} %get-tuple-element.15), channel_id=1, source_target_pairs={{0,136},{8,128},{16,152},{24,144},{32,168},{40,160},{48,184},{56,1... | collective-permute-start | bytes 786440 | tf_op jit(solution)/shard_map/ppermute | solution.py:45
  75.9 19.3 %slice-start.1 = ((s8[8388608]{0:T(1024)(128)(4,1)}), s8[4194304]{0:T(1024)(128)(4,1)S(1)}, s32[]{:S(2)}) async-start(s8[8388608]{0:T(1024)(128)(4,1)} %bitcast.55), calls=%async_computation.4 | async-start | bytes 8388608
  76.1 29.3 %collective-permute-start.4 = (bf16[2,32,4096]{2,1,0:T(8,128)(2,1)S(1)}, bf16[2,32,4096]{2,1,0:T(8,128)(2,1)S(1)}, u32[]{:S(2)}, u32[]{:S(2)}) collective-permute-start(bf16[2,32,4096]{2,1,0:T(8,128)(2,1)S(1)} %slice.60), channel_id=1, source_target_pairs={{0,136},{8,128},{16,152},{24,144},{32,168},{40,160},{48,184},{56,1... | collective-permute-start | bytes 1572872 | tf_op jit(solution)/shard_map/ppermute | solution.py:48
  98.0 14.8 %all-to-all-start = ((f32[2,6,8,2,512]{4,3,1,0,2:T(2,128)}), f32[2,6,8,2,512]{4,3,1,0,2:T(2,128)S(1)}, u32[]{:S(2)}, u32[]{:S(2)}) async-start(f32[2,6,8,2,512]{4,3,1,0,2:T(2,128)} %copy.9), calls=%async_computation | async-start | bytes 786432 | tf_op jit(solution)/shard_map/all_to_all | solution.py:31
  110.5 30.9 %copy-start = (bf16[2,512,512]{2,1,0:T(8,128)(2,1)S(1)}, bf16[2,512,512]{2,1,0:T(8,128)(2,1)}, u32[]{:S(2)}) copy-start(bf16[2,512,512]{2,1,0:T(8,128)(2,1)} %param.6) | copy-start | bytes 3145732
  112.8 12.1 %all-to-all-start.1 = ((f32[2,2,8,2,512]{4,3,1,0,2:T(2,128)}), f32[2,2,8,2,512]{4,3,1,0,2:T(2,128)S(1)}, u32[]{:S(2)}, u32[]{:S(2)}) async-start(f32[2,2,8,2,512]{4,3,1,0,2:T(2,128)} %copy.10), calls=%async_computation.1 | async-start | bytes 262144 | tf_op jit(solution)/shard_map/all_to_all | solution.py:31

commit v15 on v6

--- a/solution.py
+++ b/solution.py
@@ -31,6 +31,21 @@
     return lax.all_to_all(q, "sl", 2, 2, tiled=True).sum(axis=2)
 
 
+def pair_major_sums(stem, subtree, n_sl):
+    blocks = stem.shape[1] // RB
+    k = stem.shape[2]
+    parts = stem.reshape(2, blocks, n_sl, RB // n_sl, k)
+    left = jnp.stack(
+        [jnp.concatenate([parts[0], -parts[1]], axis=-1), jnp.concatenate([parts[1], parts[0]], axis=-1)]
+    )
+    left = jnp.transpose(left, (2, 0, 1, 3, 4)).reshape(-1, 2 * k)
+    right = subtree.reshape(-1, subtree.shape[-1])
+    out = jnp.dot(left, right, preferred_element_type=jnp.float32)
+    q = lax.reduce_precision(out, exponent_bits=8, mantissa_bits=7)
+    q = q.reshape(n_sl, 2, blocks, RB // n_sl, out.shape[-1])
+    return lax.all_to_all(q, "sl", 0, 0, tiled=True).sum(axis=0)
+
+
 def local(stem_cache, subtree_cache, final_gates, group_rows):
     stem = stem_cache[0]
     subtree = subtree_cache[0]
@@ -47,7 +62,7 @@
     last = lax.ppermute(last_src, ("sa", "sb"), diagonal)
     first = jnp.concatenate([lower, middle], axis=1)
     q_first = pair_sums(stacked_dot(first, subtree), n_sl)
-    q_last = pair_sums(stacked_dot(last, subtree), n_sl)
+    q_last = pair_major_sums(last, subtree, n_sl)
     q = jnp.concatenate([q_first, q_last], axis=1)
     wanted = jnp.take(q, group_rows, axis=1)
     chosen = lax.all_to_all(wanted, ("sa", "sb"), 1, 1, tiled=True).sum(axis=1)

time: 145 us -> 148 us (1.021)
  other arithmetic: 13.9 us -> 16.5 us
  starting transfers between devices: 26.9 us -> 28.4 us
  waiting for transfers between devices: 73.3 us -> 71.8 us
    all_to_all x2 -> x1, waiting for transfers between devices: 7.73 us -> 0.01 us  [pair_sums(): return lax.all_to_all(q, 'sl', 2, 2, tiled=True).sum(axis=2)]
    all_to_all x0 -> x1, starting transfers between devices: none -> 7.21 us  [pair_major_sums(): return lax.all_to_all(q, 'sl', 0, 0, tiled=True).sum(axis=0)]
    all_to_all x0 -> x1, waiting for transfers between devices: none -> 6.23 us  [pair_major_sums(): return lax.all_to_all(q, 'sl', 0, 0, tiled=True).sum(axis=0)]
    all_to_all x2 -> x1, starting transfers between devices: 13.2 us -> 7.46 us  [pair_sums(): return lax.all_to_all(q, 'sl', 2, 2, tiled=True).sum(axis=2)]
    dot_general x0 -> x1, matrix products: none -> 5.03 us  [pair_major_sums(): out = jnp.dot(left, right, preferred_element_type=jnp.float32)]
    dot_general x2 -> x1, matrix products: 6.73 us -> 1.79 us  [stacked_dot(): out = jnp.dot(left, right, preferred_element_type=jnp.float32)]
    concatenate x2 -> x1, other arithmetic: 12.7 us -> 12.7 us  [stacked_dot(): jnp.concatenate([jnp.concatenate([stem[0], -stem[1]], axis=1), jnp.concat...]
  transfers between devices with their start and end apart: 5 -> 5, of which waited for: 4 -> 3; matrix products, arithmetic and copies ran while one was open for 16% -> 18% of each run, Pallas kernels for 0% -> 0%
where the time goes in v15:
time: 148 us; the launch traced here: 147 us
  waiting for transfers between devices  71.8 us (49%)
  starting transfers between devices  28.4 us (19%)
  other arithmetic  16.5 us (11%)
  blocking collectives  15.3 us (10%)
  matrix products  8.07 us (5%)
  local copies, waits for them, and re-layouts  6.36 us (4%)
    ppermute x1, waiting for transfers between devices, local(): middle = lax.ppermute(stem[:, half:cut], ('sa', 'sb'), diagonal)  37 us
    ppermute x1, waiting for transfers between devices, local(): lower = lax.ppermute(stem[:, :half], 'sa', straight)  28.6 us
    all_to_all x1, blocking collectives, local(): chosen = lax.all_to_all(wanted, ('sa', 'sb'), 1, 1, tiled=True).sum(axis=1)  15.3 us
    concatenate x1, other arithmetic, stacked_dot(): jnp.concatenate([jnp.concatenate([stem[0], -stem[1]], axis=1), jnp.concat...  12.7 us
    all_to_all x1, starting transfers between devices, pair_sums(): return lax.all_to_all(q, 'sl', 2, 2, tiled=True).sum(axis=2)  7.46 us
    ppermute x1, starting transfers between devices, local(): lower = lax.ppermute(stem[:, :half], 'sa', straight)  7.28 us
    all_to_all x1, starting transfers between devices, pair_major_sums(): return lax.all_to_all(q, 'sl', 0, 0, tiled=True).sum(axis=0)  7.21 us
    ppermute x1, starting transfers between devices, local(): last = lax.ppermute(last_src, ('sa', 'sb'), diagonal)  6.34 us
  transfers between devices with their start and end apart: 5, of which 3 were waited for; matrix products, arithmetic and copies ran while one was open for 18% of the time, Pallas kernels for 0%

profile of v15, /device:TPU:2, one launch (start us, length us, event | category | flops | bytes accessed | tf_op | source)
XLA Modules:
  0.0 146.6 jit_solution(375340588744785857)
XLA Ops:
  0.0 1.3 slice.54
  1.3 7.3 %collective-permute-start = (bf16[2,64,4096]{2,1,0:T(8,128)(2,1)S(1)}, bf16[2,64,4096]{2,1,0:T(8,128)(2,1)S(1)}, u32[]{:S(2)}, u32[]{:S(2)}) collective-permute-start(bf16[2,64,4096]{2,1,0:T(8,128)(2,1)S(1)} %slice.54), channel_id=1, source_target_pairs={{0,128},{32,160},{64,192},{96,224},{128,0},{160,32},{192,64},{224,... | collective-permute-start | bytes 3145736 | tf_op jit(solution)/shard_map/ppermute | solution.py:59
  8.6 1.4 fusion.11
  10.1 28.6 %collective-permute-done = bf16[2,64,4096]{2,1,0:T(8,128)(2,1)S(1)} collective-permute-done((bf16[2,64,4096]{2,1,0:T(8,128)(2,1)S(1)}, bf16[2,64,4096]{2,1,0:T(8,128)(2,1)S(1)}, u32[]{:S(2)}, u32[]{:S(2)}) %collective-permute-start) | collective-permute-done | bytes 1048608 | tf_op jit(solution)/shard_map/ppermute | solution.py:59
  38.8 37.0 %collective-permute-done.1 = bf16[2,32,4096]{2,1,0:T(8,128)(2,1)S(1)} collective-permute-done((bf16[2,32,4096]{2,1,0:T(8,128)(2,1)S(1)}, bf16[2,32,4096]{2,1,0:T(8,128)(2,1)S(1)}, u32[]{:S(2)}, u32[]{:S(2)}) %collective-permute-start.1) | collective-permute-done | bytes 524320 | tf_op jit(solution)/shard_map/ppermute | solution.py:60
  76.0 6.3 %collective-permute-start.2 = (bf16[2,32,4096]{2,1,0:T(8,128)(2,1)S(1)}, bf16[2,32,4096]{2,1,0:T(8,128)(2,1)S(1)}, u32[]{:S(2)}, u32[]{:S(2)}) collective-permute-start(bf16[2,32,4096]{2,1,0:T(8,128)(2,1)S(1)} %get-tuple-element.6), channel_id=1, source_target_pairs={{0,136},{8,128},{16,152},{24,144},{32,168},{40,160},{48,184},{56,1... | collective-permute-start | bytes 1572872 | tf_op jit(solution)/shard_map/ppermute | solution.py:62
  82.3 12.7 %maximum_maximum_fusion = bf16[192,8192]{1,0:T(8,128)(2,1)S(1)} fusion(bf16[96,4096]{1,0:T(8,128)(2,1)S(1)} %get-tuple-element.10, bf16[96,4096]{1,0:T(8,128)(2,1)S(1)} %get-tuple-element.9, bf16[96,4096]{1,0:T(8,128)(2,1)S(1)} %fusion.10), kind=kLoop, calls=%fused_computation.1 | loop fusion | flops 12582912 | bytes 5505024 | tf_op jit(solution)/shard_map/concatenate | solution.py:19
  95.0 1.8 %convolution_reduce-precision_fusion = f32[2,96,512]{2,1,0:T(8,128)S(1)} fusion(bf16[2,96,8192]{2,1,0:T(8,128)(2,1)S(1)} %bitcast.45, bf16[8192,512,1]{1,0,2:T(8,128)(2,1)S(1)} %bitcast.44), kind=kOutput, calls=%fused_computation.2 | convolution fusion | flops 1610711040 | bytes 11927552 | tf_op jit(solution)/shard_map/dot_general | solution.py:23
  97.1 0.8 copy.19
  97.8 7.5 %all-to-all-start = ((f32[2,6,8,2,512]{4,3,1,0,2:T(2,128)}), f32[2,6,8,2,512]{4,3,1,0,2:T(2,128)S(1)}, u32[]{:S(2)}, u32[]{:S(2)}) async-start(f32[2,6,8,2,512]{4,3,1,0,2:T(2,128)} %copy.19), calls=%async_computation | async-start | bytes 786432 | tf_op jit(solution)/shard_map/all_to_all | solution.py:31
  106.0 1.0 maximum_bitcast_fusion.1
  106.9 1.4 maximum_bitcast_fusion
  108.4 0.4 reshape.22
  108.8 5.0 %convolution_reduce-precision_fusion.1 = f32[64,512]{1,0:T(8,128)S(1)} fusion(bf16[64,8192]{1,0:T(8,128)(2,1)S(1)} %reshape.22, bf16[8192,512]{1,0:T(8,128)(2,1)} %bitcast.41), kind=kOutput, calls=%fused_computation.3 | convolution fusion | flops 536903680 | bytes 9568256 | tf_op jit(solution)/shard_map/dot_general | solution.py:43
  113.9 0.7 reshape.23
  114.6 7.2 %all-to-all-start.1 = ((f32[8,2,2,2,512]{4,3,2,1,0:T(2,128)}), f32[8,2,2,2,512]{4,3,2,1,0:T(2,128)S(1)}, u32[]{:S(2)}, u32[]{:S(2)}) async-start(f32[8,2,2,2,512]{4,3,2,1,0:T(2,128)} %reshape.23), calls=%async_computation.1 | async-start | bytes 262144 | tf_op jit(solution)/shard_map/all_to_all | solution.py:46
  122.0 6.2 %all-to-all-done.1 = f32[8,2,2,2,512]{4,3,2,1,0:T(2,128)S(1)} async-done(((f32[8,2,2,2,512]{4,3,2,1,0:T(2,128)}), f32[8,2,2,2,512]{4,3,2,1,0:T(2,128)S(1)}, u32[]{:S(2)}, u32[]{:S(2)}) %all-to-all-start.1) | async-done | bytes 131104 | tf_op jit(solution)/shard_map/all_to_all | solution.py:46
  128.3 0.8 gather_fusion
  129.3 15.3 %all_to_all.15 = f32[2,32,2,512]{3,2,0,1:T(2,128)S(1)} all-to-all(f32[2,32,2,512]{3,2,0,1:T(2,128)S(1)} %select_bitcast_fusion), channel_id=1, replica_groups=mesh['sa'=8,'sb'=4,'sl'=8] {'sa','sb'}, dimensions={1} | all-to-all | bytes 524288 | tf_op jit(solution)/shard_map/all_to_all | solution.py:68
  144.7 0.3 fusion.4
  145.1 0.3 fusion
  145.4 0.3 convolution_subtract_fusion
  145.7 0.3 convolution_add_fusion
  146.0 0.6 pad_maximum_fusion.2
  (29 shorter events, 1.7 us)
Async XLA Ops:
  0.0 10.1 %copy-start.1 = (s32[32]{0:T(128)S(1)}, s32[32]{0:T(128)}, u32[]{:S(2)}) copy-start(s32[32]{0:T(128)} %param.7) | copy-start | bytes 388
  1.3 37.4 %collective-permute-start = (bf16[2,64,4096]{2,1,0:T(8,128)(2,1)S(1)}, bf16[2,64,4096]{2,1,0:T(8,128)(2,1)S(1)}, u32[]{:S(2)}, u32[]{:S(2)}) collective-permute-start(bf16[2,64,4096]{2,1,0:T(8,128)(2,1)S(1)} %slice.54), channel_id=1, source_target_pairs={{0,128},{32,160},{64,192},{96,224},{128,0},{160,32},{192,64},{224,... | collective-permute-start | bytes 3145736 | tf_op jit(solution)/shard_map/ppermute | solution.py:59
  8.6 86.4 %slice-start = ((s8[8388608]{0:T(1024)(128)(4,1)}), s8[4194304]{0:T(1024)(128)(4,1)S(1)}, s32[]{:S(2)}) async-start(s8[8388608]{0:T(1024)(128)(4,1)} %bitcast.42), calls=%async_computation.3 | async-start | bytes 8388608
  10.0 65.7 %collective-permute-start.1 = (bf16[2,32,4096]{2,1,0:T(8,128)(2,1)S(1)}, bf16[2,32,4096]{2,1,0:T(8,128)(2,1)S(1)}, u32[]{:S(2)}, u32[]{:S(2)}) collective-permute-start(bf16[2,32,4096]{2,1,0:T(8,128)(2,1)S(1)} %get-tuple-element.7), channel_id=1, source_target_pairs={{0,136},{8,128},{16,152},{24,144},{32,168},{40,160},{48,184},{56,1... | collective-permute-start | bytes 1572872 | tf_op jit(solution)/shard_map/ppermute | solution.py:60
  75.8 19.2 %slice-start.1 = ((s8[8388608]{0:T(1024)(128)(4,1)}), s8[4194304]{0:T(1024)(128)(4,1)S(1)}, s32[]{:S(2)}) async-start(s8[8388608]{0:T(1024)(128)(4,1)} %bitcast.42), calls=%async_computation.4 | async-start | bytes 8388608
  76.0 29.3 %collective-permute-start.2 = (bf16[2,32,4096]{2,1,0:T(8,128)(2,1)S(1)}, bf16[2,32,4096]{2,1,0:T(8,128)(2,1)S(1)}, u32[]{:S(2)}, u32[]{:S(2)}) collective-permute-start(bf16[2,32,4096]{2,1,0:T(8,128)(2,1)S(1)} %get-tuple-element.6), channel_id=1, source_target_pairs={{0,136},{8,128},{16,152},{24,144},{32,168},{40,160},{48,184},{56,1... | collective-permute-start | bytes 1572872 | tf_op jit(solution)/shard_map/ppermute | solution.py:62
  97.8 16.8 %all-to-all-start = ((f32[2,6,8,2,512]{4,3,1,0,2:T(2,128)}), f32[2,6,8,2,512]{4,3,1,0,2:T(2,128)S(1)}, u32[]{:S(2)}, u32[]{:S(2)}) async-start(f32[2,6,8,2,512]{4,3,1,0,2:T(2,128)} %copy.19), calls=%async_computation | async-start | bytes 786432 | tf_op jit(solution)/shard_map/all_to_all | solution.py:31
  108.8 35.9 %copy-start = (bf16[2,512,512]{2,1,0:T(8,128)(2,1)S(1)}, bf16[2,512,512]{2,1,0:T(8,128)(2,1)}, u32[]{:S(2)}) copy-start(bf16[2,512,512]{2,1,0:T(8,128)(2,1)} %param.6) | copy-start | bytes 3145732
  114.6 13.6 %all-to-all-start.1 = ((f32[8,2,2,2,512]{4,3,2,1,0:T(2,128)}), f32[8,2,2,2,512]{4,3,2,1,0:T(2,128)S(1)}, u32[]{:S(2)}, u32[]{:S(2)}) async-start(f32[8,2,2,2,512]{4,3,2,1,0:T(2,128)} %reshape.23), calls=%async_computation.1 | async-start | bytes 262144 | tf_op jit(solution)/shard_map/all_to_all | solution.py:46

commit v16 on v8

--- a/solution.py
+++ b/solution.py
@@ -45,8 +45,17 @@
     middle = lax.ppermute(stem[:, half:cut], ("sa", "sb"), diagonal)
     last_src, _, _ = lax.optimization_barrier((stem[:, cut:], lower, middle))
     last = lax.ppermute(last_src, ("sa", "sb"), diagonal)
-    first = jnp.concatenate([stacked_dot(lower, subtree), stacked_dot(middle, subtree)], axis=1)
-    q_first = pair_sums(first, n_sl)
+    left = jnp.concatenate(
+        [
+            jnp.concatenate([lower[0], -lower[1]], axis=1),
+            jnp.concatenate([middle[0], -middle[1]], axis=1),
+            jnp.concatenate([lower[1], lower[0]], axis=1),
+            jnp.concatenate([middle[1], middle[0]], axis=1),
+        ],
+        axis=0,
+    )
+    first = jnp.dot(left, subtree.reshape(-1, subtree.shape[-1]), preferred_element_type=jnp.float32)
+    q_first = pair_sums(first.reshape(2, -1, first.shape[-1]), n_sl)
     q_last = pair_sums(stacked_dot(last, subtree), n_sl)
     q = jnp.concatenate([q_first, q_last], axis=1)
     wanted = jnp.take(q, group_rows, axis=1)

time: 151 us -> 156 us (1.033)
  other arithmetic: 1.55 us -> 24.7 us
  waiting for transfers between devices: 81.5 us -> 74.6 us
  blocking collectives: 20.1 us -> 15.3 us
  matrix products: 12.5 us -> 8.08 us
  starting transfers between devices: 28.8 us -> 26.2 us
    concatenate x0 -> x1, other arithmetic: none -> 22.7 us  [local(): jnp.concatenate([jnp.concatenate([lower[0], -lower[1]], axis=1), jnp.conc...]
    ppermute x1, waiting for transfers between devices: 13 us -> 0.01 us  [local(): last = lax.ppermute(last_src, ('sa', 'sb'), diagonal)]
    dot_general x3 -> x1, matrix products: 11.3 us -> 5.03 us  [stacked_dot(): out = jnp.dot(left, right, preferred_element_type=jnp.float32)]
    ppermute x1, waiting for transfers between devices: 48.9 us -> 54 us  [local(): lower = lax.ppermute(stem[:, :half], 'sa', straight)]
    all_to_all x1, blocking collectives: 20.1 us -> 15.3 us  [local(): chosen = lax.all_to_all(wanted, ('sa', 'sb'), 1, 1, tiled=True).sum(axis=1)]
    all_to_all x2, waiting for transfers between devices: 6.24 us -> 8.75 us  [pair_sums(): return lax.all_to_all(q, 'sl', 2, 2, tiled=True).sum(axis=2)]
    all_to_all x2, starting transfers between devices: 14.9 us -> 12.6 us  [pair_sums(): return lax.all_to_all(q, 'sl', 2, 2, tiled=True).sum(axis=2)]
    dot_general x0 -> x1, matrix products: none -> 1.8 us  [local(): jnp.dot(left, subtree.reshape(-1, subtree.shape[-1]), preferred_element_t...]
  transfers between devices with their start and end apart: 5 -> 5, of which waited for: 4 -> 4; matrix products, arithmetic and copies ran while one was open for 9% -> 22% of each run, Pallas kernels for 0% -> 0%
where the time goes in v16:
time: 156 us; the launch traced here: 154 us
  waiting for transfers between devices  74.6 us (48%)
  starting transfers between devices  26.2 us (17%)
  other arithmetic  24.7 us (16%)
  blocking collectives  15.3 us (10%)
  matrix products  8.08 us (5%)
  local copies, waits for them, and re-layouts  5.29 us (3%)
    ppermute x1, waiting for transfers between devices, local(): lower = lax.ppermute(stem[:, :half], 'sa', straight)  54 us
    concatenate x1, other arithmetic, local(): jnp.concatenate([jnp.concatenate([lower[0], -lower[1]], axis=1), jnp.conc...  22.7 us
    all_to_all x1, blocking collectives, local(): chosen = lax.all_to_all(wanted, ('sa', 'sb'), 1, 1, tiled=True).sum(axis=1)  15.3 us
    all_to_all x2, starting transfers between devices, pair_sums(): return lax.all_to_all(q, 'sl', 2, 2, tiled=True).sum(axis=2)  12.6 us
    ppermute x1, waiting for transfers between devices, local(): middle = lax.ppermute(stem[:, half:cut], ('sa', 'sb'), diagonal)  11.8 us
    all_to_all x2, waiting for transfers between devices, pair_sums(): return lax.all_to_all(q, 'sl', 2, 2, tiled=True).sum(axis=2)  8.75 us
    ppermute x1, starting transfers between devices, local(): middle = lax.ppermute(stem[:, half:cut], ('sa', 'sb'), diagonal)  6.72 us
    ppermute x1, starting transfers between devices, local(): last = lax.ppermute(last_src, ('sa', 'sb'), diagonal)  6.08 us
  transfers between devices with their start and end apart: 5, of which 4 were waited for; matrix products, arithmetic and copies ran while one was open for 22% of the time, Pallas kernels for 0%

profile of v16, /device:TPU:2, one launch (start us, length us, event | category | flops | bytes accessed | tf_op | source)
XLA Modules:
  0.0 154.3 jit_solution(10742948076924444532)
XLA Ops:
  0.0 1.3 fusion.13
  1.3 6.7 %collective-permute-start.1 = (bf16[2,32,4096]{2,1,0:T(8,128)(2,1)S(1)}, bf16[2,32,4096]{2,1,0:T(8,128)(2,1)S(1)}, u32[]{:S(2)}, u32[]{:S(2)}) collective-permute-start(bf16[2,32,4096]{2,1,0:T(8,128)(2,1)S(1)} %get-tuple-element.7), channel_id=1, source_target_pairs={{0,136},{8,128},{16,152},{24,144},{32,168},{40,160},{48,184},{56,1... | collective-permute-start | bytes 1572872 | tf_op jit(solution)/shard_map/ppermute | solution.py:45
  8.0 1.3 slice.62
  9.3 0.8 collective-permute-start
  10.1 0.7 compare_select_fusion
  10.8 11.8 %collective-permute-done.1 = bf16[2,32,4096]{2,1,0:T(8,128)(2,1)S(1)} collective-permute-done((bf16[2,32,4096]{2,1,0:T(8,128)(2,1)S(1)}, bf16[2,32,4096]{2,1,0:T(8,128)(2,1)S(1)}, u32[]{:S(2)}, u32[]{:S(2)}) %collective-permute-start.1) | collective-permute-done | bytes 524320 | tf_op jit(solution)/shard_map/ppermute | solution.py:45
  22.6 54.0 %collective-permute-done = bf16[2,64,4096]{2,1,0:T(8,128)(2,1)S(1)} collective-permute-done((bf16[2,64,4096]{2,1,0:T(8,128)(2,1)S(1)}, bf16[2,64,4096]{2,1,0:T(8,128)(2,1)S(1)}, u32[]{:S(2)}, u32[]{:S(2)}) %collective-permute-start) | collective-permute-done | bytes 1048608 | tf_op jit(solution)/shard_map/ppermute | solution.py:44
  76.7 6.1 %collective-permute-start.2 = (bf16[2,32,4096]{2,1,0:T(8,128)(2,1)S(1)}, bf16[2,32,4096]{2,1,0:T(8,128)(2,1)S(1)}, u32[]{:S(2)}, u32[]{:S(2)}) collective-permute-start(bf16[2,32,4096]{2,1,0:T(8,128)(2,1)S(1)} %get-tuple-element.6), channel_id=1, source_target_pairs={{0,136},{8,128},{16,152},{24,144},{32,168},{40,160},{48,184},{56,1... | collective-permute-start | bytes 1572872 | tf_op jit(solution)/shard_map/ppermute | solution.py:47
  82.9 22.7 %maximum_maximum_fusion = bf16[192,8192]{1,0:T(8,128)(2,1)S(1)} fusion(bf16[32,4096]{1,0:T(8,128)(2,1)S(1)} %get-tuple-element.12, bf16[32,4096]{1,0:T(8,128)(2,1)S(1)} %get-tuple-element.11, bf16[64,4096]{1,0:T(8,128)(2,1)S(1)} %get-tuple-element.10, bf16[64,4096]{1,0:T(8,128)(2,1)S(1)} %get-tuple-element.9, bf16[32,4096]{1,0:T(8,128)(2,1)S(1)} %fusion.10, ...), kind=kLoop, calls=%fused_computation.1 | loop fusion | flops 25165824 | bytes 5505024 | tf_op jit(solution)/shard_map/concatenate | solution.py:48
  105.6 1.8 %convolution_reduce-precision_fusion = f32[2,96,512]{2,1,0:T(8,128)S(1)} fusion(bf16[2,96,8192]{2,1,0:T(8,128)(2,1)S(1)} %bitcast.51, bf16[8192,512,1]{1,0,2:T(8,128)(2,1)S(1)} %bitcast.49), kind=kOutput, calls=%fused_computation.2 | convolution fusion | flops 1610711040 | bytes 11927552 | tf_op jit(solution)/shard_map/dot_general | solution.py:57
  107.7 0.8 copy.9
  108.4 7.5 %all-to-all-start = ((f32[2,6,8,2,512]{4,3,1,0,2:T(2,128)}), f32[2,6,8,2,512]{4,3,1,0,2:T(2,128)S(1)}, u32[]{:S(2)}, u32[]{:S(2)}) async-start(f32[2,6,8,2,512]{4,3,1,0,2:T(2,128)} %copy.9), calls=%async_computation | async-start | bytes 786432 | tf_op jit(solution)/shard_map/all_to_all | solution.py:31
  116.1 5.0 %convolution_reduce-precision_fusion.1 = f32[2,32,512]{2,1,0:T(8,128)S(1)} fusion(bf16[2,32,8192]{2,1,0:T(8,128)(2,1)S(1)} %bitcast.50, bf16[8192,512,1]{1,0,2:T(8,128)(2,1)} %bitcast.48), kind=kOutput, calls=%fused_computation.3 | convolution fusion | flops 536903680 | bytes 9568256 | tf_op jit(solution)/shard_map/dot_general | solution.py:23
  121.2 0.7 copy.10
  121.8 2.5 %all-to-all-done = f32[2,6,8,2,512]{4,3,1,0,2:T(2,128)S(1)} async-done(((f32[2,6,8,2,512]{4,3,1,0,2:T(2,128)}), f32[2,6,8,2,512]{4,3,1,0,2:T(2,128)S(1)}, u32[]{:S(2)}, u32[]{:S(2)}) %all-to-all-start) | async-done | bytes 393248 | tf_op jit(solution)/shard_map/all_to_all | solution.py:31
  124.3 5.1 %all-to-all-start.1 = ((f32[2,2,8,2,512]{4,3,1,0,2:T(2,128)}), f32[2,2,8,2,512]{4,3,1,0,2:T(2,128)S(1)}, u32[]{:S(2)}, u32[]{:S(2)}) async-start(f32[2,2,8,2,512]{4,3,1,0,2:T(2,128)} %copy.10), calls=%async_computation.1 | async-start | bytes 262144 | tf_op jit(solution)/shard_map/all_to_all | solution.py:31
  129.6 6.2 %all-to-all-done.1 = f32[2,2,8,2,512]{4,3,1,0,2:T(2,128)S(1)} async-done(((f32[2,2,8,2,512]{4,3,1,0,2:T(2,128)}), f32[2,2,8,2,512]{4,3,1,0,2:T(2,128)S(1)}, u32[]{:S(2)}, u32[]{:S(2)}) %all-to-all-start.1) | async-done | bytes 131104 | tf_op jit(solution)/shard_map/all_to_all | solution.py:31
  135.9 0.8 gather_fusion
  137.0 15.3 %all_to_all.15 = f32[2,32,2,512]{3,2,0,1:T(2,128)S(1)} all-to-all(f32[2,32,2,512]{3,2,0,1:T(2,128)S(1)} %select_bitcast_fusion), channel_id=1, replica_groups=mesh['sa'=8,'sb'=4,'sl'=8] {'sa','sb'}, dimensions={1} | all-to-all | bytes 524288 | tf_op jit(solution)/shard_map/all_to_all | solution.py:62
  152.4 0.3 fusion.4
  152.7 0.3 fusion
  153.0 0.3 convolution_subtract_fusion
  153.3 0.3 convolution_add_fusion
  153.7 0.6 pad_maximum_fusion.1
  (23 shorter events, 1.1 us)
Async XLA Ops:
  1.3 104.3 %copy-start = (bf16[1,2,4096,512]{3,2,1,0:T(8,128)(2,1)S(1)}, bf16[1,2,4096,512]{3,2,1,0:T(8,128)(2,1)}, u32[]{:S(2)}) copy-start(bf16[1,2,4096,512]{3,2,1,0:T(8,128)(2,1)} %param.5) | copy-start | bytes 25165828
  1.3 21.3 %collective-permute-start.1 = (bf16[2,32,4096]{2,1,0:T(8,128)(2,1)S(1)}, bf16[2,32,4096]{2,1,0:T(8,128)(2,1)S(1)}, u32[]{:S(2)}, u32[]{:S(2)}) collective-permute-start(bf16[2,32,4096]{2,1,0:T(8,128)(2,1)S(1)} %get-tuple-element.7), channel_id=1, source_target_pairs={{0,136},{8,128},{16,152},{24,144},{32,168},{40,160},{48,184},{56,1... | collective-permute-start | bytes 1572872 | tf_op jit(solution)/shard_map/ppermute | solution.py:45
  9.3 67.4 %collective-permute-start = (bf16[2,64,4096]{2,1,0:T(8,128)(2,1)S(1)}, bf16[2,64,4096]{2,1,0:T(8,128)(2,1)S(1)}, u32[]{:S(2)}, u32[]{:S(2)}) collective-permute-start(bf16[2,64,4096]{2,1,0:T(8,128)(2,1)S(1)} %slice.62), channel_id=1, source_target_pairs={{0,128},{32,160},{64,192},{96,224},{128,0},{160,32},{192,64},{224,... | collective-permute-start | bytes 3145736 | tf_op jit(solution)/shard_map/ppermute | solution.py:44
  76.7 39.2 %collective-permute-start.2 = (bf16[2,32,4096]{2,1,0:T(8,128)(2,1)S(1)}, bf16[2,32,4096]{2,1,0:T(8,128)(2,1)S(1)}, u32[]{:S(2)}, u32[]{:S(2)}) collective-permute-start(bf16[2,32,4096]{2,1,0:T(8,128)(2,1)S(1)} %get-tuple-element.6), channel_id=1, source_target_pairs={{0,136},{8,128},{16,152},{24,144},{32,168},{40,160},{48,184},{56,1... | collective-permute-start | bytes 1572872 | tf_op jit(solution)/shard_map/ppermute | solution.py:47
  108.4 15.9 %all-to-all-start = ((f32[2,6,8,2,512]{4,3,1,0,2:T(2,128)}), f32[2,6,8,2,512]{4,3,1,0,2:T(2,128)S(1)}, u32[]{:S(2)}, u32[]{:S(2)}) async-start(f32[2,6,8,2,512]{4,3,1,0,2:T(2,128)} %copy.9), calls=%async_computation | async-start | bytes 786432 | tf_op jit(solution)/shard_map/all_to_all | solution.py:31
  116.0 13.4 %copy-start.2 = (s32[32]{0:T(128)S(1)}, s32[32]{0:T(128)}, u32[]{:S(2)}) copy-start(s32[32]{0:T(128)} %param.7) | copy-start | bytes 388
  116.1 36.3 %copy-start.1 = (bf16[2,512,512]{2,1,0:T(8,128)(2,1)S(1)}, bf16[2,512,512]{2,1,0:T(8,128)(2,1)}, u32[]{:S(2)}) copy-start(bf16[2,512,512]{2,1,0:T(8,128)(2,1)} %param.6) | copy-start | bytes 3145732
  124.3 11.5 %all-to-all-start.1 = ((f32[2,2,8,2,512]{4,3,1,0,2:T(2,128)}), f32[2,2,8,2,512]{4,3,1,0,2:T(2,128)S(1)}, u32[]{:S(2)}, u32[]{:S(2)}) async-start(f32[2,2,8,2,512]{4,3,1,0,2:T(2,128)} %copy.10), calls=%async_computation.1 | async-start | bytes 262144 | tf_op jit(solution)/shard_map/all_to_all | solution.py:31
